TPU v7x, 256 devices: a whole 4x4x8 slice. The times are simulated.
256 devices in a mesh: section: 2 (over core), ccd: 128 (over y, x, z).
Axes of the slice: x: 4, y: 4, z: 8, core: 2. Of those that a mesh axis runs over, the one named last changes fastest.
Arguments:
- raw_counts: float32 [128, 2, 64, 2048], P('ccd', 'section'), may hold values from -6 to 6
- overscan: float32 [128, 2, 64], P('ccd', 'section'), may hold values from -6 to 6
- response: float32 [128, 2, 64, 2048], P('ccd', 'section'), may hold values from 0.5 to 2
- warp_rows: int32 [16384], P('ccd'), may hold values from 0 to 16383, as said below
- kernel_poly: float32 [13, 6], replicated, may hold values from -1 to 1
- tile_owner: int32 [128, 2, 128, 1], P('ccd', 'section'), may hold values from 0 to 127; in each aligned block of 128 rows (0 to 127, 128 to 255, ..., all dimensions but the last counted through in order) at most 2 rows name the same one
- tile_weight: float32 [128, 2, 128], P('ccd', 'section'), may hold values from 0.03 to 0.3
Outputs:
- patches: float32 [2, 128, 32, 32], P('section', 'ccd')
Inputs may be any that keep to these rules, and one draw needn't show every extreme that they name: `warp_rows`: row g's source lies within 64 rows of g; in every draw some row takes the row 64 below it and another the row 64 above it. `tile_owner`: among the 128 tiles of one half band at most 2 have the same owner, and in every draw some half band has exactly 2 tiles on one owner.
All inputs are finite; a program needn't handle non-finite values.
Results may differ from a plain program's by a relative error of at most 0.0052.
Values may be sent and summed in bfloat16 or wider, within the bound.
No kernel may reach another device: no remote copies, remote signals or barrier semaphores. Data moves between devices by JAX's collectives and lax.ppermute only.
A program may use at most 64 MiB of HBM per device.

v0:
```python
import jax
import jax.numpy as jnp
from jax import lax
from jax.sharding import PartitionSpec as P

ROWS = 128
TILE = 32
STRIP = 128
KW = 21
NBASIS = 13
NPOLY = 6
HALF_K = 10
CH = 1024
REACH = 64


basis_sigma = (0.75, 0.75, 0.75, 0.75, 0.75, 0.75, 1.5, 1.5, 1.5, 1.5, 3.0, 3.0, 3.0)
column_power = (0, 1, 0, 2, 1, 0, 0, 1, 0, 1, 0, 1, 0)
row_power = (0, 0, 1, 0, 1, 2, 0, 0, 1, 1, 0, 0, 1)


def with_halo(array, sides, width):
    for axis, dim in sides:
        devices, length = (lax.axis_size(axis), array.shape[dim])
        up = [(i, (i + 1) % devices) for i in range(devices - 1)]
        down = [(j, i) for i, j in up]
        last = lax.slice_in_dim(array, length - width, length, axis=dim)
        leading = lax.slice_in_dim(array, 0, width, axis=dim)
        before = lax.ppermute(last, axis, up)
        after = lax.ppermute(leading, axis, down)
        array = jnp.concatenate([before, array, after], axis=dim)
    return array


def basis_taps(powers):
    offsets = jnp.arange(KW).astype(jnp.float32) - HALF_K
    sigma_col = jnp.array(basis_sigma, dtype=jnp.float32)[:, None]
    power_col = jnp.array(powers, dtype=jnp.int32)[:, None]
    spread = offsets[None, :]
    envelope = jnp.exp(-(spread * spread) / (2.0 * sigma_col * sigma_col))
    factor = jnp.where(power_col == 0, 1.0, jnp.where(power_col == 1, spread, spread * spread))
    shaped = envelope * factor
    scale = jnp.sqrt(jnp.sum(shaped * shaped, axis=1, keepdims=True))
    return (shaped / scale).astype(jnp.bfloat16)


def coefficients(terms, row_coord, col_coord):
    return (
        terms[0]
        + terms[1] * row_coord
        + terms[2] * col_coord
        + terms[3] * row_coord * row_coord
        + terms[4] * row_coord * col_coord
        + terms[5] * col_coord * col_coord
    )


def band_matrix(tap_table, inner_len):
    lead_idx = jnp.arange(inner_len + 2 * HALF_K)[:, None]
    trail_idx = jnp.arange(inner_len)[None, :]
    offset = lead_idx - trail_idx
    inside = (offset >= 0) & (offset <= 2 * HALF_K)
    picked = jnp.take(tap_table, jnp.clip(offset, 0, 2 * HALF_K), axis=1)
    return jnp.where(inside[None], picked, jnp.zeros((), tap_table.dtype))


def shards(raw_counts, overscan, response, warp_rows, kernel_poly, tile_owner, tile_weight):
    band_count = lax.axis_size("ccd")
    halves = lax.axis_size("section")
    total_rows = ROWS * band_count
    total_cols = CH * halves
    top_row = lax.axis_index("ccd") * ROWS
    left_col = lax.axis_index("section") * CH
    calibrated = ((raw_counts - overscan[..., None]) * response).astype(jnp.bfloat16)[0, 0]
    matching = lax.all_to_all(calibrated, "section", split_axis=1, concat_axis=0, tiled=True)
    window = with_halo(matching, (("ccd", 0),), REACH)
    row_picks = warp_rows - (top_row - REACH)
    warped = jnp.take(window, row_picks, axis=0, mode="clip")
    padded = with_halo(warped, (("section", 1), ("ccd", 0)), HALF_K)
    col_matrix = (
        band_matrix(basis_taps(column_power), STRIP)
        .transpose(1, 0, 2)
        .reshape(STRIP + 2 * HALF_K, NBASIS * STRIP)
    )
    row_matrix = band_matrix(basis_taps(row_power), STRIP).transpose(0, 2, 1)
    row_strips = ROWS // STRIP
    terms = tuple((kernel_poly[:, term_index][None, :, None, None] for term_index in range(NPOLY)))
    row_pos = (top_row + jnp.arange(ROWS)).astype(jnp.float32)
    row_coord = (2.0 * (row_pos + 0.5) / total_rows - 1.0).reshape(row_strips, 1, STRIP, 1)

    def one_column(column_index):
        col_start = column_index * STRIP
        strip = lax.dynamic_slice_in_dim(padded, col_start, STRIP + 2 * HALF_K, 1)
        across = jnp.dot(strip, col_matrix, preferred_element_type=jnp.float32).astype(jnp.bfloat16)
        across = across.reshape(ROWS + 2 * HALF_K, NBASIS, STRIP)
        stacked = jnp.stack([across])
        vertical = jnp.einsum(
            "kra,bakc->bkrc", row_matrix, stacked, preferred_element_type=jnp.float32
        )
        col_pos = (left_col + col_start + jnp.arange(STRIP)).astype(jnp.float32)
        col_coord = (2.0 * (col_pos + 0.5) / total_cols - 1.0)[None, None, None, :]
        coefficient = coefficients(terms, row_coord, col_coord)
        return jnp.sum(coefficient * vertical, axis=1)

    matched = lax.map(one_column, jnp.arange(CH // STRIP))
    matched = matched.transpose(1, 2, 0, 3).reshape(ROWS, CH)
    tile_stack = (
        matched.reshape(ROWS // TILE, TILE, CH // TILE, TILE)
        .transpose(2, 0, 1, 3)
        .reshape(-1, TILE * TILE)
    )
    owners = tile_owner.reshape(-1)
    weights = tile_weight.reshape(-1)
    peer_ids = jnp.arange(band_count)
    capacity = 2 * max(1, tile_stack.shape[0] // band_count)
    member = owners[:, None] == peer_ids[None, :]
    counts = jnp.cumsum(member.astype(jnp.int32), axis=0)
    slot_rank = jnp.sum(jnp.where(member, counts, 0), axis=1) - 1
    slot_index = owners * capacity + slot_rank
    outgoing = (
        jnp.zeros((band_count * capacity, TILE * TILE), jnp.float32)
        .at[slot_index]
        .set(weights[:, None] * tile_stack)
    )
    incoming = lax.all_to_all(outgoing, "ccd", split_axis=0, concat_axis=0, tiled=True)
    patch_sum = jnp.sum(incoming, axis=0, keepdims=True)
    return patch_sum.reshape(1, 1, TILE, TILE)


def solution(mesh):
    in_specs = (
        P("ccd", "section", None, None),
        P("ccd", "section", None),
        P("ccd", "section", None, None),
        P("ccd"),
        P(),
        P("ccd", "section", None, None),
        P("ccd", "section", None),
    )
    out_specs = P("section", "ccd", None, None)
    return jax.shard_map(shards, mesh=mesh, in_specs=in_specs, out_specs=out_specs, check_vma=False)
```

profile of v0, /device:TPU:1, one launch (start us, length us, event | category | flops | bytes accessed | tf_op | source)
XLA Modules:
  0.0 196.9 jit_solution(2545456917256445614)
XLA Ops:
  0.0 1.3 multiply_convert_fusion
  1.6 6.8 %all_to_all.28 = bf16[64,2,1024]{2,0,1:T(8,128)(2,1)S(1)} all-to-all(bf16[64,2,1024]{2,0,1:T(8,128)(2,1)S(1)} %copy.43), channel_id=1, replica_groups=mesh['section'=2,'ccd'=128] {'section'}, dimensions={1} | all-to-all | bytes 524288 | tf_op jit(solution)/shard_map/all_to_all | solution.py:75
  8.4 1.8 collective-permute-start
  10.2 1.3 collective-permute-start.1
  13.3 38.5 %gather_fusion.1 = bf16[18944,13]{1,0:T(8,128)(2,1)} fusion(bf16[13,21]{0,1:T(8,128)(2,1)S(1)} %get-tuple-element.300, s32[19456]{0:T(1024)S(1)} %pad_clamp_fusion), kind=kCustom, calls=%fused_computation.clone | custom fusion | bytes 1060864 | tf_op jit(solution)/shard_map/jit(_take)/gather | solution.py:63
  51.8 4.2 %copy.44 = bf16[148,128,13]{1,0,2:T(8,128)(2,1)S(1)} copy(bf16[148,128,13]{2,1,0:T(8,128)(2,1)} %bitcast.106) | data formatting | bytes 985088 | tf_op jit(solution)/shard_map/jit(_take)/gather | solution.py:63
  56.1 38.5 %gather_fusion.2 = bf16[18944,13]{1,0:T(8,128)(2,1)} fusion(bf16[13,21]{0,1:T(8,128)(2,1)S(1)} %get-tuple-element.299, s32[19456]{0:T(1024)S(1)} %pad_clamp_fusion), kind=kCustom, calls=%fused_computation.1.clone | custom fusion | bytes 1060864 | tf_op jit(solution)/shard_map/jit(_take)/gather | solution.py:63
  94.6 4.2 %copy.46 = bf16[148,128,13]{1,0,2:T(8,128)(2,1)S(1)} copy(bf16[148,128,13]{2,1,0:T(8,128)(2,1)} %bitcast.105) | data formatting | bytes 985088 | tf_op jit(solution)/shard_map/jit(_take)/gather | solution.py:63
  99.5 0.9 gather_fusion
  100.4 1.3 collective-permute-start.2
  101.7 3.0 %collective-permute-start.3 = (bf16[128,10]{1,0:T(8,128)(2,1)S(1)}, bf16[128,10]{1,0:T(8,128)(2,1)S(1)}, u32[]{:S(2)}, u32[]{:S(2)}) collective-permute-start(bf16[128,10]{1,0:T(8,128)(2,1)S(1)} %get-tuple-element.287), channel_id=1, source_target_pairs={{128,0},{129,1},{130,2},{131,3},{132,4},{133,5},{134,6},{135,7},{1... | collective-permute-start | bytes 7688 | tf_op jit(solution)/shard_map/ppermute | solution.py:30
  105.9 4.2 %collective-permute-start.4 = (bf16[10,1044]{1,0:T(8,128)(2,1)S(1)}, bf16[10,1044]{1,0:T(8,128)(2,1)S(1)}, u32[]{:S(2)}, u32[]{:S(2)}) collective-permute-start(bf16[10,1044]{1,0:T(8,128)(2,1)S(1)} %get-tuple-element.285), channel_id=1, source_target_pairs={{0,1},{1,2},{2,3},{3,4},{4,5},{5,6},{6,7},{7,8},{8,9},{9,10},{10,1... | collective-permute-start | bytes 62648 | tf_op jit(solution)/shard_map/ppermute | solution.py:29
  110.1 1.3 collective-permute-start.5
  111.8 3.2 %collective-permute-done.5 = bf16[10,1044]{1,0:T(8,128)(2,1)S(1)} collective-permute-done((bf16[10,1044]{1,0:T(8,128)(2,1)S(1)}, bf16[10,1044]{1,0:T(8,128)(2,1)S(1)}, u32[]{:S(2)}, u32[]{:S(2)}) %collective-permute-start.5) | collective-permute-done | bytes 20912 | tf_op jit(solution)/shard_map/ppermute | solution.py:30
  115.1 23.8 %while.14 = (s32[]{:T(128)}, f32[8,1,128,128]{2,3,1,0:T(8,128)S(1)}, f32[1,13,1,1]{1,3,2,0:T(1,128)S(1)}, f32[1,13,1,1]{1,3,2,0:T(1,128)S(1)}, f32[1,13,1,1]{1,3...) while((s32[]{:T(128)}, ...), condition=%wide.region_6.8_spmd.clone, body=%wide.region_4.7_spmd.clone.sunk | while | flops 137677568 | bytes 3312691 | solution.py:105
  117.2 0.8 fusion.39
  120.2 0.8 fusion.39
  123.2 0.8 fusion.39
  126.1 0.8 fusion.39
  129.1 0.8 fusion.39
  139.7 2.6 %copy.48 = f32[32,4,32,32]{3,2,1,0:T(8,128)} copy(f32[32,4,32,32]{3,0,2,1:T(8,128)S(1)} %bitcast.104) | data formatting | bytes 1048576 | tf_op jit(solution)/shard_map/transpose | solution.py:109
  142.2 2.4 %reshape.443 = f32[128,1024]{1,0:T(8,128)S(1)} reshape(f32[32,4,32,32]{3,2,1,0:T(8,128)} %copy.48) | data formatting | bytes 1048576 | tf_op jit(solution)/shard_map/reshape | solution.py:110
  144.7 1.4 scatter_custom_fusion
  146.7 49.2 %all_to_all.29 = f32[128,2,1024]{2,1,0:T(2,128)S(1)} all-to-all(f32[128,2,1024]{2,1,0:T(2,128)S(1)} %all_to_all.24), channel_id=1, replica_groups=mesh['section'=2,'ccd'=128] {'ccd'}, dimensions={0} | all-to-all | bytes 2097152 | tf_op jit(solution)/shard_map/all_to_all | solution.py:125
  (107 shorter events, 20.9 us)
Async XLA Ops:
  8.4 91.1 %collective-permute-start = (bf16[64,1024]{1,0:T(8,128)(2,1)S(1)}, bf16[64,1024]{1,0:T(8,128)(2,1)S(1)}, u32[]{:S(2)}, u32[]{:S(2)}) collective-permute-start(bf16[64,1024]{1,0:T(8,128)(2,1)S(1)} %get-tuple-element.289), channel_id=1, source_target_pairs={{0,1},{1,2},{2,3},{3,4},{4,5},{5,6},{6,7},{7,8},{8,9},{9,10},{10,1... | collective-permute-start | bytes 393224 | tf_op jit(solution)/shard_map/ppermute | solution.py:29
  10.2 89.2 %collective-permute-start.1 = (bf16[64,1024]{1,0:T(8,128)(2,1)S(1)}, bf16[64,1024]{1,0:T(8,128)(2,1)S(1)}, u32[]{:S(2)}, u32[]{:S(2)}) collective-permute-start(bf16[64,1024]{1,0:T(8,128)(2,1)S(1)} %get-tuple-element.290), channel_id=1, source_target_pairs={{1,0},{2,1},{3,2},{4,3},{5,4},{6,5},{7,6},{8,7},{9,8},{10,9},{11,1... | collective-permute-start | bytes 393224 | tf_op jit(solution)/shard_map/ppermute | solution.py:30
  56.0 42.8 %copy-start = (f32[13,6]{0,1:T(8,128)S(1)}, f32[13,6]{0,1:T(8,128)}, u32[]{:S(2)}) copy-start(f32[13,6]{0,1:T(8,128)} %param.19) | copy-start | bytes 940
  56.0 42.8 %copy-start.1 = (s32[1,1,128,1]{2,3,1,0:T(1,128)S(1)}, s32[1,1,128,1]{2,3,1,0:T(1,128)}, u32[]{:S(2)}) copy-start(s32[1,1,128,1]{2,3,1,0:T(1,128)} %param.20) | copy-start | bytes 1540
  94.6 4.6 %copy-start.3 = (s32[128]{0:T(128)S(1)}, s32[128]{0:T(128)}, u32[]{:S(2)}) copy-start(s32[128]{0:T(128)} %param.18) | copy-start | bytes 1540
  100.4 4.5 %collective-permute-start.2 = (bf16[128,10]{1,0:T(8,128)(2,1)S(1)}, bf16[128,10]{1,0:T(8,128)(2,1)S(1)}, u32[]{:S(2)}, u32[]{:S(2)}) collective-permute-start(bf16[128,10]{1,0:T(8,128)(2,1)S(1)} %get-tuple-element.288), channel_id=1, source_target_pairs={{0,128},{1,129},{2,130},{3,131},{4,132},{5,133},{6,134},{7,135},{8... | collective-permute-start | bytes 7688 | tf_op jit(solution)/shard_map/ppermute | solution.py:29
  101.7 3.9 %collective-permute-start.3 = (bf16[128,10]{1,0:T(8,128)(2,1)S(1)}, bf16[128,10]{1,0:T(8,128)(2,1)S(1)}, u32[]{:S(2)}, u32[]{:S(2)}) collective-permute-start(bf16[128,10]{1,0:T(8,128)(2,1)S(1)} %get-tuple-element.287), channel_id=1, source_target_pairs={{128,0},{129,1},{130,2},{131,3},{132,4},{133,5},{134,6},{135,7},{1... | collective-permute-start | bytes 7688 | tf_op jit(solution)/shard_map/ppermute | solution.py:30
  105.9 5.9 %collective-permute-start.4 = (bf16[10,1044]{1,0:T(8,128)(2,1)S(1)}, bf16[10,1044]{1,0:T(8,128)(2,1)S(1)}, u32[]{:S(2)}, u32[]{:S(2)}) collective-permute-start(bf16[10,1044]{1,0:T(8,128)(2,1)S(1)} %get-tuple-element.285), channel_id=1, source_target_pairs={{0,1},{1,2},{2,3},{3,4},{4,5},{5,6},{6,7},{7,8},{8,9},{9,10},{10,1... | collective-permute-start | bytes 62648 | tf_op jit(solution)/shard_map/ppermute | solution.py:29
  110.1 4.9 %collective-permute-start.5 = (bf16[10,1044]{1,0:T(8,128)(2,1)S(1)}, bf16[10,1044]{1,0:T(8,128)(2,1)S(1)}, u32[]{:S(2)}, u32[]{:S(2)}) collective-permute-start(bf16[10,1044]{1,0:T(8,128)(2,1)S(1)} %get-tuple-element.286), channel_id=1, source_target_pairs={{1,0},{2,1},{3,2},{4,3},{5,4},{6,5},{7,6},{8,7},{9,8},{10,9},{11,1... | collective-permute-start | bytes 62648 | tf_op jit(solution)/shard_map/ppermute | solution.py:30
  139.2 5.5 %copy-start.2 = (f32[1,1,128]{2,1,0:T(1,128)S(1)}, f32[1,1,128]{2,1,0:T(1,128)}, u32[]{:S(2)}) copy-start(f32[1,1,128]{2,1,0:T(1,128)} %param.21) | copy-start | bytes 1540
where the time goes:
time: 198 us; the launch traced here: 197 us
  local copies, waits for them, and re-layouts  102 us (52%)
  blocking collectives  56 us (28%)
  starting transfers between devices  12.9 us (7%)
  matrix products  9.54 us (5%)
  other arithmetic  6.42 us (3%)
  loops' own time  5.48 us (3%)
  waiting for transfers between devices  3.83 us (2%)
    gather x4, local copies, waits for them, and re-layouts, band_matrix(): picked = jnp.take(tap_table, jnp.clip(offset, 0, 2 * HALF_K), axis=1)  85.4 us
    all_to_all x1, blocking collectives, shards(): lax.all_to_all(outgoing, 'ccd', split_axis=0, concat_axis=0, tiled=True)  49.2 us
    ppermute x3, starting transfers between devices, with_halo(): before = lax.ppermute(last, axis, up)  7.3 us
    all_to_all x1, blocking collectives, shards(): lax.all_to_all(calibrated, 'section', split_axis=1, concat_axis=0, tiled=...  6.78 us
    dot_general x8, matrix products, one_column(): jnp.einsum('kra,bakc->bkrc', row_matrix, stacked, preferred_element_type=...  6.6 us
    ppermute x3, starting transfers between devices, with_halo(): after = lax.ppermute(leading, axis, down)  5.61 us
    another operation x1, loops' own time, shards(): matched = lax.map(one_column, jnp.arange(CH // STRIP))  5.48 us
    dynamic_slice x8, local copies, waits for them, and re-layouts, shards(): matched = lax.map(one_column, jnp.arange(CH // STRIP))  4.93 us
  transfers between devices with their start and end apart: 6, of which 2 were waited for; matrix products, arithmetic and copies ran while one was open for 45% of the time, Pallas kernels for 0%

commit v1 on v0

--- a/solution.py
+++ b/solution.py
@@ -59,9 +59,9 @@
     lead_idx = jnp.arange(inner_len + 2 * HALF_K)[:, None]
     trail_idx = jnp.arange(inner_len)[None, :]
     offset = lead_idx - trail_idx
-    inside = (offset >= 0) & (offset <= 2 * HALF_K)
-    picked = jnp.take(tap_table, jnp.clip(offset, 0, 2 * HALF_K), axis=1)
-    return jnp.where(inside[None], picked, jnp.zeros((), tap_table.dtype))
+    onehot = (offset[None] == jnp.arange(KW)[:, None, None]).astype(tap_table.dtype)
+    band = jnp.einsum("kt,tai->kai", tap_table, onehot, preferred_element_type=jnp.float32)
+    return band.astype(tap_table.dtype)
 
 
 def shards(raw_counts, overscan, response, warp_rows, kernel_poly, tile_owner, tile_weight):
@@ -71,12 +71,32 @@
     total_cols = CH * halves
     top_row = lax.axis_index("ccd") * ROWS
     left_col = lax.axis_index("section") * CH
+    band = lax.axis_index("ccd")
+    half = lax.axis_index("section")
     calibrated = ((raw_counts - overscan[..., None]) * response).astype(jnp.bfloat16)[0, 0]
-    matching = lax.all_to_all(calibrated, "section", split_axis=1, concat_axis=0, tiled=True)
-    window = with_halo(matching, (("ccd", 0),), REACH)
-    row_picks = warp_rows - (top_row - REACH)
-    warped = jnp.take(window, row_picks, axis=0, mode="clip")
-    padded = with_halo(warped, (("section", 1), ("ccd", 0)), HALF_K)
+    wide = jnp.pad(calibrated, ((0, 0), (HALF_K, HALF_K)))
+    width = CH + 2 * HALF_K
+    own = lax.dynamic_slice_in_dim(wide, half * CH, width, 1)
+    other = lax.dynamic_slice_in_dim(wide, (1 - half) * CH, width, 1)
+    received = lax.ppermute(other, "section", [(0, 1), (1, 0)])
+    band_rows = jnp.where(
+        half == 0,
+        jnp.concatenate([own, received], axis=0),
+        jnp.concatenate([received, own], axis=0),
+    )
+    reach = REACH + HALF_K
+    up = [(i, i + 1) for i in range(band_count - 1)]
+    down = [(i + 1, i) for i in range(band_count - 1)]
+    before = lax.ppermute(band_rows[ROWS - reach :], "ccd", up)
+    after = lax.ppermute(band_rows[:reach], "ccd", down)
+    window = jnp.concatenate([before, band_rows, after], axis=0)
+    rows_before = lax.ppermute(warp_rows[ROWS - HALF_K :], "ccd", up)
+    rows_after = lax.ppermute(warp_rows[:HALF_K], "ccd", down)
+    sources = jnp.concatenate([rows_before, warp_rows, rows_after])
+    out_rows = top_row - HALF_K + jnp.arange(ROWS + 2 * HALF_K)
+    inside = (out_rows >= 0) & (out_rows < total_rows)
+    warped = jnp.take(window, sources - (top_row - reach), axis=0, mode="clip")
+    padded = jnp.where(inside[:, None], warped, jnp.zeros((), warped.dtype))
     col_matrix = (
         band_matrix(basis_taps(column_power), STRIP)
         .transpose(1, 0, 2)
@@ -111,16 +131,11 @@
     )
     owners = tile_owner.reshape(-1)
     weights = tile_weight.reshape(-1)
-    peer_ids = jnp.arange(band_count)
-    capacity = 2 * max(1, tile_stack.shape[0] // band_count)
-    member = owners[:, None] == peer_ids[None, :]
-    counts = jnp.cumsum(member.astype(jnp.int32), axis=0)
-    slot_rank = jnp.sum(jnp.where(member, counts, 0), axis=1) - 1
-    slot_index = owners * capacity + slot_rank
-    outgoing = (
-        jnp.zeros((band_count * capacity, TILE * TILE), jnp.float32)
-        .at[slot_index]
-        .set(weights[:, None] * tile_stack)
+    selector = jnp.where(
+        jnp.arange(band_count)[:, None] == owners[None, :], weights[None, :], 0.0
+    )
+    outgoing = jnp.dot(
+        selector, tile_stack, precision=lax.Precision.HIGHEST, preferred_element_type=jnp.float32
     )
     incoming = lax.all_to_all(outgoing, "ccd", split_axis=0, concat_axis=0, tiled=True)
     patch_sum = jnp.sum(incoming, axis=0, keepdims=True)

time: 198 us -> 95.6 us (0.48)
  local copies, waits for them, and re-layouts: 102 us -> 17.4 us
  blocking collectives: 56 us -> 38.7 us
  other arithmetic: 6.42 us -> 3.05 us
  waiting for transfers between devices: 3.83 us -> 6.74 us
    gather x5 -> x1, local copies, waits for them, and re-layouts: 86.3 us -> 0.96 us  [shards(): warped = jnp.take(window, sources - (top_row - reach), axis=0, mode='clip')]
    all_to_all x1, blocking collectives: 49.2 us -> 38.7 us  [shards(): lax.all_to_all(outgoing, 'ccd', split_axis=0, concat_axis=0, tiled=True)]
    all_to_all x1 -> x0, blocking collectives: 6.78 us -> none  [shards(): lax.all_to_all(calibrated, 'section', split_axis=1, concat_axis=0, tiled=...]
    ppermute x6 -> x5, waiting for transfers between devices: 3.83 us -> 6.74 us  [the longest x1 4.22 us: shards(): after = lax.ppermute(band_rows[:reach], 'ccd', down)]
    convert_element_type x3 -> x0, other arithmetic: 2.2 us -> none  [the longest x1 1.31 us: shards(): ((raw_counts - overscan[..., None]) * response).astype(jnp.bfloat16)[0, 0]]
    ppermute x6 -> x5, starting transfers between devices: 12.9 us -> 12.2 us  [the longest x1 4.35 us: shards(): rows_before = lax.ppermute(warp_rows[ROWS - HALF_K:], 'ccd', up)]
  transfers between devices with their start and end apart: 6 -> 5, of which waited for: 2 -> 2; matrix products, arithmetic and copies ran while one was open for 45% -> 3% of each run, Pallas kernels for 0% -> 0%
where the time goes in v1:
time: 95.6 us; the launch traced here: 95.2 us
  blocking collectives  38.7 us (40%)
  local copies, waits for them, and re-layouts  17.4 us (18%)
  starting transfers between devices  12.2 us (13%)
  matrix products  11.1 us (12%)
  waiting for transfers between devices  6.74 us (7%)
  loops' own time  5.69 us (6%)
  other arithmetic  3.05 us (3%)
    all_to_all x1, blocking collectives, shards(): lax.all_to_all(outgoing, 'ccd', split_axis=0, concat_axis=0, tiled=True)  38.7 us
    dot_general x8, matrix products, one_column(): jnp.einsum('kra,bakc->bkrc', row_matrix, stacked, preferred_element_type=...  6.61 us
    another operation x1, loops' own time, shards(): matched = lax.map(one_column, jnp.arange(CH // STRIP))  5.69 us
    dynamic_slice x8, local copies, waits for them, and re-layouts, shards(): matched = lax.map(one_column, jnp.arange(CH // STRIP))  4.9 us
    ppermute x1, starting transfers between devices, shards(): rows_before = lax.ppermute(warp_rows[ROWS - HALF_K:], 'ccd', up)  4.35 us
    ppermute x1, starting transfers between devices, shards(): before = lax.ppermute(band_rows[ROWS - reach:], 'ccd', up)  4.27 us
    ppermute x1, waiting for transfers between devices, shards(): after = lax.ppermute(band_rows[:reach], 'ccd', down)  4.22 us
    another operation x8, local copies, waits for them, and re-layouts  3.01 us
  transfers between devices with their start and end apart: 5, of which 2 were waited for; matrix products, arithmetic and copies ran while one was open for 3% of the time, Pallas kernels for 0%

profile of v1, /device:TPU:1, one launch (start us, length us, event | category | flops | bytes accessed | tf_op | source)
XLA Modules:
  0.0 95.2 jit_solution(13359954791347314243)
XLA Ops:
  0.0 0.8 fusion.48
  0.8 4.3 %collective-permute-start.3 = (s32[10]{0:T(128)S(1)}, s32[10]{0:T(128)S(1)}, u32[]{:S(2)}, u32[]{:S(2)}) collective-permute-start(s32[10]{0:T(128)S(1)} %get-tuple-element.336), channel_id=1, source_target_pairs={{0,1},{1,2},{2,3},{3,4},{4,5},{5,6},{6,7},{7,8},{8,9},{9,10},{10,1... | collective-permute-start | bytes 128 | tf_op jit(solution)/shard_map/ppermute | solution.py:93
  5.2 1.3 %collective-permute-start.4 = (s32[10]{0:T(128)S(1)}, s32[10]{0:T(128)S(1)}, u32[]{:S(2)}, u32[]{:S(2)}) collective-permute-start(s32[10]{0:T(128)S(1)} %get-tuple-element.337), channel_id=1, source_target_pairs={{1,0},{2,1},{3,2},{4,3},{5,4},{6,5},{7,6},{8,7},{9,8},{10,9},{11,1... | collective-permute-start | bytes 128 | tf_op jit(solution)/shard_map/ppermute | solution.py:94
  6.5 1.3 %fusion.15 = bf16[64,2048]{1,0:T(8,128)(2,1)S(1)} fusion(f32[1,1,64,2048]{3,2,1,0:T(8,128)} %param.15, f32[1,1,64,2048]{3,2,1,0:T(8,128)} %param.13, f32[64]{0:T(128)} %bitcast.102), kind=kLoop, calls=%fused_computation.31 | loop fusion | flops 393216 | bytes 1310976 | tf_op jit(solution)/shard_map/squeeze | solution.py:76
  8.0 1.0 %collective-permute-start = (bf16[64,1044]{1,0:T(8,128)(2,1)S(1)}, bf16[64,1044]{1,0:T(8,128)(2,1)S(1)}, u32[]{:S(2)}, u32[]{:S(2)}) collective-permute-start(bf16[64,1044]{1,0:T(8,128)(2,1)S(1)} %get-tuple-element.329), channel_id=1, source_target_pairs={{0,128},{128,0},{1,129},{129,1},{2,130},{130,2},{3,131},{131,3},{4... | collective-permute-start | bytes 400904 | tf_op jit(solution)/shard_map/ppermute | solution.py:81
  10.9 4.3 %collective-permute-start.1 = (bf16[74,1044]{1,0:T(8,128)(2,1)S(1)}, bf16[74,1044]{1,0:T(8,128)(2,1)S(1)}, u32[]{:S(2)}, u32[]{:S(2)}) collective-permute-start(bf16[74,1044]{1,0:T(8,128)(2,1)S(1)} %get-tuple-element.326), channel_id=1, source_target_pairs={{0,1},{1,2},{2,3},{3,4},{4,5},{5,6},{6,7},{7,8},{8,9},{9,10},{10,1... | collective-permute-start | bytes 463544 | tf_op jit(solution)/shard_map/ppermute | solution.py:90
  15.2 1.3 %collective-permute-start.2 = (bf16[74,1044]{1,0:T(8,128)(2,1)S(1)}, bf16[74,1044]{1,0:T(8,128)(2,1)S(1)}, u32[]{:S(2)}, u32[]{:S(2)}) collective-permute-start(bf16[74,1044]{1,0:T(8,128)(2,1)S(1)} %get-tuple-element.327), channel_id=1, source_target_pairs={{1,0},{2,1},{3,2},{4,3},{5,4},{6,5},{7,6},{8,7},{9,8},{10,9},{11,1... | collective-permute-start | bytes 463544 | tf_op jit(solution)/shard_map/ppermute | solution.py:91
  16.6 2.5 %collective-permute-done.1 = bf16[74,1044]{1,0:T(8,128)(2,1)S(1)} collective-permute-done((bf16[74,1044]{1,0:T(8,128)(2,1)S(1)}, bf16[74,1044]{1,0:T(8,128)(2,1)S(1)}, u32[]{:S(2)}, u32[]{:S(2)}) %collective-permute-start.1) | collective-permute-done | bytes 154544 | tf_op jit(solution)/shard_map/ppermute | solution.py:90
  19.1 4.2 %collective-permute-done.2 = bf16[74,1044]{1,0:T(8,128)(2,1)S(1)} collective-permute-done((bf16[74,1044]{1,0:T(8,128)(2,1)S(1)}, bf16[74,1044]{1,0:T(8,128)(2,1)S(1)}, u32[]{:S(2)}, u32[]{:S(2)}) %collective-permute-start.2) | collective-permute-done | bytes 154544 | tf_op jit(solution)/shard_map/ppermute | solution.py:91
  23.5 1.0 %gather_fusion = bf16[148,1044]{1,0:T(8,128)(2,1)S(1)} fusion(bf16[276,1044]{1,0:T(8,128)(2,1)S(1)} %pad_maximum_fusion, s32[1024]{0:T(1024)S(1)} %pad_clamp_fusion), kind=kCustom, calls=%fused_computation | custom fusion | bytes 618640 | tf_op jit(solution)/shard_map/jit(_take)/gather | solution.py:98
  24.6 24.0 %while.14 = (s32[]{:T(128)}, f32[8,1,128,128]{2,3,1,0:T(8,128)S(1)}, f32[1,13,1,1]{1,3,2,0:T(1,128)S(1)}, f32[1,13,1,1]{1,3,2,0:T(1,128)S(1)}, f32[1,13,1,1]{1,3...) while((s32[]{:T(128)}, ...), condition=%wide.region_4.5_spmd.clone, body=%wide.region_2.4_spmd.clone.sunk | while | flops 137677568 | bytes 3312699 | solution.py:125
  26.7 0.8 fusion.61
  27.6 0.6 dynamic_slice.32
  29.7 0.8 fusion.61
  32.7 0.8 fusion.61
  35.7 0.8 fusion.61
  38.7 0.8 fusion.61
  41.7 0.8 fusion.61
  44.7 0.8 fusion.61
  47.7 0.8 fusion.61
  49.3 2.6 %copy.21 = f32[32,4,32,32]{3,2,1,0:T(8,128)} copy(f32[32,4,32,32]{3,0,2,1:T(8,128)S(1)} %bitcast.89) | data formatting | bytes 1048576 | tf_op jit(solution)/shard_map/transpose | solution.py:129
  51.9 2.5 %reshape.444 = f32[128,1024]{1,0:T(8,128)S(1)} reshape(f32[32,4,32,32]{3,2,1,0:T(8,128)} %copy.21) | data formatting | bytes 1048576 | tf_op jit(solution)/shard_map/reshape | solution.py:130
  55.5 38.7 %all_to_all.9 = f32[128,1,1024]{2,1,0:T(1,128)S(1)} all-to-all(f32[128,1,1024]{2,1,0:T(1,128)S(1)} %copy.22), channel_id=1, replica_groups=mesh['section'=2,'ccd'=128] {'ccd'}, dimensions={0} | all-to-all | bytes 1048576 | tf_op jit(solution)/shard_map/all_to_all | solution.py:140
  94.6 0.7 reshape_broadcast_in_dim.3
  (103 shorter events, 15.5 us)
Async XLA Ops:
  0.0 9.1 %copy-start = (f32[13]{0:T(128)S(1)}, f32[13]{0:T(128)}, u32[]{:S(2)}) copy-start(f32[13]{0:T(128)} %constant.135) | copy-start | bytes 160
  0.0 9.1 %copy-start.5 = (pred[13]{0:T(512)(128)(4,1)S(1)}, pred[13]{0:T(512)(128)(4,1)}, u32[]{:S(2)}) copy-start(pred[13]{0:T(512)(128)(4,1)} %constant.134) | copy-start | bytes 43
  0.0 9.1 %copy-start.6 = (pred[13]{0:T(512)(128)(4,1)S(1)}, pred[13]{0:T(512)(128)(4,1)}, u32[]{:S(2)}) copy-start(pred[13]{0:T(512)(128)(4,1)} %constant.133) | copy-start | bytes 43
  0.0 9.1 %copy-start.3 = (pred[13]{0:T(512)(128)(4,1)S(1)}, pred[13]{0:T(512)(128)(4,1)}, u32[]{:S(2)}) copy-start(pred[13]{0:T(512)(128)(4,1)} %constant.132) | copy-start | bytes 43
  0.0 9.1 %copy-start.4 = (pred[13]{0:T(512)(128)(4,1)S(1)}, pred[13]{0:T(512)(128)(4,1)}, u32[]{:S(2)}) copy-start(pred[13]{0:T(512)(128)(4,1)} %constant.131) | copy-start | bytes 43
  0.8 15.6 %collective-permute-start.3 = (s32[10]{0:T(128)S(1)}, s32[10]{0:T(128)S(1)}, u32[]{:S(2)}, u32[]{:S(2)}) collective-permute-start(s32[10]{0:T(128)S(1)} %get-tuple-element.336), channel_id=1, source_target_pairs={{0,1},{1,2},{2,3},{3,4},{4,5},{5,6},{6,7},{7,8},{8,9},{9,10},{10,1... | collective-permute-start | bytes 128 | tf_op jit(solution)/shard_map/ppermute | solution.py:93
  5.2 11.3 %collective-permute-start.4 = (s32[10]{0:T(128)S(1)}, s32[10]{0:T(128)S(1)}, u32[]{:S(2)}, u32[]{:S(2)}) collective-permute-start(s32[10]{0:T(128)S(1)} %get-tuple-element.337), channel_id=1, source_target_pairs={{1,0},{2,1},{3,2},{4,3},{5,4},{6,5},{7,6},{8,7},{9,8},{10,9},{11,1... | collective-permute-start | bytes 128 | tf_op jit(solution)/shard_map/ppermute | solution.py:94
  7.8 2.5 %copy-start.2 = (f32[13,6]{0,1:T(8,128)S(1)}, f32[13,6]{0,1:T(8,128)}, u32[]{:S(2)}) copy-start(f32[13,6]{0,1:T(8,128)} %param.17) | copy-start | bytes 940
  8.0 2.8 %collective-permute-start = (bf16[64,1044]{1,0:T(8,128)(2,1)S(1)}, bf16[64,1044]{1,0:T(8,128)(2,1)S(1)}, u32[]{:S(2)}, u32[]{:S(2)}) collective-permute-start(bf16[64,1044]{1,0:T(8,128)(2,1)S(1)} %get-tuple-element.329), channel_id=1, source_target_pairs={{0,128},{128,0},{1,129},{129,1},{2,130},{130,2},{3,131},{131,3},{4... | collective-permute-start | bytes 400904 | tf_op jit(solution)/shard_map/ppermute | solution.py:81
  10.6 5.9 %copy-start.1 = (s32[128]{0:T(128)S(1)}, s32[128]{0:T(128)}, u32[]{:S(2)}) copy-start(s32[128]{0:T(128)} %param.16) | copy-start | bytes 1540
  10.9 8.2 %collective-permute-start.1 = (bf16[74,1044]{1,0:T(8,128)(2,1)S(1)}, bf16[74,1044]{1,0:T(8,128)(2,1)S(1)}, u32[]{:S(2)}, u32[]{:S(2)}) collective-permute-start(bf16[74,1044]{1,0:T(8,128)(2,1)S(1)} %get-tuple-element.326), channel_id=1, source_target_pairs={{0,1},{1,2},{2,3},{3,4},{4,5},{5,6},{6,7},{7,8},{8,9},{9,10},{10,1... | collective-permute-start | bytes 463544 | tf_op jit(solution)/shard_map/ppermute | solution.py:90
  15.2 8.2 %collective-permute-start.2 = (bf16[74,1044]{1,0:T(8,128)(2,1)S(1)}, bf16[74,1044]{1,0:T(8,128)(2,1)S(1)}, u32[]{:S(2)}, u32[]{:S(2)}) collective-permute-start(bf16[74,1044]{1,0:T(8,128)(2,1)S(1)} %get-tuple-element.327), channel_id=1, source_target_pairs={{1,0},{2,1},{3,2},{4,3},{5,4},{6,5},{7,6},{8,7},{9,8},{10,9},{11,1... | collective-permute-start | bytes 463544 | tf_op jit(solution)/shard_map/ppermute | solution.py:91
  51.9 2.5 %copy-start.7 = (f32[1,1,128]{2,1,0:T(1,128)S(1)}, f32[1,1,128]{2,1,0:T(1,128)}, u32[]{:S(2)}) copy-start(f32[1,1,128]{2,1,0:T(1,128)} %param.19) | copy-start | bytes 1540
  51.9 2.5 %copy-start.8 = (s32[1,1,128,1]{2,3,1,0:T(1,128)S(1)}, s32[1,1,128,1]{2,3,1,0:T(1,128)}, u32[]{:S(2)}) copy-start(s32[1,1,128,1]{2,3,1,0:T(1,128)} %param.18) | copy-start | bytes 1540

commit v2 on v1

--- a/solution.py
+++ b/solution.py
@@ -2,6 +2,7 @@
 import jax.numpy as jnp
 from jax import lax
 from jax.sharding import PartitionSpec as P
+from jax.experimental import pallas as pl
 
 ROWS = 128
 TILE = 32
@@ -71,7 +72,6 @@
     total_cols = CH * halves
     top_row = lax.axis_index("ccd") * ROWS
     left_col = lax.axis_index("section") * CH
-    band = lax.axis_index("ccd")
     half = lax.axis_index("section")
     calibrated = ((raw_counts - overscan[..., None]) * response).astype(jnp.bfloat16)[0, 0]
     wide = jnp.pad(calibrated, ((0, 0), (HALF_K, HALF_K)))
@@ -97,33 +97,58 @@
     inside = (out_rows >= 0) & (out_rows < total_rows)
     warped = jnp.take(window, sources - (top_row - reach), axis=0, mode="clip")
     padded = jnp.where(inside[:, None], warped, jnp.zeros((), warped.dtype))
-    col_matrix = (
-        band_matrix(basis_taps(column_power), STRIP)
-        .transpose(1, 0, 2)
-        .reshape(STRIP + 2 * HALF_K, NBASIS * STRIP)
-    )
-    row_matrix = band_matrix(basis_taps(row_power), STRIP).transpose(0, 2, 1)
-    row_strips = ROWS // STRIP
-    terms = tuple((kernel_poly[:, term_index][None, :, None, None] for term_index in range(NPOLY)))
+    strips = CH // STRIP
+    span = 2 * STRIP
+    lead = ROWS + 2 * HALF_K
+    lead_pad = -(-lead // 16) * 16
+    image = jnp.pad(padded, ((0, lead_pad - lead), (0, strips * STRIP + STRIP - padded.shape[1])))
+    col_band = band_matrix(basis_taps(column_power), STRIP)
+    col_band = jnp.pad(col_band, ((0, 0), (0, span - col_band.shape[1]), (0, 0)))
+    col_matrix = col_band.transpose(1, 0, 2).reshape(span, NBASIS * STRIP)
+    row_matrix = band_matrix(basis_taps(row_power), ROWS).transpose(0, 2, 1)
+    row_matrix = jnp.pad(row_matrix, ((0, 0), (0, 0), (0, lead_pad - lead)))
     row_pos = (top_row + jnp.arange(ROWS)).astype(jnp.float32)
-    row_coord = (2.0 * (row_pos + 0.5) / total_rows - 1.0).reshape(row_strips, 1, STRIP, 1)
+    row_coord = (2.0 * (row_pos + 0.5) / total_rows - 1.0)[None, :, None]
+    col_pos = (left_col + jnp.arange(CH)).astype(jnp.float32)
+    col_coord = (2.0 * (col_pos + 0.5) / total_cols - 1.0).reshape(strips, 1, STRIP)
+    poly = kernel_poly[:, :, None, None]
+    row_part = poly[:, 0] + poly[:, 1] * row_coord + poly[:, 3] * row_coord * row_coord
+    slope_part = poly[:, 2] + poly[:, 4] * row_coord
+    square_part = poly[:, 5]
 
-    def one_column(column_index):
-        col_start = column_index * STRIP
-        strip = lax.dynamic_slice_in_dim(padded, col_start, STRIP + 2 * HALF_K, 1)
-        across = jnp.dot(strip, col_matrix, preferred_element_type=jnp.float32).astype(jnp.bfloat16)
-        across = across.reshape(ROWS + 2 * HALF_K, NBASIS, STRIP)
-        stacked = jnp.stack([across])
-        vertical = jnp.einsum(
-            "kra,bakc->bkrc", row_matrix, stacked, preferred_element_type=jnp.float32
-        )
-        col_pos = (left_col + col_start + jnp.arange(STRIP)).astype(jnp.float32)
-        col_coord = (2.0 * (col_pos + 0.5) / total_cols - 1.0)[None, None, None, :]
-        coefficient = coefficients(terms, row_coord, col_coord)
-        return jnp.sum(coefficient * vertical, axis=1)
+    def match_kernel(img_ref, colm_ref, rowm_ref, a_ref, b_ref, c_ref, v_ref, out_ref):
+        i = pl.program_id(0)
+        offset = pl.multiple_of(i * STRIP, STRIP)
+        strip = img_ref[:, pl.ds(offset, span)]
+        across = jnp.dot(strip, colm_ref[...], preferred_element_type=jnp.float32)
+        across = across.astype(jnp.bfloat16)
+        v = v_ref[0]
+        acc = jnp.zeros((ROWS, STRIP), jnp.float32)
+        for k in range(NBASIS):
+            vert = jnp.dot(
+                rowm_ref[k], across[:, k * STRIP : (k + 1) * STRIP],
+                preferred_element_type=jnp.float32,
+            )
+            coef = a_ref[k] + v * (b_ref[k] + c_ref[k] * v)
+            acc = acc + coef * vert
+        out_ref[...] = acc
 
-    matched = lax.map(one_column, jnp.arange(CH // STRIP))
-    matched = matched.transpose(1, 2, 0, 3).reshape(ROWS, CH)
+    full = lambda shape: pl.BlockSpec(shape, lambda i: (0,) * len(shape))
+    matched = pl.pallas_call(
+        match_kernel,
+        grid=(strips,),
+        in_specs=[
+            full(image.shape),
+            full(col_matrix.shape),
+            full(row_matrix.shape),
+            full(row_part.shape),
+            full(slope_part.shape),
+            full(square_part.shape),
+            pl.BlockSpec((1, 1, STRIP), lambda i: (i, 0, 0)),
+        ],
+        out_specs=pl.BlockSpec((ROWS, STRIP), lambda i: (0, i)),
+        out_shape=jax.ShapeDtypeStruct((ROWS, CH), jnp.float32),
+    )(image, col_matrix, row_matrix, row_part, slope_part, square_part, col_coord)
     tile_stack = (
         matched.reshape(ROWS // TILE, TILE, CH // TILE, TILE)
         .transpose(2, 0, 1, 3)

time: 95.6 us -> 89.1 us (0.932)
  matrix products: 11.1 us -> 1.51 us
  Pallas kernels: 0 us -> 7.66 us
  loops' own time: 5.69 us -> 0 us
  other arithmetic: 3.05 us -> 5.53 us
  local copies, waits for them, and re-layouts: 17.4 us -> 16.1 us
    dot_general x16 -> x0, matrix products: 9.56 us -> none  [the longest x8 6.61 us: one_column(): jnp.einsum('kra,bakc->bkrc', row_matrix, stacked, preferred_element_type=...]
    pallas_call x0 -> x1, Pallas kernels: none -> 7.66 us  [shards(): pl.pallas_call(match_kernel, grid=(strips,), in_specs=[full(image.shape),...]
    another operation x1 -> x0, loops' own time: 5.69 us -> none  [shards(): matched = lax.map(one_column, jnp.arange(CH // STRIP))]
    reshape x0 -> x3, local copies, waits for them, and re-layouts: none -> 5.65 us  [the longest x2 4.3 us: shards(): matched.reshape(ROWS // TILE, TILE, CH // TILE, TILE).transpose(2, 0, 1, 3)]
    dynamic_slice x8 -> x0, local copies, waits for them, and re-layouts: 4.9 us -> none  [shards(): matched = lax.map(one_column, jnp.arange(CH // STRIP))]
    another operation x10 -> x0, local copies, waits for them, and re-layouts: 3.48 us -> none
    pad x0 -> x2, local copies, waits for them, and re-layouts: none -> 1.86 us  [the longest x1 1.09 us: shards(): row_matrix = jnp.pad(row_matrix, ((0, 0), (0, 0), (0, lead_pad - lead)))]
    transpose x2, local copies, waits for them, and re-layouts: 2.79 us -> 1.09 us  [shards(): col_matrix = col_band.transpose(1, 0, 2).reshape(span, NBASIS * STRIP)]
  transfers between devices with their start and end apart: 5 -> 5, of which waited for: 2 -> 2; matrix products, arithmetic and copies ran while one was open for 3% -> 13% of each run, Pallas kernels for 0% -> 0%
where the time goes in v2:
time: 89.1 us; the launch traced here: 88.7 us
  blocking collectives  38.7 us (43%)
  local copies, waits for them, and re-layouts  16.1 us (18%)
  starting transfers between devices  12.2 us (14%)
  Pallas kernels  7.66 us (9%)
  waiting for transfers between devices  6.74 us (8%)
  other arithmetic  5.53 us (6%)
  matrix products  1.51 us (2%)
    all_to_all x1, blocking collectives, shards(): lax.all_to_all(outgoing, 'ccd', split_axis=0, concat_axis=0, tiled=True)  38.7 us
    pallas_call x1, Pallas kernels, shards(): pl.pallas_call(match_kernel, grid=(strips,), in_specs=[full(image.shape),...  7.66 us
    ppermute x1, starting transfers between devices, shards(): rows_before = lax.ppermute(warp_rows[ROWS - HALF_K:], 'ccd', up)  4.35 us
    reshape x2, local copies, waits for them, and re-layouts, shards(): matched.reshape(ROWS // TILE, TILE, CH // TILE, TILE).transpose(2, 0, 1, 3)  4.3 us
    ppermute x1, starting transfers between devices, shards(): before = lax.ppermute(band_rows[ROWS - reach:], 'ccd', up)  4.28 us
    ppermute x1, waiting for transfers between devices, shards(): after = lax.ppermute(band_rows[:reach], 'ccd', down)  4.19 us
    ppermute x1, waiting for transfers between devices, shards(): before = lax.ppermute(band_rows[ROWS - reach:], 'ccd', up)  2.55 us
    reshape x1, local copies, waits for them, and re-layouts, shards(): tile_stack = matched.reshape(ROWS // TILE, TILE, CH // TILE, TILE).transp...  2.46 us
  transfers between devices with their start and end apart: 5, of which 2 were waited for; matrix products, arithmetic and copies ran while one was open for 13% of the time, Pallas kernels for 0%

profile of v2, /device:TPU:1, one launch (start us, length us, event | category | flops | bytes accessed | tf_op | source)
XLA Modules:
  0.0 88.7 jit_solution(6980738155748242764)
XLA Ops:
  0.0 0.8 fusion.38
  0.8 4.3 %collective-permute-start.3 = (s32[10]{0:T(128)S(1)}, s32[10]{0:T(128)S(1)}, u32[]{:S(2)}, u32[]{:S(2)}) collective-permute-start(s32[10]{0:T(128)S(1)} %get-tuple-element.19), channel_id=1, source_target_pairs={{0,1},{1,2},{2,3},{3,4},{4,5},{5,6},{6,7},{7,8},{8,9},{9,10},{10,1... | collective-permute-start | bytes 128 | tf_op jit(solution)/shard_map/ppermute | solution.py:93
  5.2 1.3 %collective-permute-start.4 = (s32[10]{0:T(128)S(1)}, s32[10]{0:T(128)S(1)}, u32[]{:S(2)}, u32[]{:S(2)}) collective-permute-start(s32[10]{0:T(128)S(1)} %get-tuple-element.20), channel_id=1, source_target_pairs={{1,0},{2,1},{3,2},{4,3},{5,4},{6,5},{7,6},{8,7},{9,8},{10,9},{11,1... | collective-permute-start | bytes 128 | tf_op jit(solution)/shard_map/ppermute | solution.py:94
  6.5 1.3 %fusion.5 = bf16[64,2048]{1,0:T(8,128)(2,1)S(1)} fusion(f32[1,1,64,2048]{3,2,1,0:T(8,128)} %param.13, f32[1,1,64,2048]{3,2,1,0:T(8,128)} %param.11, f32[64]{0:T(128)} %bitcast.50), kind=kLoop, calls=%fused_computation.17 | loop fusion | flops 393216 | bytes 1310976 | tf_op jit(solution)/shard_map/squeeze | solution.py:76
  7.8 0.8 pad_dynamic-slice_fusion.1
  8.6 1.0 %collective-permute-start = (bf16[64,1044]{1,0:T(8,128)(2,1)}, bf16[64,1044]{1,0:T(8,128)(2,1)}, u32[]{:S(2)}, u32[]{:S(2)}) collective-permute-start(bf16[64,1044]{1,0:T(8,128)(2,1)} %get-tuple-element.10), channel_id=1, source_target_pairs={{0,128},{128,0},{1,129},{129,1},{2,130},{130,2},{3,131},{131,3},{4... | collective-permute-start | bytes 400904 | tf_op jit(solution)/shard_map/ppermute | solution.py:81
  11.5 1.7 %multiply_add_fusion = (f32[13,128,1]{2,1,0:T(8,128)}, f32[13,128,1]{2,1,0:T(8,128)}) fusion(f32[13]{0:T(128)S(1)} %get-tuple-element.13, f32[13]{0:T(128)S(1)} %get-tuple-element.12, f32[128]{0:T(128)S(1)} %multiply_add_fusion.3, f32[13]{0:T(128)S(1)} %get-tuple-element.14, f32[13]{0:T(128)S(1)} %get-tuple-element.15, f32[13]{0:T(128)S(1)} %get-tuple-element.16), kind=kLoop, calls=%fused_computation.11 | loop fusion | flops 11648 | bytes 14084 | tf_op jit(solution)/shard_map/add | solution.py:116
  13.3 0.7 copy.32.c_ref
  14.5 0.9 %copy.25 = bf16[256,13,128]{0,2,1:T(8,128)(2,1)S(1)} copy(bf16[256,13,128]{2,1,0:T(8,128)(2,1)S(1)} %pad_bitcast_fusion) | data formatting | bytes 1703936 | tf_op jit(solution)/shard_map/transpose | solution.py:107
  15.4 1.4 %copy.31.colm_ref = bf16[256,1664]{1,0:T(8,128)(2,1)} copy(bf16[256,1664]{0,1:T(8,128)(2,1)S(1)} %bitcast.43) | data formatting | bytes 1703936 | tf_op jit(solution)/shard_map/reshape | solution.py:107
  16.8 1.1 %pad.19.rowm_ref = bf16[13,128,160]{2,1,0:T(8,128)(2,1)} pad(bf16[13,128,148]{2,1,0:T(8,128)(2,1)S(1)} %bitcast.42, bf16[]{:T(256)} %constant.20.clone.1), padding=0_0x0_0x0_12 | pad | bytes 1025026 | tf_op jit(solution)/shard_map/jit(_pad)/pad | solution.py:109
  17.9 1.1 %maximum_select_fusion = bf16[128,1044]{1,0:T(8,128)(2,1)S(1)} fusion(bf16[64,1044]{1,0:T(8,128)(2,1)} %collective-permute-done, bf16[64,1044]{1,0:T(8,128)(2,1)S(1)} %get-tuple-element.9, pred[]{:T(512)S(6)} %eq.64), kind=kLoop, calls=%fused_computation.16 | loop fusion | flops 1202688 | bytes 534529 | tf_op jit(solution)/shard_map/jit(_where)/select_n | solution.py:82
  19.0 4.3 %collective-permute-start.1 = (bf16[74,1044]{1,0:T(8,128)(2,1)S(1)}, bf16[74,1044]{1,0:T(8,128)(2,1)S(1)}, u32[]{:S(2)}, u32[]{:S(2)}) collective-permute-start(bf16[74,1044]{1,0:T(8,128)(2,1)S(1)} %get-tuple-element.7), channel_id=1, source_target_pairs={{0,1},{1,2},{2,3},{3,4},{4,5},{5,6},{6,7},{7,8},{8,9},{9,10},{10,1... | collective-permute-start | bytes 463544 | tf_op jit(solution)/shard_map/ppermute | solution.py:90
  23.3 1.3 %collective-permute-start.2 = (bf16[74,1044]{1,0:T(8,128)(2,1)S(1)}, bf16[74,1044]{1,0:T(8,128)(2,1)S(1)}, u32[]{:S(2)}, u32[]{:S(2)}) collective-permute-start(bf16[74,1044]{1,0:T(8,128)(2,1)S(1)} %get-tuple-element.8), channel_id=1, source_target_pairs={{1,0},{2,1},{3,2},{4,3},{5,4},{6,5},{7,6},{8,7},{9,8},{10,9},{11,1... | collective-permute-start | bytes 463544 | tf_op jit(solution)/shard_map/ppermute | solution.py:91
  24.7 2.5 %collective-permute-done.1 = bf16[74,1044]{1,0:T(8,128)(2,1)S(1)} collective-permute-done((bf16[74,1044]{1,0:T(8,128)(2,1)S(1)}, bf16[74,1044]{1,0:T(8,128)(2,1)S(1)}, u32[]{:S(2)}, u32[]{:S(2)}) %collective-permute-start.1) | collective-permute-done | bytes 154544 | tf_op jit(solution)/shard_map/ppermute | solution.py:90
  27.2 4.2 %collective-permute-done.2 = bf16[74,1044]{1,0:T(8,128)(2,1)S(1)} collective-permute-done((bf16[74,1044]{1,0:T(8,128)(2,1)S(1)}, bf16[74,1044]{1,0:T(8,128)(2,1)S(1)}, u32[]{:S(2)}, u32[]{:S(2)}) %collective-permute-start.2) | collective-permute-done | bytes 154544 | tf_op jit(solution)/shard_map/ppermute | solution.py:91
  31.5 1.0 %gather_fusion = bf16[148,1044]{1,0:T(8,128)(2,1)S(1)} fusion(bf16[276,1044]{1,0:T(8,128)(2,1)S(1)} %pad_maximum_fusion, s32[1024]{0:T(1024)S(1)} %pad_clamp_fusion), kind=kCustom, calls=%fused_computation | custom fusion | bytes 618640 | tf_op jit(solution)/shard_map/jit(_take)/gather | solution.py:98
  32.6 0.8 pad.17.img_ref
  33.4 7.7 %shard_map.109 = f32[128,1024]{1,0:T(8,128)} custom-call(bf16[160,1152]{1,0:T(8,128)(2,1)} %pad.17.img_ref, bf16[256,1664]{1,0:T(8,128)(2,1)} %copy.31.colm_ref, bf16[13,128,160]{2,1,0:T(8,128)(2,1)} %pad.19.rowm_ref, f32[13,128,1]{2,1,0:T(8,128)} %get-tuple-element.18.a_ref, f32[13,128,1]{2,1,0:T(8,128)} %get-tuple-element.17.b_ref, ...), custom_call_target="tpu_custom_call" | custom-call | tf_op jit(solution)/shard_map/pallas_call | solution.py:137
  41.0 1.7 %reshape.391 = f32[4,32,32,32]{3,2,1,0:T(8,128)S(1)} reshape(f32[128,1024]{1,0:T(8,128)} %shard_map.109) | data formatting | bytes 1048576 | tf_op jit(solution)/shard_map/reshape | solution.py:153
  42.8 2.5 %copy.38 = f32[4,32,32,32]{3,1,0,2:T(8,128)} copy(f32[4,32,32,32]{3,2,1,0:T(8,128)S(1)} %reshape.391) | data formatting | bytes 1048576 | tf_op jit(solution)/shard_map/reshape | solution.py:153
  45.4 2.5 %reshape.392 = f32[128,1024]{1,0:T(8,128)S(1)} reshape(f32[32,4,32,32]{3,2,1,0:T(8,128)} %bitcast.41) | data formatting | bytes 1048576 | tf_op jit(solution)/shard_map/reshape | solution.py:155
  49.0 38.7 %all_to_all.9 = f32[128,1,1024]{2,1,0:T(1,128)S(1)} all-to-all(f32[128,1,1024]{2,1,0:T(1,128)S(1)} %copy.34), channel_id=1, replica_groups=mesh['section'=2,'ccd'=128] {'ccd'}, dimensions={0} | all-to-all | bytes 1048576 | tf_op jit(solution)/shard_map/all_to_all | solution.py:165
  88.0 0.7 reshape_broadcast_in_dim.3
  (45 shorter events, 4.3 us)
Async XLA Ops:
  0.0 9.6 %copy-start = (f32[13]{0:T(128)S(1)}, f32[13]{0:T(128)}, u32[]{:S(2)}) copy-start(f32[13]{0:T(128)} %constant.91) | copy-start | bytes 160
  0.0 9.6 %copy-start.5 = (pred[13]{0:T(512)(128)(4,1)S(1)}, pred[13]{0:T(512)(128)(4,1)}, u32[]{:S(2)}) copy-start(pred[13]{0:T(512)(128)(4,1)} %constant.90) | copy-start | bytes 43
  0.0 9.7 %copy-start.6 = (pred[13]{0:T(512)(128)(4,1)S(1)}, pred[13]{0:T(512)(128)(4,1)}, u32[]{:S(2)}) copy-start(pred[13]{0:T(512)(128)(4,1)} %constant.89) | copy-start | bytes 43
  0.0 9.7 %copy-start.3 = (pred[13]{0:T(512)(128)(4,1)S(1)}, pred[13]{0:T(512)(128)(4,1)}, u32[]{:S(2)}) copy-start(pred[13]{0:T(512)(128)(4,1)} %constant.88) | copy-start | bytes 43
  0.0 9.7 %copy-start.4 = (pred[13]{0:T(512)(128)(4,1)S(1)}, pred[13]{0:T(512)(128)(4,1)}, u32[]{:S(2)}) copy-start(pred[13]{0:T(512)(128)(4,1)} %constant.87) | copy-start | bytes 43
  0.0 9.9 %copy-start.2 = (f32[13,6]{0,1:T(8,128)S(1)}, f32[13,6]{0,1:T(8,128)}, u32[]{:S(2)}) copy-start(f32[13,6]{0,1:T(8,128)} %param.15) | copy-start | bytes 940
  0.8 23.7 %collective-permute-start.3 = (s32[10]{0:T(128)S(1)}, s32[10]{0:T(128)S(1)}, u32[]{:S(2)}, u32[]{:S(2)}) collective-permute-start(s32[10]{0:T(128)S(1)} %get-tuple-element.19), channel_id=1, source_target_pairs={{0,1},{1,2},{2,3},{3,4},{4,5},{5,6},{6,7},{7,8},{8,9},{9,10},{10,1... | collective-permute-start | bytes 128 | tf_op jit(solution)/shard_map/ppermute | solution.py:93
  5.2 19.4 %collective-permute-start.4 = (s32[10]{0:T(128)S(1)}, s32[10]{0:T(128)S(1)}, u32[]{:S(2)}, u32[]{:S(2)}) collective-permute-start(s32[10]{0:T(128)S(1)} %get-tuple-element.20), channel_id=1, source_target_pairs={{1,0},{2,1},{3,2},{4,3},{5,4},{6,5},{7,6},{8,7},{9,8},{10,9},{11,1... | collective-permute-start | bytes 128 | tf_op jit(solution)/shard_map/ppermute | solution.py:94
  8.6 9.2 %collective-permute-start = (bf16[64,1044]{1,0:T(8,128)(2,1)}, bf16[64,1044]{1,0:T(8,128)(2,1)}, u32[]{:S(2)}, u32[]{:S(2)}) collective-permute-start(bf16[64,1044]{1,0:T(8,128)(2,1)} %get-tuple-element.10), channel_id=1, source_target_pairs={{0,128},{128,0},{1,129},{129,1},{2,130},{130,2},{3,131},{131,3},{4... | collective-permute-start | bytes 400904 | tf_op jit(solution)/shard_map/ppermute | solution.py:81
  16.8 7.8 %copy-start.1 = (s32[128]{0:T(128)S(1)}, s32[128]{0:T(128)}, u32[]{:S(2)}) copy-start(s32[128]{0:T(128)} %param.14) | copy-start | bytes 1540
  19.0 8.3 %collective-permute-start.1 = (bf16[74,1044]{1,0:T(8,128)(2,1)S(1)}, bf16[74,1044]{1,0:T(8,128)(2,1)S(1)}, u32[]{:S(2)}, u32[]{:S(2)}) collective-permute-start(bf16[74,1044]{1,0:T(8,128)(2,1)S(1)} %get-tuple-element.7), channel_id=1, source_target_pairs={{0,1},{1,2},{2,3},{3,4},{4,5},{5,6},{6,7},{7,8},{8,9},{9,10},{10,1... | collective-permute-start | bytes 463544 | tf_op jit(solution)/shard_map/ppermute | solution.py:90
  23.3 8.2 %collective-permute-start.2 = (bf16[74,1044]{1,0:T(8,128)(2,1)S(1)}, bf16[74,1044]{1,0:T(8,128)(2,1)S(1)}, u32[]{:S(2)}, u32[]{:S(2)}) collective-permute-start(bf16[74,1044]{1,0:T(8,128)(2,1)S(1)} %get-tuple-element.8), channel_id=1, source_target_pairs={{1,0},{2,1},{3,2},{4,3},{5,4},{6,5},{7,6},{8,7},{9,8},{10,9},{11,1... | collective-permute-start | bytes 463544 | tf_op jit(solution)/shard_map/ppermute | solution.py:91
  45.4 2.5 %copy-start.7 = (f32[1,1,128]{2,1,0:T(1,128)S(1)}, f32[1,1,128]{2,1,0:T(1,128)}, u32[]{:S(2)}) copy-start(f32[1,1,128]{2,1,0:T(1,128)} %param.17) | copy-start | bytes 1540
  45.4 2.5 %copy-start.8 = (s32[1,1,128,1]{2,3,1,0:T(1,128)S(1)}, s32[1,1,128,1]{2,3,1,0:T(1,128)}, u32[]{:S(2)}) copy-start(s32[1,1,128,1]{2,3,1,0:T(1,128)} %param.16) | copy-start | bytes 1540

commit v3 on v2

--- a/solution.py
+++ b/solution.py
@@ -3,6 +3,7 @@
 from jax import lax
 from jax.sharding import PartitionSpec as P
 from jax.experimental import pallas as pl
+from jax.experimental.pallas import tpu as pltpu
 
 ROWS = 128
 TILE = 32
@@ -116,7 +117,18 @@
     slope_part = poly[:, 2] + poly[:, 4] * row_coord
     square_part = poly[:, 5]
 
-    def match_kernel(img_ref, colm_ref, rowm_ref, a_ref, b_ref, c_ref, v_ref, out_ref):
+    owners = tile_owner.reshape(-1)
+    weights = tile_weight.reshape(-1)
+    selector = jnp.where(
+        jnp.arange(band_count)[:, None] == owners[None, :], weights[None, :], 0.0
+    )
+    groups = TILE * TILE // STRIP
+    tiles = selector.shape[1]
+    row_tiles = ROWS // TILE
+    per_lane = STRIP // TILE
+
+    def match_kernel(img_ref, colm_ref, rowm_ref, a_ref, b_ref, c_ref, v_ref, s_ref,
+                     out_ref, acc_ref, pack_ref):
         i = pl.program_id(0)
         offset = pl.multiple_of(i * STRIP, STRIP)
         strip = img_ref[:, pl.ds(offset, span)]
@@ -131,10 +143,33 @@
             )
             coef = a_ref[k] + v * (b_ref[k] + c_ref[k] * v)
             acc = acc + coef * vert
-        out_ref[...] = acc
+        acc_ref[...] = acc
+        lane_group = lax.broadcasted_iota(jnp.int32, (groups, STRIP), 1) // TILE
+        for rb in range(row_tiles):
+            picked = [
+                acc_ref[pl.ds(rb * TILE + g, groups, stride=per_lane), :] for g in range(per_lane)
+            ]
+            for cbl in range(per_lane):
+                packed = jnp.zeros((groups, STRIP), jnp.float32)
+                for g in range(per_lane):
+                    shift = ((g - cbl) % per_lane) * TILE
+                    rolled = pltpu.roll(picked[g], shift, 1) if shift else picked[g]
+                    packed = jnp.where(lane_group == g, rolled, packed)
+                j = (i * per_lane + cbl) * row_tiles + rb
+                pack_ref[pl.ds(pl.multiple_of(j * groups, groups), groups), :] = packed
+
+        @pl.when(i == strips - 1)
+        def _():
+            sel = s_ref[...]
+            for q in range(groups):
+                part = pack_ref[pl.ds(q, tiles, stride=groups), :]
+                out_ref[pl.ds(q, band_count, stride=groups), :] = jnp.dot(
+                    sel, part, precision=lax.Precision.HIGHEST,
+                    preferred_element_type=jnp.float32,
+                )
 
     full = lambda shape: pl.BlockSpec(shape, lambda i: (0,) * len(shape))
-    matched = pl.pallas_call(
+    outgoing = pl.pallas_call(
         match_kernel,
         grid=(strips,),
         in_specs=[
@@ -145,23 +180,16 @@
             full(slope_part.shape),
             full(square_part.shape),
             pl.BlockSpec((1, 1, STRIP), lambda i: (i, 0, 0)),
+            full(selector.shape),
         ],
-        out_specs=pl.BlockSpec((ROWS, STRIP), lambda i: (0, i)),
-        out_shape=jax.ShapeDtypeStruct((ROWS, CH), jnp.float32),
-    )(image, col_matrix, row_matrix, row_part, slope_part, square_part, col_coord)
-    tile_stack = (
-        matched.reshape(ROWS // TILE, TILE, CH // TILE, TILE)
-        .transpose(2, 0, 1, 3)
-        .reshape(-1, TILE * TILE)
-    )
-    owners = tile_owner.reshape(-1)
-    weights = tile_weight.reshape(-1)
-    selector = jnp.where(
-        jnp.arange(band_count)[:, None] == owners[None, :], weights[None, :], 0.0
-    )
-    outgoing = jnp.dot(
-        selector, tile_stack, precision=lax.Precision.HIGHEST, preferred_element_type=jnp.float32
-    )
+        out_specs=full((band_count * groups, STRIP)),
+        out_shape=jax.ShapeDtypeStruct((band_count * groups, STRIP), jnp.float32),
+        scratch_shapes=[
+            pltpu.VMEM((ROWS, STRIP), jnp.float32),
+            pltpu.VMEM((tiles * groups, STRIP), jnp.float32),
+        ],
+    )(image, col_matrix, row_matrix, row_part, slope_part, square_part, col_coord, selector)
+    outgoing = outgoing.reshape(band_count, groups, STRIP)
     incoming = lax.all_to_all(outgoing, "ccd", split_axis=0, concat_axis=0, tiled=True)
     patch_sum = jnp.sum(incoming, axis=0, keepdims=True)
     return patch_sum.reshape(1, 1, TILE, TILE)

time: 89.1 us -> 81.7 us (0.917)
  local copies, waits for them, and re-layouts: 16.1 us -> 8.17 us
  Pallas kernels: 7.66 us -> 9.09 us
    reshape x3 -> x0, local copies, waits for them, and re-layouts: 6.76 us -> none  [the longest x2 4.3 us: shards(): matched.reshape(ROWS // TILE, TILE, CH // TILE, TILE).transpose(2, 0, 1, 3)]
    pallas_call x1, Pallas kernels: 7.66 us -> 9.09 us  [shards(): pl.pallas_call(match_kernel, grid=(strips,), in_specs=[full(image.shape),...]
    select_n x1, other arithmetic: 1.05 us -> 0.06 us  [shards(): jnp.where(half == 0, jnp.concatenate([own, received], axis=0), jnp.concat...]
where the time goes in v3:
time: 81.7 us; the launch traced here: 81.3 us
  blocking collectives  38.9 us (48%)
  starting transfers between devices  12.3 us (15%)
  Pallas kernels  9.09 us (11%)
  local copies, waits for them, and re-layouts  8.17 us (10%)
  waiting for transfers between devices  6.72 us (8%)
  other arithmetic  4.95 us (6%)
  matrix products  0.94 us (1%)
    all_to_all x1, blocking collectives, shards(): lax.all_to_all(outgoing, 'ccd', split_axis=0, concat_axis=0, tiled=True)  38.9 us
    pallas_call x1, Pallas kernels, shards(): pl.pallas_call(match_kernel, grid=(strips,), in_specs=[full(image.shape),...  9.09 us
    ppermute x1, starting transfers between devices, shards(): rows_before = lax.ppermute(warp_rows[ROWS - HALF_K:], 'ccd', up)  4.35 us
    ppermute x1, starting transfers between devices, shards(): before = lax.ppermute(band_rows[ROWS - reach:], 'ccd', up)  4.28 us
    ppermute x1, waiting for transfers between devices, shards(): after = lax.ppermute(band_rows[:reach], 'ccd', down)  4.19 us
    ppermute x1, waiting for transfers between devices, shards(): before = lax.ppermute(band_rows[ROWS - reach:], 'ccd', up)  2.52 us
    add x1, other arithmetic, shards(): slope_part = poly[:, 2] + poly[:, 4] * row_coord  1.67 us
  transfers between devices with their start and end apart: 5, of which 2 were waited for; matrix products, arithmetic and copies ran while one was open for 13% of the time, Pallas kernels for 0%

profile of v3, /device:TPU:1, one launch (start us, length us, event | category | flops | bytes accessed | tf_op | source)
XLA Modules:
  0.0 81.3 jit_solution(12868175301179134757)
XLA Ops:
  0.0 0.8 fusion.34
  0.8 4.3 %collective-permute-start.3 = (s32[10]{0:T(128)S(1)}, s32[10]{0:T(128)S(1)}, u32[]{:S(2)}, u32[]{:S(2)}) collective-permute-start(s32[10]{0:T(128)S(1)} %get-tuple-element.19), channel_id=1, source_target_pairs={{0,1},{1,2},{2,3},{3,4},{4,5},{5,6},{6,7},{7,8},{8,9},{9,10},{10,1... | collective-permute-start | bytes 128 | tf_op jit(solution)/shard_map/ppermute | solution.py:94
  5.2 1.3 %collective-permute-start.4 = (s32[10]{0:T(128)S(1)}, s32[10]{0:T(128)S(1)}, u32[]{:S(2)}, u32[]{:S(2)}) collective-permute-start(s32[10]{0:T(128)S(1)} %get-tuple-element.20), channel_id=1, source_target_pairs={{1,0},{2,1},{3,2},{4,3},{5,4},{6,5},{7,6},{8,7},{9,8},{10,9},{11,1... | collective-permute-start | bytes 128 | tf_op jit(solution)/shard_map/ppermute | solution.py:95
  6.5 1.3 %fusion.5 = bf16[64,2048]{1,0:T(8,128)(2,1)S(1)} fusion(f32[1,1,64,2048]{3,2,1,0:T(8,128)} %param.13, f32[1,1,64,2048]{3,2,1,0:T(8,128)} %param.11, f32[64]{0:T(128)} %bitcast.41), kind=kLoop, calls=%fused_computation.15 | loop fusion | flops 393216 | bytes 1310976 | tf_op jit(solution)/shard_map/squeeze | solution.py:77
  8.0 1.0 %collective-permute-start = (bf16[64,1044]{1,0:T(8,128)(2,1)S(1)}, bf16[64,1044]{1,0:T(8,128)(2,1)S(1)}, u32[]{:S(2)}, u32[]{:S(2)}) collective-permute-start(bf16[64,1044]{1,0:T(8,128)(2,1)S(1)} %get-tuple-element.10), channel_id=1, source_target_pairs={{0,128},{128,0},{1,129},{129,1},{2,130},{130,2},{3,131},{131,3},{4... | collective-permute-start | bytes 400904 | tf_op jit(solution)/shard_map/ppermute | solution.py:82
  9.4 0.6 multiply_add_fusion.2.v_ref
  10.0 0.5 fusion
  10.5 0.5 fusion.2
  11.0 0.6 fusion.6.s_ref
  11.6 1.7 %multiply_add_fusion = (f32[13,128,1]{2,1,0:T(8,128)}, f32[13,128,1]{2,1,0:T(8,128)}) fusion(f32[13]{0:T(128)S(1)} %get-tuple-element.13, f32[13]{0:T(128)S(1)} %get-tuple-element.12, f32[128]{0:T(128)S(1)} %multiply_add_fusion.3, f32[13]{0:T(128)S(1)} %get-tuple-element.14, f32[13]{0:T(128)S(1)} %get-tuple-element.15, f32[13]{0:T(128)S(1)} %get-tuple-element.16), kind=kLoop, calls=%fused_computation.9 | loop fusion | flops 11648 | bytes 14084 | tf_op jit(solution)/shard_map/add | solution.py:117
  13.5 0.7 copy.25.c_ref
  14.3 0.3 copy.20
  14.6 0.9 %copy.18 = bf16[256,13,128]{0,2,1:T(8,128)(2,1)S(1)} copy(bf16[256,13,128]{2,1,0:T(8,128)(2,1)S(1)} %pad_bitcast_fusion) | data formatting | bytes 1703936 | tf_op jit(solution)/shard_map/transpose | solution.py:108
  15.5 1.4 %copy.24.colm_ref = bf16[256,1664]{1,0:T(8,128)(2,1)} copy(bf16[256,1664]{0,1:T(8,128)(2,1)S(1)} %bitcast.35) | data formatting | bytes 1703936 | tf_op jit(solution)/shard_map/reshape | solution.py:108
  16.9 1.1 %pad.19.rowm_ref = bf16[13,128,160]{2,1,0:T(8,128)(2,1)} pad(bf16[13,128,148]{2,1,0:T(8,128)(2,1)S(1)} %bitcast.34, bf16[]{:T(256)} %constant.19.clone.1), padding=0_0x0_0x0_12 | pad | bytes 1025026 | tf_op jit(solution)/shard_map/jit(_pad)/pad | solution.py:110
  18.1 4.3 %collective-permute-start.1 = (bf16[74,1044]{1,0:T(8,128)(2,1)S(1)}, bf16[74,1044]{1,0:T(8,128)(2,1)S(1)}, u32[]{:S(2)}, u32[]{:S(2)}) collective-permute-start(bf16[74,1044]{1,0:T(8,128)(2,1)S(1)} %get-tuple-element.7), channel_id=1, source_target_pairs={{0,1},{1,2},{2,3},{3,4},{4,5},{5,6},{6,7},{7,8},{8,9},{9,10},{10,1... | collective-permute-start | bytes 463544 | tf_op jit(solution)/shard_map/ppermute | solution.py:91
  22.4 1.3 %collective-permute-start.2 = (bf16[74,1044]{1,0:T(8,128)(2,1)S(1)}, bf16[74,1044]{1,0:T(8,128)(2,1)S(1)}, u32[]{:S(2)}, u32[]{:S(2)}) collective-permute-start(bf16[74,1044]{1,0:T(8,128)(2,1)S(1)} %get-tuple-element.8), channel_id=1, source_target_pairs={{1,0},{2,1},{3,2},{4,3},{5,4},{6,5},{7,6},{8,7},{9,8},{10,9},{11,1... | collective-permute-start | bytes 463544 | tf_op jit(solution)/shard_map/ppermute | solution.py:92
  23.8 2.5 %collective-permute-done.1 = bf16[74,1044]{1,0:T(8,128)(2,1)S(1)} collective-permute-done((bf16[74,1044]{1,0:T(8,128)(2,1)S(1)}, bf16[74,1044]{1,0:T(8,128)(2,1)S(1)}, u32[]{:S(2)}, u32[]{:S(2)}) %collective-permute-start.1) | collective-permute-done | bytes 154544 | tf_op jit(solution)/shard_map/ppermute | solution.py:91
  26.3 4.2 %collective-permute-done.2 = bf16[74,1044]{1,0:T(8,128)(2,1)S(1)} collective-permute-done((bf16[74,1044]{1,0:T(8,128)(2,1)S(1)}, bf16[74,1044]{1,0:T(8,128)(2,1)S(1)}, u32[]{:S(2)}, u32[]{:S(2)}) %collective-permute-start.2) | collective-permute-done | bytes 154544 | tf_op jit(solution)/shard_map/ppermute | solution.py:92
  30.7 1.0 %gather_fusion = bf16[148,1044]{1,0:T(8,128)(2,1)S(1)} fusion(bf16[276,1044]{1,0:T(8,128)(2,1)S(1)} %pad_maximum_fusion, s32[1024]{0:T(1024)S(1)} %pad_clamp_fusion), kind=kCustom, calls=%fused_computation | custom fusion | bytes 618640 | tf_op jit(solution)/shard_map/jit(_take)/gather | solution.py:99
  31.7 0.8 pad.17.img_ref
  32.5 9.1 %shard_map.109 = f32[1024,128]{1,0:T(8,128)} custom-call(bf16[160,1152]{1,0:T(8,128)(2,1)} %pad.17.img_ref, bf16[256,1664]{1,0:T(8,128)(2,1)} %copy.24.colm_ref, bf16[13,128,160]{2,1,0:T(8,128)(2,1)} %pad.19.rowm_ref, f32[13,128,1]{2,1,0:T(8,128)} %get-tuple-element.18.a_ref, f32[13,128,1]{2,1,0:T(8,128)} %get-tuple-element.17.b_ref, ...), custom_call_target="tpu_custom_call" | custom-call | tf_op jit(solution)/shard_map/pallas_call | solution.py:172
  41.6 38.9 %all_to_all.5 = f32[128,8,128]{2,1,0:T(8,128)S(1)} all-to-all(f32[128,8,128]{2,1,0:T(8,128)} %bitcast.36), channel_id=1, replica_groups=mesh['section'=2,'ccd'=128] {'ccd'}, dimensions={0} | all-to-all | bytes 1048576 | tf_op jit(solution)/shard_map/all_to_all | solution.py:193
  80.6 0.7 reshape_broadcast_in_dim.3
  (41 shorter events, 1.3 us)
Async XLA Ops:
  0.0 9.1 %copy-start = (f32[13]{0:T(128)S(1)}, f32[13]{0:T(128)}, u32[]{:S(2)}) copy-start(f32[13]{0:T(128)} %constant.91) | copy-start | bytes 160
  0.0 9.1 %copy-start.5 = (pred[13]{0:T(512)(128)(4,1)S(1)}, pred[13]{0:T(512)(128)(4,1)}, u32[]{:S(2)}) copy-start(pred[13]{0:T(512)(128)(4,1)} %constant.90) | copy-start | bytes 43
  0.0 9.1 %copy-start.6 = (pred[13]{0:T(512)(128)(4,1)S(1)}, pred[13]{0:T(512)(128)(4,1)}, u32[]{:S(2)}) copy-start(pred[13]{0:T(512)(128)(4,1)} %constant.89) | copy-start | bytes 43
  0.0 9.1 %copy-start.3 = (pred[13]{0:T(512)(128)(4,1)S(1)}, pred[13]{0:T(512)(128)(4,1)}, u32[]{:S(2)}) copy-start(pred[13]{0:T(512)(128)(4,1)} %constant.88) | copy-start | bytes 43
  0.0 9.1 %copy-start.4 = (pred[13]{0:T(512)(128)(4,1)S(1)}, pred[13]{0:T(512)(128)(4,1)}, u32[]{:S(2)}) copy-start(pred[13]{0:T(512)(128)(4,1)} %constant.87) | copy-start | bytes 43
  0.0 9.4 %copy-start.2 = (f32[13,6]{0,1:T(8,128)S(1)}, f32[13,6]{0,1:T(8,128)}, u32[]{:S(2)}) copy-start(f32[13,6]{0,1:T(8,128)} %param.15) | copy-start | bytes 940
  0.8 22.9 %collective-permute-start.3 = (s32[10]{0:T(128)S(1)}, s32[10]{0:T(128)S(1)}, u32[]{:S(2)}, u32[]{:S(2)}) collective-permute-start(s32[10]{0:T(128)S(1)} %get-tuple-element.19), channel_id=1, source_target_pairs={{0,1},{1,2},{2,3},{3,4},{4,5},{5,6},{6,7},{7,8},{8,9},{9,10},{10,1... | collective-permute-start | bytes 128 | tf_op jit(solution)/shard_map/ppermute | solution.py:94
  5.2 18.5 %collective-permute-start.4 = (s32[10]{0:T(128)S(1)}, s32[10]{0:T(128)S(1)}, u32[]{:S(2)}, u32[]{:S(2)}) collective-permute-start(s32[10]{0:T(128)S(1)} %get-tuple-element.20), channel_id=1, source_target_pairs={{1,0},{2,1},{3,2},{4,3},{5,4},{6,5},{7,6},{8,7},{9,8},{10,9},{11,1... | collective-permute-start | bytes 128 | tf_op jit(solution)/shard_map/ppermute | solution.py:95
  7.8 3.1 %copy-start.7 = (f32[1,1,128]{2,1,0:T(1,128)S(1)}, f32[1,1,128]{2,1,0:T(1,128)}, u32[]{:S(2)}) copy-start(f32[1,1,128]{2,1,0:T(1,128)} %param.17) | copy-start | bytes 1540
  7.8 3.1 %copy-start.8 = (s32[1,1,128,1]{2,3,1,0:T(1,128)S(1)}, s32[1,1,128,1]{2,3,1,0:T(1,128)}, u32[]{:S(2)}) copy-start(s32[1,1,128,1]{2,3,1,0:T(1,128)} %param.16) | copy-start | bytes 1540
  8.0 10.0 %collective-permute-start = (bf16[64,1044]{1,0:T(8,128)(2,1)S(1)}, bf16[64,1044]{1,0:T(8,128)(2,1)S(1)}, u32[]{:S(2)}, u32[]{:S(2)}) collective-permute-start(bf16[64,1044]{1,0:T(8,128)(2,1)S(1)} %get-tuple-element.10), channel_id=1, source_target_pairs={{0,128},{128,0},{1,129},{129,1},{2,130},{130,2},{3,131},{131,3},{4... | collective-permute-start | bytes 400904 | tf_op jit(solution)/shard_map/ppermute | solution.py:82
  18.0 5.7 %copy-start.1 = (s32[128]{0:T(128)S(1)}, s32[128]{0:T(128)}, u32[]{:S(2)}) copy-start(s32[128]{0:T(128)} %param.14) | copy-start | bytes 1540
  18.1 8.2 %collective-permute-start.1 = (bf16[74,1044]{1,0:T(8,128)(2,1)S(1)}, bf16[74,1044]{1,0:T(8,128)(2,1)S(1)}, u32[]{:S(2)}, u32[]{:S(2)}) collective-permute-start(bf16[74,1044]{1,0:T(8,128)(2,1)S(1)} %get-tuple-element.7), channel_id=1, source_target_pairs={{0,1},{1,2},{2,3},{3,4},{4,5},{5,6},{6,7},{7,8},{8,9},{9,10},{10,1... | collective-permute-start | bytes 463544 | tf_op jit(solution)/shard_map/ppermute | solution.py:91
  22.4 8.1 %collective-permute-start.2 = (bf16[74,1044]{1,0:T(8,128)(2,1)S(1)}, bf16[74,1044]{1,0:T(8,128)(2,1)S(1)}, u32[]{:S(2)}, u32[]{:S(2)}) collective-permute-start(bf16[74,1044]{1,0:T(8,128)(2,1)S(1)} %get-tuple-element.8), channel_id=1, source_target_pairs={{1,0},{2,1},{3,2},{4,3},{5,4},{6,5},{7,6},{8,7},{9,8},{10,9},{11,1... | collective-permute-start | bytes 463544 | tf_op jit(solution)/shard_map/ppermute | solution.py:92

commit v4 on v3

--- a/solution.py
+++ b/solution.py
@@ -74,35 +74,60 @@
     top_row = lax.axis_index("ccd") * ROWS
     left_col = lax.axis_index("section") * CH
     half = lax.axis_index("section")
+    strips = CH // STRIP
+    wide_cols = strips * STRIP + STRIP
+    rh = raw_counts.shape[2]
     calibrated = ((raw_counts - overscan[..., None]) * response).astype(jnp.bfloat16)[0, 0]
+    shifts = (warp_rows - (top_row + jnp.arange(ROWS))).astype(jnp.bfloat16)
+    my_shifts = lax.dynamic_slice_in_dim(shifts, half * rh, rh)[:, None]
     wide = jnp.pad(calibrated, ((0, 0), (HALF_K, HALF_K)))
     width = CH + 2 * HALF_K
-    own = lax.dynamic_slice_in_dim(wide, half * CH, width, 1)
-    other = lax.dynamic_slice_in_dim(wide, (1 - half) * CH, width, 1)
-    received = lax.ppermute(other, "section", [(0, 1), (1, 0)])
-    band_rows = jnp.where(
+    filler = jnp.zeros((rh, wide_cols - width - 1), jnp.bfloat16)
+
+    def slab(col_start):
+        cols = lax.dynamic_slice_in_dim(wide, col_start, width, 1)
+        return jnp.concatenate([cols, my_shifts, filler], axis=1)
+
+    own = slab(half * CH)
+    other = slab((1 - half) * CH)
+    nb = band_count
+    dev = lambda s, b: s * nb + b
+    axes = ("section", "ccd")
+    swap = [(dev(s, b), dev(1 - s, b)) for s in range(2) for b in range(nb)]
+    cross = [(dev(1, b), dev(0, b + 1)) for b in range(nb - 1)] + [
+        (dev(0, b), dev(1, b - 1)) for b in range(1, nb)
+    ]
+    straight = [(dev(1, b), dev(1, b + 1)) for b in range(nb - 1)] + [
+        (dev(0, b), dev(0, b - 1)) for b in range(1, nb)
+    ]
+    straight_down = [(dev(0, b), dev(0, b + 1)) for b in range(nb - 1)] + [
+        (dev(1, b), dev(1, b - 1)) for b in range(1, nb)
+    ]
+    cross_down = [(dev(0, b), dev(1, b + 1)) for b in range(nb - 1)] + [
+        (dev(1, b), dev(0, b - 1)) for b in range(1, nb)
+    ]
+    edge = lambda x: jnp.where(half == 0, x[rh - HALF_K :], x[:HALF_K])
+    got_swap = lax.ppermute(other, axes, swap)
+    got_cross = lax.ppermute(other, axes, cross)
+    got_straight = lax.ppermute(own, axes, straight)
+    got_edge = lax.ppermute(edge(own), axes, straight_down)
+    got_edge_cross = lax.ppermute(edge(other), axes, cross_down)
+    window = jnp.where(
         half == 0,
-        jnp.concatenate([own, received], axis=0),
-        jnp.concatenate([received, own], axis=0),
+        jnp.concatenate([got_edge, got_cross, own, got_swap, got_straight, got_edge_cross], axis=0),
+        jnp.concatenate([got_edge_cross, got_straight, got_swap, own, got_cross, got_edge], axis=0),
     )
     reach = REACH + HALF_K
-    up = [(i, i + 1) for i in range(band_count - 1)]
-    down = [(i + 1, i) for i in range(band_count - 1)]
-    before = lax.ppermute(band_rows[ROWS - reach :], "ccd", up)
-    after = lax.ppermute(band_rows[:reach], "ccd", down)
-    window = jnp.concatenate([before, band_rows, after], axis=0)
-    rows_before = lax.ppermute(warp_rows[ROWS - HALF_K :], "ccd", up)
-    rows_after = lax.ppermute(warp_rows[:HALF_K], "ccd", down)
-    sources = jnp.concatenate([rows_before, warp_rows, rows_after])
-    out_rows = top_row - HALF_K + jnp.arange(ROWS + 2 * HALF_K)
+    lead = ROWS + 2 * HALF_K
+    steps = window[REACH : REACH + lead, width].astype(jnp.int32)
+    picks = jnp.arange(lead) + REACH + steps
+    out_rows = top_row - HALF_K + jnp.arange(lead)
     inside = (out_rows >= 0) & (out_rows < total_rows)
-    warped = jnp.take(window, sources - (top_row - reach), axis=0, mode="clip")
+    warped = jnp.take(window, picks, axis=0, mode="clip")
     padded = jnp.where(inside[:, None], warped, jnp.zeros((), warped.dtype))
-    strips = CH // STRIP
     span = 2 * STRIP
-    lead = ROWS + 2 * HALF_K
     lead_pad = -(-lead // 16) * 16
-    image = jnp.pad(padded, ((0, lead_pad - lead), (0, strips * STRIP + STRIP - padded.shape[1])))
+    image = jnp.pad(padded, ((0, lead_pad - lead), (0, 0)))
     col_band = band_matrix(basis_taps(column_power), STRIP)
     col_band = jnp.pad(col_band, ((0, 0), (0, span - col_band.shape[1]), (0, 0)))
     col_matrix = col_band.transpose(1, 0, 2).reshape(span, NBASIS * STRIP)

time: 81.7 us -> 76.5 us (0.936)
  waiting for transfers between devices: 6.72 us -> 0.01 us
  local copies, waits for them, and re-layouts: 8.17 us -> 10.7 us
  blocking collectives: 38.9 us -> 37.6 us
    ppermute x5, waiting for transfers between devices: 6.72 us -> 0.01 us  [the longest x1 0.01 us: shards(): got_straight = lax.ppermute(own, axes, straight)]
    concatenate x0 -> x4, local copies, waits for them, and re-layouts: none -> 3.2 us  [the longest x1 1.5 us: shards(): jnp.concatenate([got_edge_cross, got_straight, got_swap, own, got_cross,...]
    all_to_all x1, blocking collectives: 38.9 us -> 37.6 us  [shards(): lax.all_to_all(outgoing, 'ccd', split_axis=0, concat_axis=0, tiled=True)]
    slice x2 -> x0, local copies, waits for them, and re-layouts: 0.85 us -> none  [the longest x1 0.8 us: shards(): rows_before = lax.ppermute(warp_rows[ROWS - HALF_K:], 'ccd', up)]
  transfers between devices with their start and end apart: 5 -> 5, of which waited for: 2 -> 0; matrix products, arithmetic and copies ran while one was open for 13% -> 12% of each run, Pallas kernels for 0% -> 0%
where the time goes in v4:
time: 76.5 us; the launch traced here: 76.2 us
  blocking collectives  37.6 us (49%)
  starting transfers between devices  11.8 us (15%)
  local copies, waits for them, and re-layouts  10.7 us (14%)
  Pallas kernels  9.07 us (12%)
  other arithmetic  5.65 us (7%)
  matrix products  0.95 us (1%)
    all_to_all x1, blocking collectives, shards(): lax.all_to_all(outgoing, 'ccd', split_axis=0, concat_axis=0, tiled=True)  37.6 us
    pallas_call x1, Pallas kernels, shards(): pl.pallas_call(match_kernel, grid=(strips,), in_specs=[full(image.shape),...  9.07 us
    ppermute x1, starting transfers between devices, shards(): got_straight = lax.ppermute(own, axes, straight)  4.64 us
    ppermute x1, starting transfers between devices, shards(): got_swap = lax.ppermute(other, axes, swap)  3.29 us
    ppermute x1, starting transfers between devices, shards(): got_cross = lax.ppermute(other, axes, cross)  1.91 us
    add x1, other arithmetic, shards(): slope_part = poly[:, 2] + poly[:, 4] * row_coord  1.66 us
  transfers between devices with their start and end apart: 5, of which 0 were waited for; matrix products, arithmetic and copies ran while one was open for 12% of the time, Pallas kernels for 0%

profile of v4, /device:TPU:1, one launch (start us, length us, event | category | flops | bytes accessed | tf_op | source)
XLA Modules:
  0.0 76.2 jit_solution(1755999530234411787)
XLA Ops:
  0.0 0.7 subtract_convert_fusion
  0.9 1.3 %fusion.5 = bf16[64,2048]{1,0:T(8,128)(2,1)S(1)} fusion(f32[1,1,64,2048]{3,2,1,0:T(8,128)} %param.13, f32[1,1,64,2048]{3,2,1,0:T(8,128)} %param.11, f32[64]{0:T(128)} %bitcast.37), kind=kLoop, calls=%fused_computation.14 | loop fusion | flops 393216 | bytes 1310976 | tf_op jit(solution)/shard_map/squeeze | solution.py:80
  2.6 3.3 %collective-permute-start.2 = (bf16[64,1152]{1,0:T(8,128)(2,1)S(1)}, bf16[64,1152]{1,0:T(8,128)(2,1)S(1)}, u32[]{:S(2)}, u32[]{:S(2)}) collective-permute-start(bf16[64,1152]{1,0:T(8,128)(2,1)S(1)} %concatenate.13), channel_id=1, source_target_pairs={{0,128},{1,129},{2,130},{3,131},{4,132},{5,133},{6,134},{7,135},{8... | collective-permute-start | bytes 442376 | tf_op jit(solution)/shard_map/ppermute | solution.py:110
  5.9 1.9 %collective-permute-start.1 = (bf16[64,1152]{1,0:T(8,128)(2,1)S(1)}, bf16[64,1152]{1,0:T(8,128)(2,1)S(1)}, u32[]{:S(2)}, u32[]{:S(2)}) collective-permute-start(bf16[64,1152]{1,0:T(8,128)(2,1)S(1)} %concatenate.13), channel_id=1, source_target_pairs={{128,1},{129,2},{130,3},{131,4},{132,5},{133,6},{134,7},{135,8},{1... | collective-permute-start | bytes 442376 | tf_op jit(solution)/shard_map/ppermute | solution.py:111
  7.8 0.7 collective-permute-start.4
  8.6 4.6 %collective-permute-start.3 = (bf16[64,1152]{1,0:T(8,128)(2,1)S(1)}, bf16[64,1152]{1,0:T(8,128)(2,1)S(1)}, u32[]{:S(2)}, u32[]{:S(2)}) collective-permute-start(bf16[64,1152]{1,0:T(8,128)(2,1)S(1)} %concatenate.12), channel_id=1, source_target_pairs={{128,129},{129,130},{130,131},{131,132},{132,133},{133,134},{134,1... | collective-permute-start | bytes 442376 | tf_op jit(solution)/shard_map/ppermute | solution.py:112
  13.2 1.3 %collective-permute-start = (bf16[10,1152]{1,0:T(8,128)(2,1)S(1)}, bf16[10,1152]{1,0:T(8,128)(2,1)S(1)}, u32[]{:S(2)}, u32[]{:S(2)}) collective-permute-start(bf16[10,1152]{1,0:T(8,128)(2,1)S(1)} %slice_select_fusion.1), channel_id=1, source_target_pairs={{0,1},{1,2},{2,3},{3,4},{4,5},{5,6},{6,7},{7,8},{8,9},{9,10},{10,1... | collective-permute-start | bytes 69128 | tf_op jit(solution)/shard_map/ppermute | solution.py:113
  14.9 0.6 multiply_add_fusion.2.v_ref
  15.5 0.5 fusion
  16.0 0.5 fusion.2
  16.5 0.6 fusion.6.s_ref
  17.1 1.7 %multiply_add_fusion = (f32[13,128,1]{2,1,0:T(8,128)}, f32[13,128,1]{2,1,0:T(8,128)}) fusion(f32[13]{0:T(128)S(1)} %get-tuple-element.11, f32[13]{0:T(128)S(1)} %get-tuple-element.10, f32[128]{0:T(128)S(1)} %multiply_add_fusion.3, f32[13]{0:T(128)S(1)} %get-tuple-element.12, f32[13]{0:T(128)S(1)} %get-tuple-element.13, f32[13]{0:T(128)S(1)} %get-tuple-element.14), kind=kLoop, calls=%fused_computation.9 | loop fusion | flops 11648 | bytes 14084 | tf_op jit(solution)/shard_map/add | solution.py:142
  18.9 0.7 copy.31.c_ref
  19.8 0.3 copy.26
  20.1 1.1 %pad.19.rowm_ref = bf16[13,128,160]{2,1,0:T(8,128)(2,1)} pad(bf16[13,128,148]{2,1,0:T(8,128)(2,1)S(1)} %bitcast.32, bf16[]{:T(256)} %constant.30.clone.1), padding=0_0x0_0x0_12 | pad | bytes 1025026 | tf_op jit(solution)/shard_map/jit(_pad)/pad | solution.py:135
  21.2 0.9 %copy.24 = bf16[256,13,128]{0,2,1:T(8,128)(2,1)S(1)} copy(bf16[256,13,128]{2,1,0:T(8,128)(2,1)S(1)} %pad_bitcast_fusion) | data formatting | bytes 1703936 | tf_op jit(solution)/shard_map/transpose | solution.py:133
  22.1 1.4 %copy.30.colm_ref = bf16[256,1664]{1,0:T(8,128)(2,1)} copy(bf16[256,1664]{0,1:T(8,128)(2,1)S(1)} %bitcast.33) | data formatting | bytes 1703936 | tf_op jit(solution)/shard_map/reshape | solution.py:133
  23.5 1.5 %concatenate.15 = bf16[276,1152]{1,0:T(8,128)(2,1)S(1)} concatenate(bf16[10,1152]{1,0:T(8,128)(2,1)S(1)} %collective-permute-done.4, bf16[64,1152]{1,0:T(8,128)(2,1)S(1)} %collective-permute-done.3, bf16[64,1152]{1,0:T(8,128)(2,1)S(1)} %collective-permute-done.2, bf16[64,1152]{1,0:T(8,128)(2,1)S(1)} %concatenate.12, bf16[64,1152]{1,0:T(8,128)(2,1)S(1)} %collective-permute-done.1, ...), dimensions={0} | concatenate | bytes 1271808 | tf_op jit(solution)/shard_map/concatenate | solution.py:118
  25.0 1.5 %concatenate.14 = bf16[276,1152]{1,0:T(8,128)(2,1)S(1)} concatenate(bf16[10,1152]{1,0:T(8,128)(2,1)S(1)} %collective-permute-done, bf16[64,1152]{1,0:T(8,128)(2,1)S(1)} %collective-permute-done.1, bf16[64,1152]{1,0:T(8,128)(2,1)S(1)} %concatenate.12, bf16[64,1152]{1,0:T(8,128)(2,1)S(1)} %collective-permute-done.2, bf16[64,1152]{1,0:T(8,128)(2,1)S(1)} %collective-permute-done.3, ...), dimensions={0} | concatenate | bytes 1271808 | tf_op jit(solution)/shard_map/concatenate | solution.py:117
  26.8 1.0 %gather_fusion = bf16[148,1152]{1,0:T(8,128)(2,1)S(1)} fusion(bf16[276,1152]{1,0:T(8,128)(2,1)S(1)} %broadcast_select_fusion, s32[1024]{0:T(1024)S(1)} %pad_clamp_fusion), kind=kCustom, calls=%fused_computation | custom fusion | bytes 682576 | tf_op jit(solution)/shard_map/jit(_take)/gather | solution.py:126
  27.9 0.8 pad.17.img_ref
  28.6 9.1 %shard_map.109 = f32[1024,128]{1,0:T(8,128)} custom-call(bf16[160,1152]{1,0:T(8,128)(2,1)} %pad.17.img_ref, bf16[256,1664]{1,0:T(8,128)(2,1)} %copy.30.colm_ref, bf16[13,128,160]{2,1,0:T(8,128)(2,1)} %pad.19.rowm_ref, f32[13,128,1]{2,1,0:T(8,128)} %get-tuple-element.16.a_ref, f32[13,128,1]{2,1,0:T(8,128)} %get-tuple-element.15.b_ref, ...), custom_call_target="tpu_custom_call" | custom-call | tf_op jit(solution)/shard_map/pallas_call | solution.py:197
  37.7 37.6 %all_to_all.5 = f32[128,8,128]{2,1,0:T(8,128)S(1)} all-to-all(f32[128,8,128]{2,1,0:T(8,128)} %bitcast.34), channel_id=1, replica_groups=mesh['section'=2,'ccd'=128] {'ccd'}, dimensions={0} | all-to-all | bytes 1048576 | tf_op jit(solution)/shard_map/all_to_all | solution.py:218
  75.5 0.7 reshape_broadcast_in_dim.3
  (46 shorter events, 1.7 us)
Async XLA Ops:
  2.2 12.4 %copy-start = (f32[13]{0:T(128)S(1)}, f32[13]{0:T(128)}, u32[]{:S(2)}) copy-start(f32[13]{0:T(128)} %constant.92) | copy-start | bytes 160
  2.2 12.4 %copy-start.2 = (pred[13]{0:T(512)(128)(4,1)S(1)}, pred[13]{0:T(512)(128)(4,1)}, u32[]{:S(2)}) copy-start(pred[13]{0:T(512)(128)(4,1)} %constant.89) | copy-start | bytes 43
  2.2 12.4 %copy-start.3 = (pred[13]{0:T(512)(128)(4,1)S(1)}, pred[13]{0:T(512)(128)(4,1)}, u32[]{:S(2)}) copy-start(pred[13]{0:T(512)(128)(4,1)} %constant.88) | copy-start | bytes 43
  2.2 12.4 %copy-start.4 = (pred[13]{0:T(512)(128)(4,1)S(1)}, pred[13]{0:T(512)(128)(4,1)}, u32[]{:S(2)}) copy-start(pred[13]{0:T(512)(128)(4,1)} %constant.91) | copy-start | bytes 43
  2.2 12.4 %copy-start.5 = (pred[13]{0:T(512)(128)(4,1)S(1)}, pred[13]{0:T(512)(128)(4,1)}, u32[]{:S(2)}) copy-start(pred[13]{0:T(512)(128)(4,1)} %constant.90) | copy-start | bytes 43
  2.2 12.6 %copy-start.1 = (f32[13,6]{0,1:T(8,128)S(1)}, f32[13,6]{0,1:T(8,128)}, u32[]{:S(2)}) copy-start(f32[13,6]{0,1:T(8,128)} %param.15) | copy-start | bytes 940
  2.5 13.9 %copy-start.6 = (f32[1,1,128]{2,1,0:T(1,128)S(1)}, f32[1,1,128]{2,1,0:T(1,128)}, u32[]{:S(2)}) copy-start(f32[1,1,128]{2,1,0:T(1,128)} %param.17) | copy-start | bytes 1540
  2.6 13.9 %copy-start.7 = (s32[1,1,128,1]{2,3,1,0:T(1,128)S(1)}, s32[1,1,128,1]{2,3,1,0:T(1,128)}, u32[]{:S(2)}) copy-start(s32[1,1,128,1]{2,3,1,0:T(1,128)} %param.16) | copy-start | bytes 1540
  2.6 20.9 %collective-permute-start.2 = (bf16[64,1152]{1,0:T(8,128)(2,1)S(1)}, bf16[64,1152]{1,0:T(8,128)(2,1)S(1)}, u32[]{:S(2)}, u32[]{:S(2)}) collective-permute-start(bf16[64,1152]{1,0:T(8,128)(2,1)S(1)} %concatenate.13), channel_id=1, source_target_pairs={{0,128},{1,129},{2,130},{3,131},{4,132},{5,133},{6,134},{7,135},{8... | collective-permute-start | bytes 442376 | tf_op jit(solution)/shard_map/ppermute | solution.py:110
  5.9 17.6 %collective-permute-start.1 = (bf16[64,1152]{1,0:T(8,128)(2,1)S(1)}, bf16[64,1152]{1,0:T(8,128)(2,1)S(1)}, u32[]{:S(2)}, u32[]{:S(2)}) collective-permute-start(bf16[64,1152]{1,0:T(8,128)(2,1)S(1)} %concatenate.13), channel_id=1, source_target_pairs={{128,1},{129,2},{130,3},{131,4},{132,5},{133,6},{134,7},{135,8},{1... | collective-permute-start | bytes 442376 | tf_op jit(solution)/shard_map/ppermute | solution.py:111
  7.8 15.7 %collective-permute-start.4 = (bf16[10,1152]{1,0:T(8,128)(2,1)S(1)}, bf16[10,1152]{1,0:T(8,128)(2,1)S(1)}, u32[]{:S(2)}, u32[]{:S(2)}) collective-permute-start(bf16[10,1152]{1,0:T(8,128)(2,1)S(1)} %slice_select_fusion), channel_id=1, source_target_pairs={{0,129},{1,130},{2,131},{3,132},{4,133},{5,134},{6,135},{7,136},{8... | collective-permute-start | bytes 69128 | tf_op jit(solution)/shard_map/ppermute | solution.py:114
  8.6 14.9 %collective-permute-start.3 = (bf16[64,1152]{1,0:T(8,128)(2,1)S(1)}, bf16[64,1152]{1,0:T(8,128)(2,1)S(1)}, u32[]{:S(2)}, u32[]{:S(2)}) collective-permute-start(bf16[64,1152]{1,0:T(8,128)(2,1)S(1)} %concatenate.12), channel_id=1, source_target_pairs={{128,129},{129,130},{130,131},{131,132},{132,133},{133,134},{134,1... | collective-permute-start | bytes 442376 | tf_op jit(solution)/shard_map/ppermute | solution.py:112
  13.2 10.2 %collective-permute-start = (bf16[10,1152]{1,0:T(8,128)(2,1)S(1)}, bf16[10,1152]{1,0:T(8,128)(2,1)S(1)}, u32[]{:S(2)}, u32[]{:S(2)}) collective-permute-start(bf16[10,1152]{1,0:T(8,128)(2,1)S(1)} %slice_select_fusion.1), channel_id=1, source_target_pairs={{0,1},{1,2},{2,3},{3,4},{4,5},{5,6},{6,7},{7,8},{8,9},{9,10},{10,1... | collective-permute-start | bytes 69128 | tf_op jit(solution)/shard_map/ppermute | solution.py:113

commit v5 on v4

--- a/solution.py
+++ b/solution.py
@@ -112,61 +112,65 @@
     got_straight = lax.ppermute(own, axes, straight)
     got_edge = lax.ppermute(edge(own), axes, straight_down)
     got_edge_cross = lax.ppermute(edge(other), axes, cross_down)
-    window = jnp.where(
-        half == 0,
-        jnp.concatenate([got_edge, got_cross, own, got_swap, got_straight, got_edge_cross], axis=0),
-        jnp.concatenate([got_edge_cross, got_straight, got_swap, own, got_cross, got_edge], axis=0),
+    pick = lambda a, b: jnp.where(half == 0, a, b)
+    window = jnp.concatenate(
+        [
+            pick(got_edge, got_edge_cross),
+            pick(got_cross, got_straight),
+            pick(own, got_swap),
+            pick(got_swap, own),
+            pick(got_straight, got_cross),
+            pick(got_edge_cross, got_edge),
+        ],
+        axis=0,
     )
-    reach = REACH + HALF_K
     lead = ROWS + 2 * HALF_K
+    lead_pad = -(-lead // 16) * 16
     steps = window[REACH : REACH + lead, width].astype(jnp.int32)
-    picks = jnp.arange(lead) + REACH + steps
-    out_rows = top_row - HALF_K + jnp.arange(lead)
-    inside = (out_rows >= 0) & (out_rows < total_rows)
+    picks = jnp.pad(jnp.arange(lead) + REACH + steps, (0, lead_pad - lead))
+    out_rows = top_row - HALF_K + jnp.arange(lead_pad)
+    inside = (out_rows >= 0) & (out_rows < total_rows) & (jnp.arange(lead_pad) < lead)
     warped = jnp.take(window, picks, axis=0, mode="clip")
-    padded = jnp.where(inside[:, None], warped, jnp.zeros((), warped.dtype))
+    image = jnp.where(inside[:, None], warped, jnp.zeros((), warped.dtype))
     span = 2 * STRIP
-    lead_pad = -(-lead // 16) * 16
-    image = jnp.pad(padded, ((0, lead_pad - lead), (0, 0)))
     col_band = band_matrix(basis_taps(column_power), STRIP)
     col_band = jnp.pad(col_band, ((0, 0), (0, span - col_band.shape[1]), (0, 0)))
     col_matrix = col_band.transpose(1, 0, 2).reshape(span, NBASIS * STRIP)
     row_matrix = band_matrix(basis_taps(row_power), ROWS).transpose(0, 2, 1)
     row_matrix = jnp.pad(row_matrix, ((0, 0), (0, 0), (0, lead_pad - lead)))
-    row_pos = (top_row + jnp.arange(ROWS)).astype(jnp.float32)
-    row_coord = (2.0 * (row_pos + 0.5) / total_rows - 1.0)[None, :, None]
-    col_pos = (left_col + jnp.arange(CH)).astype(jnp.float32)
-    col_coord = (2.0 * (col_pos + 0.5) / total_cols - 1.0).reshape(strips, 1, STRIP)
-    poly = kernel_poly[:, :, None, None]
-    row_part = poly[:, 0] + poly[:, 1] * row_coord + poly[:, 3] * row_coord * row_coord
-    slope_part = poly[:, 2] + poly[:, 4] * row_coord
-    square_part = poly[:, 5]
-
-    owners = tile_owner.reshape(-1)
-    weights = tile_weight.reshape(-1)
-    selector = jnp.where(
-        jnp.arange(band_count)[:, None] == owners[None, :], weights[None, :], 0.0
-    )
+    positions = jnp.stack([top_row, left_col]).astype(jnp.int32)
+    owners = tile_owner.reshape(1, -1)
+    weights = tile_weight.reshape(1, -1)
     groups = TILE * TILE // STRIP
-    tiles = selector.shape[1]
+    tiles = owners.shape[1]
     row_tiles = ROWS // TILE
     per_lane = STRIP // TILE
 
-    def match_kernel(img_ref, colm_ref, rowm_ref, a_ref, b_ref, c_ref, v_ref, s_ref,
-                     out_ref, acc_ref, pack_ref):
+    def match_kernel(kp_ref, pos_ref, img_ref, colm_ref, rowm_ref, own_ref, w_ref,
+                     out_ref, acc_ref, pack_ref, a_ref, b_ref):
         i = pl.program_id(0)
+
+        @pl.when(i == 0)
+        def _():
+            rows = lax.broadcasted_iota(jnp.int32, (ROWS, STRIP), 0) + pos_ref[0]
+            u = 2.0 * (rows.astype(jnp.float32) + 0.5) / total_rows - 1.0
+            for k in range(NBASIS):
+                a_ref[k] = kp_ref[k, 0] + kp_ref[k, 1] * u + kp_ref[k, 3] * u * u
+                b_ref[k] = kp_ref[k, 2] + kp_ref[k, 4] * u
+
         offset = pl.multiple_of(i * STRIP, STRIP)
         strip = img_ref[:, pl.ds(offset, span)]
         across = jnp.dot(strip, colm_ref[...], preferred_element_type=jnp.float32)
         across = across.astype(jnp.bfloat16)
-        v = v_ref[0]
+        cols = lax.broadcasted_iota(jnp.int32, (1, STRIP), 1) + (pos_ref[1] + i * STRIP)
+        v = 2.0 * (cols.astype(jnp.float32) + 0.5) / total_cols - 1.0
         acc = jnp.zeros((ROWS, STRIP), jnp.float32)
         for k in range(NBASIS):
             vert = jnp.dot(
                 rowm_ref[k], across[:, k * STRIP : (k + 1) * STRIP],
                 preferred_element_type=jnp.float32,
             )
-            coef = a_ref[k] + v * (b_ref[k] + c_ref[k] * v)
+            coef = a_ref[k] + v * (b_ref[k] + kp_ref[k, 5] * v)
             acc = acc + coef * vert
         acc_ref[...] = acc
         lane_group = lax.broadcasted_iota(jnp.int32, (groups, STRIP), 1) // TILE
@@ -185,7 +189,8 @@
 
         @pl.when(i == strips - 1)
         def _():
-            sel = s_ref[...]
+            owner_ids = lax.broadcasted_iota(jnp.int32, (band_count, tiles), 0)
+            sel = jnp.where(owner_ids == own_ref[...], w_ref[...], 0.0)
             for q in range(groups):
                 part = pack_ref[pl.ds(q, tiles, stride=groups), :]
                 out_ref[pl.ds(q, band_count, stride=groups), :] = jnp.dot(
@@ -198,22 +203,23 @@
         match_kernel,
         grid=(strips,),
         in_specs=[
+            pl.BlockSpec(memory_space=pltpu.SMEM),
+            pl.BlockSpec(memory_space=pltpu.SMEM),
             full(image.shape),
             full(col_matrix.shape),
             full(row_matrix.shape),
-            full(row_part.shape),
-            full(slope_part.shape),
-            full(square_part.shape),
-            pl.BlockSpec((1, 1, STRIP), lambda i: (i, 0, 0)),
-            full(selector.shape),
+            full(owners.shape),
+            full(weights.shape),
         ],
         out_specs=full((band_count * groups, STRIP)),
         out_shape=jax.ShapeDtypeStruct((band_count * groups, STRIP), jnp.float32),
         scratch_shapes=[
             pltpu.VMEM((ROWS, STRIP), jnp.float32),
             pltpu.VMEM((tiles * groups, STRIP), jnp.float32),
+            pltpu.VMEM((NBASIS, ROWS, STRIP), jnp.float32),
+            pltpu.VMEM((NBASIS, ROWS, STRIP), jnp.float32),
         ],
-    )(image, col_matrix, row_matrix, row_part, slope_part, square_part, col_coord, selector)
+    )(kernel_poly, positions, image, col_matrix, row_matrix, owners, weights)
     outgoing = outgoing.reshape(band_count, groups, STRIP)
     incoming = lax.all_to_all(outgoing, "ccd", split_axis=0, concat_axis=0, tiled=True)
     patch_sum = jnp.sum(incoming, axis=0, keepdims=True)

time: 76.5 us -> 72.7 us (0.950)
  local copies, waits for them, and re-layouts: 10.7 us -> 8.46 us
  blocking collectives: 37.6 us -> 39.2 us
  other arithmetic: 5.65 us -> 4.18 us
  starting transfers between devices: 11.8 us -> 10.5 us
    add x2 -> x1, other arithmetic: 1.85 us -> 0.01 us  [shards(): picks = jnp.pad(jnp.arange(lead) + REACH + steps, (0, lead_pad - lead))]
    all_to_all x1, blocking collectives: 37.6 us -> 39.2 us  [shards(): lax.all_to_all(outgoing, 'ccd', split_axis=0, concat_axis=0, tiled=True)]
    concatenate x2 -> x1, local copies, waits for them, and re-layouts: 3 us -> 1.5 us  [shards(): jnp.concatenate([pick(got_edge, got_edge_cross), pick(got_cross, got_stra...]
    ppermute x1, starting transfers between devices: 4.64 us -> 3.38 us  [shards(): got_straight = lax.ppermute(own, axes, straight)]
  transfers between devices with their start and end apart: 5 -> 5, of which waited for: 0 -> 0; matrix products, arithmetic and copies ran while one was open for 12% -> 9% of each run, Pallas kernels for 0% -> 0%
where the time goes in v5:
time: 72.7 us; the launch traced here: 72.4 us
  blocking collectives  39.2 us (54%)
  starting transfers between devices  10.5 us (14%)
  Pallas kernels  8.76 us (12%)
  local copies, waits for them, and re-layouts  8.46 us (12%)
  other arithmetic  4.18 us (6%)
  matrix products  0.95 us (1%)
    all_to_all x1, blocking collectives, shards(): lax.all_to_all(outgoing, 'ccd', split_axis=0, concat_axis=0, tiled=True)  39.2 us
    pallas_call x1, Pallas kernels, shards(): pl.pallas_call(match_kernel, grid=(strips,), in_specs=[pl.BlockSpec(memor...  8.76 us
    ppermute x1, starting transfers between devices, shards(): got_straight = lax.ppermute(own, axes, straight)  3.38 us
    ppermute x1, starting transfers between devices, shards(): got_swap = lax.ppermute(other, axes, swap)  3.29 us
    ppermute x1, starting transfers between devices, shards(): got_cross = lax.ppermute(other, axes, cross)  1.91 us
    concatenate x1, local copies, waits for them, and re-layouts, shards(): jnp.concatenate([pick(got_edge, got_edge_cross), pick(got_cross, got_stra...  1.5 us
  transfers between devices with their start and end apart: 5, of which 0 were waited for; matrix products, arithmetic and copies ran while one was open for 9% of the time, Pallas kernels for 0%

profile of v5, /device:TPU:1, one launch (start us, length us, event | category | flops | bytes accessed | tf_op | source)
XLA Modules:
  0.0 72.4 jit_solution(11678175441573389161)
XLA Ops:
  0.0 0.7 subtract_convert_fusion
  0.9 1.3 %fusion.5 = bf16[64,2048]{1,0:T(8,128)(2,1)S(1)} fusion(f32[1,1,64,2048]{3,2,1,0:T(8,128)} %param.13, f32[1,1,64,2048]{3,2,1,0:T(8,128)} %param.11, f32[64]{0:T(128)} %bitcast.23), kind=kLoop, calls=%fused_computation.11 | loop fusion | flops 393216 | bytes 1310976 | tf_op jit(solution)/shard_map/squeeze | solution.py:80
  2.2 0.2 pad_dynamic-slice_fusion
  2.5 3.3 %collective-permute-start.4 = (bf16[64,1152]{1,0:T(8,128)(2,1)S(1)}, bf16[64,1152]{1,0:T(8,128)(2,1)S(1)}, u32[]{:S(2)}, u32[]{:S(2)}) collective-permute-start(bf16[64,1152]{1,0:T(8,128)(2,1)S(1)} %concatenate.13), channel_id=1, source_target_pairs={{0,128},{1,129},{2,130},{3,131},{4,132},{5,133},{6,134},{7,135},{8... | collective-permute-start | bytes 442376 | tf_op jit(solution)/shard_map/ppermute | solution.py:110
  5.8 1.9 %collective-permute-start.2 = (bf16[64,1152]{1,0:T(8,128)(2,1)S(1)}, bf16[64,1152]{1,0:T(8,128)(2,1)S(1)}, u32[]{:S(2)}, u32[]{:S(2)}) collective-permute-start(bf16[64,1152]{1,0:T(8,128)(2,1)S(1)} %concatenate.13), channel_id=1, source_target_pairs={{128,1},{129,2},{130,3},{131,4},{132,5},{133,6},{134,7},{135,8},{1... | collective-permute-start | bytes 442376 | tf_op jit(solution)/shard_map/ppermute | solution.py:111
  7.8 3.4 %collective-permute-start.3 = (bf16[64,1152]{1,0:T(8,128)(2,1)S(1)}, bf16[64,1152]{1,0:T(8,128)(2,1)S(1)}, u32[]{:S(2)}, u32[]{:S(2)}) collective-permute-start(bf16[64,1152]{1,0:T(8,128)(2,1)S(1)} %concatenate.12), channel_id=1, source_target_pairs={{128,129},{129,130},{130,131},{131,132},{132,133},{133,134},{134,1... | collective-permute-start | bytes 442376 | tf_op jit(solution)/shard_map/ppermute | solution.py:112
  11.3 1.3 %collective-permute-start = (bf16[10,1152]{1,0:T(8,128)(2,1)S(1)}, bf16[10,1152]{1,0:T(8,128)(2,1)S(1)}, u32[]{:S(2)}, u32[]{:S(2)}) collective-permute-start(bf16[10,1152]{1,0:T(8,128)(2,1)S(1)} %slice_select_fusion.1), channel_id=1, source_target_pairs={{0,1},{1,2},{2,3},{3,4},{4,5},{5,6},{6,7},{7,8},{8,9},{9,10},{10,1... | collective-permute-start | bytes 69128 | tf_op jit(solution)/shard_map/ppermute | solution.py:113
  12.6 0.7 collective-permute-start.1
  13.4 0.2 multiply_reduce_fusion
  13.6 0.5 fusion.2
  14.2 0.5 fusion
  14.7 0.7 pad_add_fusion.pos_ref
  15.4 0.9 %copy.24 = bf16[256,13,128]{0,2,1:T(8,128)(2,1)S(1)} copy(bf16[256,13,128]{2,1,0:T(8,128)(2,1)S(1)} %pad_bitcast_fusion) | data formatting | bytes 1703936 | tf_op jit(solution)/shard_map/transpose | solution.py:138
  16.3 1.4 %copy.28.colm_ref = bf16[256,1664]{1,0:T(8,128)(2,1)} copy(bf16[256,1664]{0,1:T(8,128)(2,1)S(1)} %bitcast.21) | data formatting | bytes 1703936 | tf_op jit(solution)/shard_map/reshape | solution.py:138
  17.8 0.3 copy.26
  18.1 1.1 %pad.19.rowm_ref = bf16[13,128,160]{2,1,0:T(8,128)(2,1)} pad(bf16[13,128,148]{2,1,0:T(8,128)(2,1)S(1)} %bitcast.20, bf16[]{:T(256)} %constant.13.clone.1), padding=0_0x0_0x0_12 | pad | bytes 1025026 | tf_op jit(solution)/shard_map/jit(_pad)/pad | solution.py:140
  19.2 0.7 copy.27.kp_ref
  20.0 0.2 convert_reduce_fusion
  20.3 1.5 %concatenate.14 = bf16[276,1152]{1,0:T(8,128)(2,1)S(1)} concatenate(bf16[10,1152]{1,0:T(8,128)(2,1)S(1)} %get-tuple-element.14, bf16[64,1152]{1,0:T(8,128)(2,1)S(1)} %get-tuple-element.8, bf16[64,1152]{1,0:T(8,128)(2,1)S(1)} %get-tuple-element.10, bf16[64,1152]{1,0:T(8,128)(2,1)S(1)} %get-tuple-element.9, bf16[64,1152]{1,0:T(8,128)(2,1)S(1)} %get-tuple-element.7, ...), dimensions={0} | concatenate | bytes 1271808 | tf_op jit(solution)/shard_map/concatenate | solution.py:116
  21.8 1.0 %gather_fusion = bf16[160,1152]{1,0:T(8,128)(2,1)S(1)} fusion(bf16[276,1152]{1,0:T(8,128)(2,1)S(1)} %concatenate.14, s32[1024]{0:T(1024)S(1)} %select_clamp_fusion), kind=kCustom, calls=%fused_computation | custom fusion | bytes 737920 | tf_op jit(solution)/shard_map/jit(_take)/gather | solution.py:133
  22.8 0.8 %broadcast_select_fusion.img_ref = bf16[160,1152]{1,0:T(8,128)(2,1)} fusion(bf16[160,1152]{1,0:T(8,128)(2,1)S(1)} %gather_fusion, pred[160]{0:T(512)(128)(4,1)S(1)} %compare_and_fusion), kind=kLoop, calls=%fused_computation.10 | loop fusion | flops 184320 | bytes 737440 | tf_op jit(solution)/shard_map/jit(_where)/select_n | solution.py:134
  23.6 8.8 %shard_map.109 = f32[1024,128]{1,0:T(8,128)} custom-call(f32[13,6]{1,0:T(8,128)} %copy.27.kp_ref, s32[2]{0:T(128)} %pad_add_fusion.pos_ref, bf16[160,1152]{1,0:T(8,128)(2,1)} %broadcast_select_fusion.img_ref, bf16[256,1664]{1,0:T(8,128)(2,1)} %copy.28.colm_ref, bf16[13,128,160]{2,1,0:T(8,128)(2,1)} %pad.19.rowm_ref, s32[1,128]{1,0:T(1,128)} %bitcast.24, ...), custom_call_target="tpu_custom_call" | custom-call | tf_op jit(solution)/shard_map/pallas_call | solution.py:202
  32.4 39.2 %all_to_all.5 = f32[128,8,128]{2,1,0:T(8,128)S(1)} all-to-all(f32[128,8,128]{2,1,0:T(8,128)} %bitcast.22), channel_id=1, replica_groups=mesh['section'=2,'ccd'=128] {'ccd'}, dimensions={0} | all-to-all | bytes 1048576 | tf_op jit(solution)/shard_map/all_to_all | solution.py:224
  71.8 0.7 reshape_broadcast_in_dim.3
  (38 shorter events, 1.1 us)
Async XLA Ops:
  2.2 11.1 %copy-start = (f32[13]{0:T(128)S(1)}, f32[13]{0:T(128)}, u32[]{:S(2)}) copy-start(f32[13]{0:T(128)} %constant.73) | copy-start | bytes 160
  2.2 11.1 %copy-start.2 = (pred[13]{0:T(512)(128)(4,1)S(1)}, pred[13]{0:T(512)(128)(4,1)}, u32[]{:S(2)}) copy-start(pred[13]{0:T(512)(128)(4,1)} %constant.71) | copy-start | bytes 43
  2.2 11.1 %copy-start.3 = (pred[13]{0:T(512)(128)(4,1)S(1)}, pred[13]{0:T(512)(128)(4,1)}, u32[]{:S(2)}) copy-start(pred[13]{0:T(512)(128)(4,1)} %constant.72) | copy-start | bytes 43
  2.2 11.1 %copy-start.4 = (pred[13]{0:T(512)(128)(4,1)S(1)}, pred[13]{0:T(512)(128)(4,1)}, u32[]{:S(2)}) copy-start(pred[13]{0:T(512)(128)(4,1)} %constant.69) | copy-start | bytes 43
  2.2 11.1 %copy-start.5 = (pred[13]{0:T(512)(128)(4,1)S(1)}, pred[13]{0:T(512)(128)(4,1)}, u32[]{:S(2)}) copy-start(pred[13]{0:T(512)(128)(4,1)} %constant.70) | copy-start | bytes 43
  2.5 17.4 %collective-permute-start.4 = (bf16[64,1152]{1,0:T(8,128)(2,1)S(1)}, bf16[64,1152]{1,0:T(8,128)(2,1)S(1)}, u32[]{:S(2)}, u32[]{:S(2)}) collective-permute-start(bf16[64,1152]{1,0:T(8,128)(2,1)S(1)} %concatenate.13), channel_id=1, source_target_pairs={{0,128},{1,129},{2,130},{3,131},{4,132},{5,133},{6,134},{7,135},{8... | collective-permute-start | bytes 442376 | tf_op jit(solution)/shard_map/ppermute | solution.py:110
  5.8 14.2 %collective-permute-start.2 = (bf16[64,1152]{1,0:T(8,128)(2,1)S(1)}, bf16[64,1152]{1,0:T(8,128)(2,1)S(1)}, u32[]{:S(2)}, u32[]{:S(2)}) collective-permute-start(bf16[64,1152]{1,0:T(8,128)(2,1)S(1)} %concatenate.13), channel_id=1, source_target_pairs={{128,1},{129,2},{130,3},{131,4},{132,5},{133,6},{134,7},{135,8},{1... | collective-permute-start | bytes 442376 | tf_op jit(solution)/shard_map/ppermute | solution.py:111
  7.8 12.1 %collective-permute-start.3 = (bf16[64,1152]{1,0:T(8,128)(2,1)S(1)}, bf16[64,1152]{1,0:T(8,128)(2,1)S(1)}, u32[]{:S(2)}, u32[]{:S(2)}) collective-permute-start(bf16[64,1152]{1,0:T(8,128)(2,1)S(1)} %concatenate.12), channel_id=1, source_target_pairs={{128,129},{129,130},{130,131},{131,132},{132,133},{133,134},{134,1... | collective-permute-start | bytes 442376 | tf_op jit(solution)/shard_map/ppermute | solution.py:112
  11.3 8.6 %collective-permute-start = (bf16[10,1152]{1,0:T(8,128)(2,1)S(1)}, bf16[10,1152]{1,0:T(8,128)(2,1)S(1)}, u32[]{:S(2)}, u32[]{:S(2)}) collective-permute-start(bf16[10,1152]{1,0:T(8,128)(2,1)S(1)} %slice_select_fusion.1), channel_id=1, source_target_pairs={{0,1},{1,2},{2,3},{3,4},{4,5},{5,6},{6,7},{7,8},{8,9},{9,10},{10,1... | collective-permute-start | bytes 69128 | tf_op jit(solution)/shard_map/ppermute | solution.py:113
  12.6 7.3 %collective-permute-start.1 = (bf16[10,1152]{1,0:T(8,128)(2,1)S(1)}, bf16[10,1152]{1,0:T(8,128)(2,1)S(1)}, u32[]{:S(2)}, u32[]{:S(2)}) collective-permute-start(bf16[10,1152]{1,0:T(8,128)(2,1)S(1)} %slice_select_fusion), channel_id=1, source_target_pairs={{0,129},{1,130},{2,131},{3,132},{4,133},{5,134},{6,135},{7,136},{8... | collective-permute-start | bytes 69128 | tf_op jit(solution)/shard_map/ppermute | solution.py:114
  18.1 1.1 %copy-start.1 = (f32[13,6]{0,1:T(8,128)S(1)}, f32[13,6]{0,1:T(8,128)}, u32[]{:S(2)}) copy-start(f32[13,6]{0,1:T(8,128)} %param.15) | copy-start | bytes 940

commit v6 on v5

--- a/solution.py
+++ b/solution.py
@@ -221,8 +221,9 @@
         ],
     )(kernel_poly, positions, image, col_matrix, row_matrix, owners, weights)
     outgoing = outgoing.reshape(band_count, groups, STRIP)
+    outgoing = outgoing.astype(jnp.bfloat16)
     incoming = lax.all_to_all(outgoing, "ccd", split_axis=0, concat_axis=0, tiled=True)
-    patch_sum = jnp.sum(incoming, axis=0, keepdims=True)
+    patch_sum = jnp.sum(incoming.astype(jnp.float32), axis=0, keepdims=True)
     return patch_sum.reshape(1, 1, TILE, TILE)
 
 

time: 72.7 us -> 68.2 us (0.938)
  blocking collectives: 39.2 us -> 33.6 us
  other arithmetic: 4.18 us -> 5.24 us
    all_to_all x1, blocking collectives: 39.2 us -> 33.6 us  [shards(): lax.all_to_all(outgoing, 'ccd', split_axis=0, concat_axis=0, tiled=True)]
    convert_element_type x0 -> x1, other arithmetic: none -> 1.07 us  [shards(): outgoing = outgoing.astype(jnp.bfloat16)]
  transfers between devices with their start and end apart: 5 -> 5, of which waited for: 0 -> 0; matrix products, arithmetic and copies ran while one was open for 9% -> 10% of each run, Pallas kernels for 0% -> 0%
where the time goes in v6:
time: 68.2 us; the launch traced here: 67.9 us
  blocking collectives  33.6 us (49%)
  starting transfers between devices  10.5 us (15%)
  Pallas kernels  8.76 us (13%)
  local copies, waits for them, and re-layouts  8.46 us (12%)
  other arithmetic  5.24 us (8%)
  matrix products  0.95 us (1%)
    all_to_all x1, blocking collectives, shards(): lax.all_to_all(outgoing, 'ccd', split_axis=0, concat_axis=0, tiled=True)  33.6 us
    pallas_call x1, Pallas kernels, shards(): pl.pallas_call(match_kernel, grid=(strips,), in_specs=[pl.BlockSpec(memor...  8.76 us
    ppermute x1, starting transfers between devices, shards(): got_straight = lax.ppermute(own, axes, straight)  3.38 us
    ppermute x1, starting transfers between devices, shards(): got_swap = lax.ppermute(other, axes, swap)  3.29 us
    ppermute x1, starting transfers between devices, shards(): got_cross = lax.ppermute(other, axes, cross)  1.91 us
    concatenate x1, local copies, waits for them, and re-layouts, shards(): jnp.concatenate([pick(got_edge, got_edge_cross), pick(got_cross, got_stra...  1.5 us
  transfers between devices with their start and end apart: 5, of which 0 were waited for; matrix products, arithmetic and copies ran while one was open for 10% of the time, Pallas kernels for 0%

profile of v6, /device:TPU:1, one launch (start us, length us, event | category | flops | bytes accessed | tf_op | source)
XLA Modules:
  0.0 67.9 jit_solution(3316280877440022948)
XLA Ops:
  0.0 0.7 subtract_convert_fusion
  0.9 1.3 %fusion.5 = bf16[64,2048]{1,0:T(8,128)(2,1)S(1)} fusion(f32[1,1,64,2048]{3,2,1,0:T(8,128)} %param.13, f32[1,1,64,2048]{3,2,1,0:T(8,128)} %param.11, f32[64]{0:T(128)} %bitcast.23), kind=kLoop, calls=%fused_computation.12 | loop fusion | flops 393216 | bytes 1310976 | tf_op jit(solution)/shard_map/squeeze | solution.py:80
  2.5 3.3 %collective-permute-start.4 = (bf16[64,1152]{1,0:T(8,128)(2,1)S(1)}, bf16[64,1152]{1,0:T(8,128)(2,1)S(1)}, u32[]{:S(2)}, u32[]{:S(2)}) collective-permute-start(bf16[64,1152]{1,0:T(8,128)(2,1)S(1)} %concatenate.13), channel_id=1, source_target_pairs={{0,128},{1,129},{2,130},{3,131},{4,132},{5,133},{6,134},{7,135},{8... | collective-permute-start | bytes 442376 | tf_op jit(solution)/shard_map/ppermute | solution.py:110
  5.8 1.9 %collective-permute-start.2 = (bf16[64,1152]{1,0:T(8,128)(2,1)S(1)}, bf16[64,1152]{1,0:T(8,128)(2,1)S(1)}, u32[]{:S(2)}, u32[]{:S(2)}) collective-permute-start(bf16[64,1152]{1,0:T(8,128)(2,1)S(1)} %concatenate.13), channel_id=1, source_target_pairs={{128,1},{129,2},{130,3},{131,4},{132,5},{133,6},{134,7},{135,8},{1... | collective-permute-start | bytes 442376 | tf_op jit(solution)/shard_map/ppermute | solution.py:111
  7.8 3.4 %collective-permute-start.3 = (bf16[64,1152]{1,0:T(8,128)(2,1)S(1)}, bf16[64,1152]{1,0:T(8,128)(2,1)S(1)}, u32[]{:S(2)}, u32[]{:S(2)}) collective-permute-start(bf16[64,1152]{1,0:T(8,128)(2,1)S(1)} %concatenate.12), channel_id=1, source_target_pairs={{128,129},{129,130},{130,131},{131,132},{132,133},{133,134},{134,1... | collective-permute-start | bytes 442376 | tf_op jit(solution)/shard_map/ppermute | solution.py:112
  11.3 1.3 %collective-permute-start = (bf16[10,1152]{1,0:T(8,128)(2,1)S(1)}, bf16[10,1152]{1,0:T(8,128)(2,1)S(1)}, u32[]{:S(2)}, u32[]{:S(2)}) collective-permute-start(bf16[10,1152]{1,0:T(8,128)(2,1)S(1)} %slice_select_fusion.1), channel_id=1, source_target_pairs={{0,1},{1,2},{2,3},{3,4},{4,5},{5,6},{6,7},{7,8},{8,9},{9,10},{10,1... | collective-permute-start | bytes 69128 | tf_op jit(solution)/shard_map/ppermute | solution.py:113
  12.6 0.7 collective-permute-start.1
  13.4 0.2 multiply_reduce_fusion
  13.6 0.5 fusion.2
  14.2 0.5 fusion
  14.7 0.7 pad_add_fusion.pos_ref
  15.4 0.9 %copy.24 = bf16[256,13,128]{0,2,1:T(8,128)(2,1)S(1)} copy(bf16[256,13,128]{2,1,0:T(8,128)(2,1)S(1)} %pad_bitcast_fusion) | data formatting | bytes 1703936 | tf_op jit(solution)/shard_map/transpose | solution.py:138
  16.3 1.4 %copy.28.colm_ref = bf16[256,1664]{1,0:T(8,128)(2,1)} copy(bf16[256,1664]{0,1:T(8,128)(2,1)S(1)} %bitcast.22) | data formatting | bytes 1703936 | tf_op jit(solution)/shard_map/reshape | solution.py:138
  17.8 0.3 copy.26
  18.1 1.1 %pad.19.rowm_ref = bf16[13,128,160]{2,1,0:T(8,128)(2,1)} pad(bf16[13,128,148]{2,1,0:T(8,128)(2,1)S(1)} %bitcast.21, bf16[]{:T(256)} %constant.13.clone.1), padding=0_0x0_0x0_12 | pad | bytes 1025026 | tf_op jit(solution)/shard_map/jit(_pad)/pad | solution.py:140
  19.2 0.7 %copy.27.kp_ref = f32[13,6]{1,0:T(8,128)} copy(f32[13,6]{0,1:T(8,128)S(1)} %copy-done.1) | data formatting | bytes 624 | tf_op args[4]
  20.0 0.2 convert_reduce_fusion.1
  20.3 1.5 %concatenate.14 = bf16[276,1152]{1,0:T(8,128)(2,1)S(1)} concatenate(bf16[10,1152]{1,0:T(8,128)(2,1)S(1)} %get-tuple-element.14, bf16[64,1152]{1,0:T(8,128)(2,1)S(1)} %get-tuple-element.8, bf16[64,1152]{1,0:T(8,128)(2,1)S(1)} %get-tuple-element.10, bf16[64,1152]{1,0:T(8,128)(2,1)S(1)} %get-tuple-element.9, bf16[64,1152]{1,0:T(8,128)(2,1)S(1)} %get-tuple-element.7, ...), dimensions={0} | concatenate | bytes 1271808 | tf_op jit(solution)/shard_map/concatenate | solution.py:116
  21.8 1.0 %gather_fusion = bf16[160,1152]{1,0:T(8,128)(2,1)S(1)} fusion(bf16[276,1152]{1,0:T(8,128)(2,1)S(1)} %concatenate.14, s32[1024]{0:T(1024)S(1)} %select_clamp_fusion), kind=kCustom, calls=%fused_computation | custom fusion | bytes 737920 | tf_op jit(solution)/shard_map/jit(_take)/gather | solution.py:133
  22.8 0.8 %broadcast_select_fusion.img_ref = bf16[160,1152]{1,0:T(8,128)(2,1)} fusion(bf16[160,1152]{1,0:T(8,128)(2,1)S(1)} %gather_fusion, pred[160]{0:T(512)(128)(4,1)S(1)} %compare_and_fusion), kind=kLoop, calls=%fused_computation.11 | loop fusion | flops 184320 | bytes 737440 | tf_op jit(solution)/shard_map/jit(_where)/select_n | solution.py:134
  23.6 8.8 %shard_map.109 = f32[1024,128]{1,0:T(8,128)} custom-call(f32[13,6]{1,0:T(8,128)} %copy.27.kp_ref, s32[2]{0:T(128)} %pad_add_fusion.pos_ref, bf16[160,1152]{1,0:T(8,128)(2,1)} %broadcast_select_fusion.img_ref, bf16[256,1664]{1,0:T(8,128)(2,1)} %copy.28.colm_ref, bf16[13,128,160]{2,1,0:T(8,128)(2,1)} %pad.19.rowm_ref, s32[1,128]{1,0:T(1,128)} %bitcast.24, ...), custom_call_target="tpu_custom_call" | custom-call | tf_op jit(solution)/shard_map/pallas_call | solution.py:202
  32.4 1.1 %convert_bitcast_fusion = bf16[128,8,128]{2,1,0:T(8,128)(2,1)S(1)} fusion(f32[1024,128]{1,0:T(8,128)} %shard_map.109), kind=kLoop, calls=%fused_computation.13 | loop fusion | flops 131072 | bytes 786432 | tf_op jit(solution)/shard_map/convert_element_type | solution.py:224
  33.4 33.6 %all_to_all.5 = bf16[128,8,128]{2,1,0:T(8,128)(2,1)S(1)} all-to-all(bf16[128,8,128]{2,1,0:T(8,128)(2,1)S(1)} %convert_bitcast_fusion), channel_id=1, replica_groups=mesh['section'=2,'ccd'=128] {'ccd'}, dimensions={0} | all-to-all | bytes 524288 | tf_op jit(solution)/shard_map/all_to_all | solution.py:225
  67.2 0.7 %reshape_broadcast_in_dim.3 = f32[1,1,32,32]{3,2,1,0:T(8,128)} reshape(f32[8,128]{1,0:T(8,128)S(1)} %convert_reduce_fusion) | data formatting | bytes 8192 | tf_op jit(solution)/shard_map/reshape;broadcast_in_dim | solution.py:227
  (39 shorter events, 1.2 us)
Async XLA Ops:
  2.2 11.1 %copy-start = (f32[13]{0:T(128)S(1)}, f32[13]{0:T(128)}, u32[]{:S(2)}) copy-start(f32[13]{0:T(128)} %constant.73) | copy-start | bytes 160
  2.2 11.1 %copy-start.2 = (pred[13]{0:T(512)(128)(4,1)S(1)}, pred[13]{0:T(512)(128)(4,1)}, u32[]{:S(2)}) copy-start(pred[13]{0:T(512)(128)(4,1)} %constant.71) | copy-start | bytes 43
  2.2 11.1 %copy-start.3 = (pred[13]{0:T(512)(128)(4,1)S(1)}, pred[13]{0:T(512)(128)(4,1)}, u32[]{:S(2)}) copy-start(pred[13]{0:T(512)(128)(4,1)} %constant.72) | copy-start | bytes 43
  2.2 11.1 %copy-start.4 = (pred[13]{0:T(512)(128)(4,1)S(1)}, pred[13]{0:T(512)(128)(4,1)}, u32[]{:S(2)}) copy-start(pred[13]{0:T(512)(128)(4,1)} %constant.69) | copy-start | bytes 43
  2.2 11.1 %copy-start.5 = (pred[13]{0:T(512)(128)(4,1)S(1)}, pred[13]{0:T(512)(128)(4,1)}, u32[]{:S(2)}) copy-start(pred[13]{0:T(512)(128)(4,1)} %constant.70) | copy-start | bytes 43
  2.5 17.4 %collective-permute-start.4 = (bf16[64,1152]{1,0:T(8,128)(2,1)S(1)}, bf16[64,1152]{1,0:T(8,128)(2,1)S(1)}, u32[]{:S(2)}, u32[]{:S(2)}) collective-permute-start(bf16[64,1152]{1,0:T(8,128)(2,1)S(1)} %concatenate.13), channel_id=1, source_target_pairs={{0,128},{1,129},{2,130},{3,131},{4,132},{5,133},{6,134},{7,135},{8... | collective-permute-start | bytes 442376 | tf_op jit(solution)/shard_map/ppermute | solution.py:110
  5.8 14.2 %collective-permute-start.2 = (bf16[64,1152]{1,0:T(8,128)(2,1)S(1)}, bf16[64,1152]{1,0:T(8,128)(2,1)S(1)}, u32[]{:S(2)}, u32[]{:S(2)}) collective-permute-start(bf16[64,1152]{1,0:T(8,128)(2,1)S(1)} %concatenate.13), channel_id=1, source_target_pairs={{128,1},{129,2},{130,3},{131,4},{132,5},{133,6},{134,7},{135,8},{1... | collective-permute-start | bytes 442376 | tf_op jit(solution)/shard_map/ppermute | solution.py:111
  7.8 12.1 %collective-permute-start.3 = (bf16[64,1152]{1,0:T(8,128)(2,1)S(1)}, bf16[64,1152]{1,0:T(8,128)(2,1)S(1)}, u32[]{:S(2)}, u32[]{:S(2)}) collective-permute-start(bf16[64,1152]{1,0:T(8,128)(2,1)S(1)} %concatenate.12), channel_id=1, source_target_pairs={{128,129},{129,130},{130,131},{131,132},{132,133},{133,134},{134,1... | collective-permute-start | bytes 442376 | tf_op jit(solution)/shard_map/ppermute | solution.py:112
  11.3 8.6 %collective-permute-start = (bf16[10,1152]{1,0:T(8,128)(2,1)S(1)}, bf16[10,1152]{1,0:T(8,128)(2,1)S(1)}, u32[]{:S(2)}, u32[]{:S(2)}) collective-permute-start(bf16[10,1152]{1,0:T(8,128)(2,1)S(1)} %slice_select_fusion.1), channel_id=1, source_target_pairs={{0,1},{1,2},{2,3},{3,4},{4,5},{5,6},{6,7},{7,8},{8,9},{9,10},{10,1... | collective-permute-start | bytes 69128 | tf_op jit(solution)/shard_map/ppermute | solution.py:113
  12.6 7.3 %collective-permute-start.1 = (bf16[10,1152]{1,0:T(8,128)(2,1)S(1)}, bf16[10,1152]{1,0:T(8,128)(2,1)S(1)}, u32[]{:S(2)}, u32[]{:S(2)}) collective-permute-start(bf16[10,1152]{1,0:T(8,128)(2,1)S(1)} %slice_select_fusion), channel_id=1, source_target_pairs={{0,129},{1,130},{2,131},{3,132},{4,133},{5,134},{6,135},{7,136},{8... | collective-permute-start | bytes 69128 | tf_op jit(solution)/shard_map/ppermute | solution.py:114
  18.1 1.1 %copy-start.1 = (f32[13,6]{0,1:T(8,128)S(1)}, f32[13,6]{0,1:T(8,128)}, u32[]{:S(2)}) copy-start(f32[13,6]{0,1:T(8,128)} %param.15) | copy-start | bytes 940

commit v7 on v6

--- a/solution.py
+++ b/solution.py
@@ -133,11 +133,11 @@
     warped = jnp.take(window, picks, axis=0, mode="clip")
     image = jnp.where(inside[:, None], warped, jnp.zeros((), warped.dtype))
     span = 2 * STRIP
-    col_band = band_matrix(basis_taps(column_power), STRIP)
-    col_band = jnp.pad(col_band, ((0, 0), (0, span - col_band.shape[1]), (0, 0)))
-    col_matrix = col_band.transpose(1, 0, 2).reshape(span, NBASIS * STRIP)
-    row_matrix = band_matrix(basis_taps(row_power), ROWS).transpose(0, 2, 1)
-    row_matrix = jnp.pad(row_matrix, ((0, 0), (0, 0), (0, lead_pad - lead)))
+    tap_lanes = lambda powers: jnp.pad(
+        basis_taps(powers).astype(jnp.float32), ((0, 0), (0, span - KW))
+    )
+    col_taps = tap_lanes(column_power)
+    row_taps = tap_lanes(row_power)
     positions = jnp.stack([top_row, left_col]).astype(jnp.int32)
     owners = tile_owner.reshape(1, -1)
     weights = tile_weight.reshape(1, -1)
@@ -146,12 +146,19 @@
     row_tiles = ROWS // TILE
     per_lane = STRIP // TILE
 
-    def match_kernel(kp_ref, pos_ref, img_ref, colm_ref, rowm_ref, own_ref, w_ref,
-                     out_ref, acc_ref, pack_ref, a_ref, b_ref):
+    def match_kernel(kp_ref, pos_ref, img_ref, ctap_ref, rtap_ref, own_ref, w_ref,
+                     out_ref, acc_ref, pack_ref, a_ref, b_ref, colm_ref, rowm_ref):
         i = pl.program_id(0)
 
         @pl.when(i == 0)
         def _():
+            for k in range(NBASIS):
+                spread = jnp.broadcast_to(ctap_ref[pl.ds(k, 1), :], (STRIP, span))
+                band_t = pltpu.roll(spread, 0, 1, stride=1, stride_axis=0)
+                colm_ref[:, k * STRIP : (k + 1) * STRIP] = band_t.T.astype(jnp.bfloat16)
+                spread = jnp.broadcast_to(rtap_ref[pl.ds(k, 1), :], (ROWS, span))
+                band = pltpu.roll(spread, 0, 1, stride=1, stride_axis=0)
+                rowm_ref[k] = band.astype(jnp.bfloat16)
             rows = lax.broadcasted_iota(jnp.int32, (ROWS, STRIP), 0) + pos_ref[0]
             u = 2.0 * (rows.astype(jnp.float32) + 0.5) / total_rows - 1.0
             for k in range(NBASIS):
@@ -167,7 +174,7 @@
         acc = jnp.zeros((ROWS, STRIP), jnp.float32)
         for k in range(NBASIS):
             vert = jnp.dot(
-                rowm_ref[k], across[:, k * STRIP : (k + 1) * STRIP],
+                rowm_ref[k, :, pl.ds(0, lead_pad)], across[:, k * STRIP : (k + 1) * STRIP],
                 preferred_element_type=jnp.float32,
             )
             coef = a_ref[k] + v * (b_ref[k] + kp_ref[k, 5] * v)
@@ -206,8 +213,8 @@
             pl.BlockSpec(memory_space=pltpu.SMEM),
             pl.BlockSpec(memory_space=pltpu.SMEM),
             full(image.shape),
-            full(col_matrix.shape),
-            full(row_matrix.shape),
+            full(col_taps.shape),
+            full(row_taps.shape),
             full(owners.shape),
             full(weights.shape),
         ],
@@ -218,8 +225,10 @@
             pltpu.VMEM((tiles * groups, STRIP), jnp.float32),
             pltpu.VMEM((NBASIS, ROWS, STRIP), jnp.float32),
             pltpu.VMEM((NBASIS, ROWS, STRIP), jnp.float32),
+            pltpu.VMEM((span, NBASIS * STRIP), jnp.bfloat16),
+            pltpu.VMEM((NBASIS, ROWS, span), jnp.bfloat16),
         ],
-    )(kernel_poly, positions, image, col_matrix, row_matrix, owners, weights)
+    )(kernel_poly, positions, image, col_taps, row_taps, owners, weights)
     outgoing = outgoing.reshape(band_count, groups, STRIP)
     outgoing = outgoing.astype(jnp.bfloat16)
     incoming = lax.all_to_all(outgoing, "ccd", split_axis=0, concat_axis=0, tiled=True)

time: 68.2 us -> 67.4 us (0.988)
  the two profiles are of different devices: /device:TPU:1 before, /device:TPU:32 now
where the time goes in v7:
time: 67.4 us; the launch traced here: 67 us
  blocking collectives  31.2 us (46%)
  starting transfers between devices  14.1 us (21%)
  Pallas kernels  9.08 us (13%)
  local copies, waits for them, and re-layouts  6.49 us (10%)
  other arithmetic  5.83 us (9%)
    all_to_all x1, blocking collectives, shards(): lax.all_to_all(outgoing, 'ccd', split_axis=0, concat_axis=0, tiled=True)  31.2 us
    pallas_call x1, Pallas kernels, shards(): pl.pallas_call(match_kernel, grid=(strips,), in_specs=[pl.BlockSpec(memor...  9.08 us
    ppermute x1, starting transfers between devices, shards(): got_edge_cross = lax.ppermute(edge(other), axes, cross_down)  4.39 us
    ppermute x1, starting transfers between devices, shards(): got_edge = lax.ppermute(edge(own), axes, straight_down)  3.92 us
    ppermute x1, starting transfers between devices, shards(): got_cross = lax.ppermute(other, axes, cross)  3.81 us
    unnamed x17, local copies, waits for them, and re-layouts  2.73 us
    ppermute x1, starting transfers between devices, shards(): got_straight = lax.ppermute(own, axes, straight)  1.92 us
    concatenate x1, local copies, waits for them, and re-layouts, shards(): jnp.concatenate([pick(got_edge, got_edge_cross), pick(got_cross, got_stra...  1.5 us
  transfers between devices with their start and end apart: 5, of which 0 were waited for; matrix products, arithmetic and copies ran while one was open for 4% of the time, Pallas kernels for 0%

profile of v7, /device:TPU:32, one launch (start us, length us, event | category | flops | bytes accessed | tf_op | source)
XLA Modules:
  0.0 67.0 jit_solution(9806440346888707269)
XLA Ops:
  0.0 0.7 copy-done.7
  0.7 0.1 copy.15
  0.9 0.7 copy-done.6
  1.5 1.3 %fusion = bf16[64,2048]{1,0:T(8,128)(2,1)S(1)} fusion(f32[1,1,64,2048]{3,2,1,0:T(8,128)} %param.13, f32[1,1,64,2048]{3,2,1,0:T(8,128)} %param.11, f32[64]{0:T(128)S(1)} %bitcast.11), kind=kLoop, calls=%fused_computation.4 | loop fusion | flops 393216 | bytes 1310976 | tf_op jit(solution)/shard_map/squeeze | solution.py:80
  2.8 0.2 pad_dynamic-slice_fusion
  3.2 3.8 %collective-permute-start.2 = (bf16[64,1152]{1,0:T(8,128)(2,1)S(1)}, bf16[64,1152]{1,0:T(8,128)(2,1)S(1)}, u32[]{:S(2)}, u32[]{:S(2)}) collective-permute-start(bf16[64,1152]{1,0:T(8,128)(2,1)S(1)} %concatenate.13), channel_id=1, source_target_pairs={{128,1},{129,2},{130,3},{131,4},{132,5},{133,6},{134,7},{135,8},{1... | collective-permute-start | bytes 442376 | tf_op jit(solution)/shard_map/ppermute | solution.py:111
  7.2 1.9 %collective-permute-start.3 = (bf16[64,1152]{1,0:T(8,128)(2,1)S(1)}, bf16[64,1152]{1,0:T(8,128)(2,1)S(1)}, u32[]{:S(2)}, u32[]{:S(2)}) collective-permute-start(bf16[64,1152]{1,0:T(8,128)(2,1)S(1)} %concatenate.12), channel_id=1, source_target_pairs={{128,129},{129,130},{130,131},{131,132},{132,133},{133,134},{134,1... | collective-permute-start | bytes 442376 | tf_op jit(solution)/shard_map/ppermute | solution.py:112
  9.1 3.9 %collective-permute-start = (bf16[10,1152]{1,0:T(8,128)(2,1)S(1)}, bf16[10,1152]{1,0:T(8,128)(2,1)S(1)}, u32[]{:S(2)}, u32[]{:S(2)}) collective-permute-start(bf16[10,1152]{1,0:T(8,128)(2,1)S(1)} %slice_select_fusion.1), channel_id=1, source_target_pairs={{0,1},{1,2},{2,3},{3,4},{4,5},{5,6},{6,7},{7,8},{8,9},{9,10},{10,1... | collective-permute-start | bytes 69128 | tf_op jit(solution)/shard_map/ppermute | solution.py:113
  13.1 4.4 %collective-permute-start.1 = (bf16[10,1152]{1,0:T(8,128)(2,1)S(1)}, bf16[10,1152]{1,0:T(8,128)(2,1)S(1)}, u32[]{:S(2)}, u32[]{:S(2)}) collective-permute-start(bf16[10,1152]{1,0:T(8,128)(2,1)S(1)} %slice_select_fusion), channel_id=1, source_target_pairs={{0,129},{1,130},{2,131},{3,132},{4,133},{5,134},{6,135},{7,136},{8... | collective-permute-start | bytes 69128 | tf_op jit(solution)/shard_map/ppermute | solution.py:114
  17.6 0.6 copy-done.1
  18.2 0.2 multiply_reduce_fusion
  18.5 0.6 pad_convert_fusion.rtap_ref
  19.1 0.6 pad_convert_fusion.1.ctap_ref
  19.8 0.6 pad_add_fusion.pos_ref
  20.4 0.7 %copy.17.kp_ref = f32[13,6]{1,0:T(8,128)} copy(f32[13,6]{0,1:T(8,128)S(1)} %copy-done) | data formatting | bytes 624 | tf_op args[4]
  21.3 0.2 convert_reduce_fusion.1
  21.5 1.5 %concatenate.14 = bf16[276,1152]{1,0:T(8,128)(2,1)S(1)} concatenate(bf16[10,1152]{1,0:T(8,128)(2,1)S(1)} %get-tuple-element.14, bf16[64,1152]{1,0:T(8,128)(2,1)S(1)} %get-tuple-element.8, bf16[64,1152]{1,0:T(8,128)(2,1)S(1)} %get-tuple-element.10, bf16[64,1152]{1,0:T(8,128)(2,1)S(1)} %get-tuple-element.9, bf16[64,1152]{1,0:T(8,128)(2,1)S(1)} %get-tuple-element.7, ...), dimensions={0} | concatenate | bytes 1271808 | tf_op jit(solution)/shard_map/concatenate | solution.py:116
  23.0 1.0 %gather_fusion = bf16[160,1152]{1,0:T(8,128)(2,1)S(1)} fusion(bf16[276,1152]{1,0:T(8,128)(2,1)S(1)} %concatenate.14, s32[1024]{0:T(1024)S(1)} %select_clamp_fusion), kind=kCustom, calls=%fused_computation | custom fusion | bytes 737920 | tf_op jit(solution)/shard_map/jit(_take)/gather | solution.py:133
  24.0 0.9 %broadcast_select_fusion.img_ref = bf16[160,1152]{1,0:T(8,128)(2,1)} fusion(bf16[160,1152]{1,0:T(8,128)(2,1)S(1)} %gather_fusion, pred[160]{0:T(512)(128)(4,1)S(1)} %compare_and_fusion), kind=kLoop, calls=%fused_computation.3 | loop fusion | flops 184320 | bytes 737440 | tf_op jit(solution)/shard_map/jit(_where)/select_n | solution.py:134
  24.9 9.1 %shard_map.109 = f32[1024,128]{1,0:T(8,128)} custom-call(f32[13,6]{1,0:T(8,128)} %copy.17.kp_ref, s32[2]{0:T(128)} %pad_add_fusion.pos_ref, bf16[160,1152]{1,0:T(8,128)(2,1)} %broadcast_select_fusion.img_ref, f32[13,256]{1,0:T(8,128)} %pad_convert_fusion.1.ctap_ref, f32[13,256]{1,0:T(8,128)} %pad_convert_fusion.rtap_ref, s32[1,128]{1,0:T(1,128)} %bitcast.12, ...), custom_call_target="tpu_custom_call" | custom-call | tf_op jit(solution)/shard_map/pallas_call | solution.py:209
  33.9 1.1 %convert_bitcast_fusion = bf16[128,8,128]{2,1,0:T(8,128)(2,1)S(1)} fusion(f32[1024,128]{1,0:T(8,128)} %shard_map.109), kind=kLoop, calls=%fused_computation.5 | loop fusion | flops 131072 | bytes 786432 | tf_op jit(solution)/shard_map/convert_element_type | solution.py:233
  35.0 31.2 %all_to_all.5 = bf16[128,8,128]{2,1,0:T(8,128)(2,1)S(1)} all-to-all(bf16[128,8,128]{2,1,0:T(8,128)(2,1)S(1)} %convert_bitcast_fusion), channel_id=1, replica_groups=mesh['section'=2,'ccd'=128] {'ccd'}, dimensions={0} | all-to-all | bytes 524288 | tf_op jit(solution)/shard_map/all_to_all | solution.py:234
  66.2 0.1 convert_reduce_fusion
  66.3 0.7 %reshape_broadcast_in_dim.3 = f32[1,1,32,32]{3,2,1,0:T(8,128)} reshape(f32[8,128]{1,0:T(8,128)S(1)} %convert_reduce_fusion) | data formatting | bytes 8192 | tf_op jit(solution)/shard_map/reshape;broadcast_in_dim | solution.py:236
  (37 shorter events, 0.8 us)
Async XLA Ops:
  0.0 0.7 copy-start.7
  0.9 0.7 copy-start.6
  3.1 18.0 %collective-permute-start.4 = (bf16[64,1152]{1,0:T(8,128)(2,1)S(1)}, bf16[64,1152]{1,0:T(8,128)(2,1)S(1)}, u32[]{:S(2)}, u32[]{:S(2)}) collective-permute-start(bf16[64,1152]{1,0:T(8,128)(2,1)S(1)} %concatenate.13), channel_id=1, source_target_pairs={{0,128},{1,129},{2,130},{3,131},{4,132},{5,133},{6,134},{7,135},{8... | collective-permute-start | bytes 442376 | tf_op jit(solution)/shard_map/ppermute | solution.py:110
  3.2 18.0 %collective-permute-start.2 = (bf16[64,1152]{1,0:T(8,128)(2,1)S(1)}, bf16[64,1152]{1,0:T(8,128)(2,1)S(1)}, u32[]{:S(2)}, u32[]{:S(2)}) collective-permute-start(bf16[64,1152]{1,0:T(8,128)(2,1)S(1)} %concatenate.13), channel_id=1, source_target_pairs={{128,1},{129,2},{130,3},{131,4},{132,5},{133,6},{134,7},{135,8},{1... | collective-permute-start | bytes 442376 | tf_op jit(solution)/shard_map/ppermute | solution.py:111
  7.2 14.0 %collective-permute-start.3 = (bf16[64,1152]{1,0:T(8,128)(2,1)S(1)}, bf16[64,1152]{1,0:T(8,128)(2,1)S(1)}, u32[]{:S(2)}, u32[]{:S(2)}) collective-permute-start(bf16[64,1152]{1,0:T(8,128)(2,1)S(1)} %concatenate.12), channel_id=1, source_target_pairs={{128,129},{129,130},{130,131},{131,132},{132,133},{133,134},{134,1... | collective-permute-start | bytes 442376 | tf_op jit(solution)/shard_map/ppermute | solution.py:112
  9.1 12.0 %collective-permute-start = (bf16[10,1152]{1,0:T(8,128)(2,1)S(1)}, bf16[10,1152]{1,0:T(8,128)(2,1)S(1)}, u32[]{:S(2)}, u32[]{:S(2)}) collective-permute-start(bf16[10,1152]{1,0:T(8,128)(2,1)S(1)} %slice_select_fusion.1), channel_id=1, source_target_pairs={{0,1},{1,2},{2,3},{3,4},{4,5},{5,6},{6,7},{7,8},{8,9},{9,10},{10,1... | collective-permute-start | bytes 69128 | tf_op jit(solution)/shard_map/ppermute | solution.py:113
  13.0 4.5 %copy-start.4 = (pred[13]{0:T(512)(128)(4,1)S(1)}, pred[13]{0:T(512)(128)(4,1)}, u32[]{:S(2)}) copy-start(pred[13]{0:T(512)(128)(4,1)} %constant.74) | copy-start | bytes 43
  13.1 4.5 %copy-start.5 = (f32[13]{0:T(128)S(1)}, f32[13]{0:T(128)}, u32[]{:S(2)}) copy-start(f32[13]{0:T(128)} %constant.75) | copy-start | bytes 160
  13.1 8.0 %collective-permute-start.1 = (bf16[10,1152]{1,0:T(8,128)(2,1)S(1)}, bf16[10,1152]{1,0:T(8,128)(2,1)S(1)}, u32[]{:S(2)}, u32[]{:S(2)}) collective-permute-start(bf16[10,1152]{1,0:T(8,128)(2,1)S(1)} %slice_select_fusion), channel_id=1, source_target_pairs={{0,129},{1,130},{2,131},{3,132},{4,133},{5,134},{6,135},{7,136},{8... | collective-permute-start | bytes 69128 | tf_op jit(solution)/shard_map/ppermute | solution.py:114
  17.5 0.7 copy-start.1
  17.5 0.7 copy-start.2
  17.6 0.7 copy-start.3
  19.8 0.7 %copy-start = (f32[13,6]{0,1:T(8,128)S(1)}, f32[13,6]{0,1:T(8,128)}, u32[]{:S(2)}) copy-start(f32[13,6]{0,1:T(8,128)} %param.15) | copy-start | bytes 940

commit v8 on v7

--- a/solution.py
+++ b/solution.py
@@ -34,9 +34,9 @@
     return array
 
 
-def basis_taps(powers):
+def basis_taps(powers, sigmas=basis_sigma):
     offsets = jnp.arange(KW).astype(jnp.float32) - HALF_K
-    sigma_col = jnp.array(basis_sigma, dtype=jnp.float32)[:, None]
+    sigma_col = jnp.array(sigmas, dtype=jnp.float32)[:, None]
     power_col = jnp.array(powers, dtype=jnp.int32)[:, None]
     spread = offsets[None, :]
     envelope = jnp.exp(-(spread * spread) / (2.0 * sigma_col * sigma_col))
@@ -133,12 +133,12 @@
     warped = jnp.take(window, picks, axis=0, mode="clip")
     image = jnp.where(inside[:, None], warped, jnp.zeros((), warped.dtype))
     span = 2 * STRIP
-    tap_lanes = lambda powers: jnp.pad(
-        basis_taps(powers).astype(jnp.float32), ((0, 0), (0, span - KW))
-    )
-    col_taps = tap_lanes(column_power)
-    row_taps = tap_lanes(row_power)
-    positions = jnp.stack([top_row, left_col]).astype(jnp.int32)
+    both_taps = basis_taps(column_power + row_power, basis_sigma + basis_sigma)
+    taps = jnp.pad(both_taps.astype(jnp.float32), ((0, 0), (0, span - KW)))
+    params = jnp.concatenate(
+        [kernel_poly.reshape(-1), jnp.stack([top_row, left_col]).astype(jnp.float32)]
+    )
+    at = NBASIS * NPOLY
     owners = tile_owner.reshape(1, -1)
     weights = tile_weight.reshape(1, -1)
     groups = TILE * TILE // STRIP
@@ -146,38 +146,39 @@
     row_tiles = ROWS // TILE
     per_lane = STRIP // TILE
 
-    def match_kernel(kp_ref, pos_ref, img_ref, ctap_ref, rtap_ref, own_ref, w_ref,
+    def match_kernel(kp_ref, img_ref, tap_ref, own_ref, w_ref,
                      out_ref, acc_ref, pack_ref, a_ref, b_ref, colm_ref, rowm_ref):
         i = pl.program_id(0)
 
         @pl.when(i == 0)
         def _():
             for k in range(NBASIS):
-                spread = jnp.broadcast_to(ctap_ref[pl.ds(k, 1), :], (STRIP, span))
+                spread = jnp.broadcast_to(tap_ref[pl.ds(k, 1), :], (STRIP, span))
                 band_t = pltpu.roll(spread, 0, 1, stride=1, stride_axis=0)
                 colm_ref[:, k * STRIP : (k + 1) * STRIP] = band_t.T.astype(jnp.bfloat16)
-                spread = jnp.broadcast_to(rtap_ref[pl.ds(k, 1), :], (ROWS, span))
+                spread = jnp.broadcast_to(tap_ref[pl.ds(NBASIS + k, 1), :], (ROWS, span))
                 band = pltpu.roll(spread, 0, 1, stride=1, stride_axis=0)
                 rowm_ref[k] = band.astype(jnp.bfloat16)
-            rows = lax.broadcasted_iota(jnp.int32, (ROWS, STRIP), 0) + pos_ref[0]
-            u = 2.0 * (rows.astype(jnp.float32) + 0.5) / total_rows - 1.0
+            rows = lax.broadcasted_iota(jnp.int32, (ROWS, STRIP), 0).astype(jnp.float32)
+            u = 2.0 * (rows + kp_ref[at] + 0.5) / total_rows - 1.0
             for k in range(NBASIS):
-                a_ref[k] = kp_ref[k, 0] + kp_ref[k, 1] * u + kp_ref[k, 3] * u * u
-                b_ref[k] = kp_ref[k, 2] + kp_ref[k, 4] * u
+                p = lambda m: kp_ref[k * NPOLY + m]
+                a_ref[k] = p(0) + p(1) * u + p(3) * u * u
+                b_ref[k] = p(2) + p(4) * u
 
         offset = pl.multiple_of(i * STRIP, STRIP)
         strip = img_ref[:, pl.ds(offset, span)]
         across = jnp.dot(strip, colm_ref[...], preferred_element_type=jnp.float32)
         across = across.astype(jnp.bfloat16)
-        cols = lax.broadcasted_iota(jnp.int32, (1, STRIP), 1) + (pos_ref[1] + i * STRIP)
-        v = 2.0 * (cols.astype(jnp.float32) + 0.5) / total_cols - 1.0
+        cols = lax.broadcasted_iota(jnp.int32, (1, STRIP), 1) + i * STRIP
+        v = 2.0 * (cols.astype(jnp.float32) + kp_ref[at + 1] + 0.5) / total_cols - 1.0
         acc = jnp.zeros((ROWS, STRIP), jnp.float32)
         for k in range(NBASIS):
             vert = jnp.dot(
                 rowm_ref[k, :, pl.ds(0, lead_pad)], across[:, k * STRIP : (k + 1) * STRIP],
                 preferred_element_type=jnp.float32,
             )
-            coef = a_ref[k] + v * (b_ref[k] + kp_ref[k, 5] * v)
+            coef = a_ref[k] + v * (b_ref[k] + kp_ref[k * NPOLY + 5] * v)
             acc = acc + coef * vert
         acc_ref[...] = acc
         lane_group = lax.broadcasted_iota(jnp.int32, (groups, STRIP), 1) // TILE
@@ -211,10 +212,8 @@
         grid=(strips,),
         in_specs=[
             pl.BlockSpec(memory_space=pltpu.SMEM),
-            pl.BlockSpec(memory_space=pltpu.SMEM),
             full(image.shape),
-            full(col_taps.shape),
-            full(row_taps.shape),
+            full(taps.shape),
             full(owners.shape),
             full(weights.shape),
         ],
@@ -228,9 +227,8 @@
             pltpu.VMEM((span, NBASIS * STRIP), jnp.bfloat16),
             pltpu.VMEM((NBASIS, ROWS, span), jnp.bfloat16),
         ],
-    )(kernel_poly, positions, image, col_taps, row_taps, owners, weights)
-    outgoing = outgoing.reshape(band_count, groups, STRIP)
-    outgoing = outgoing.astype(jnp.bfloat16)
+    )(params, image, taps, owners, weights)
+    outgoing = outgoing.reshape(band_count, groups, STRIP).astype(jnp.bfloat16)
     incoming = lax.all_to_all(outgoing, "ccd", split_axis=0, concat_axis=0, tiled=True)
     patch_sum = jnp.sum(incoming.astype(jnp.float32), axis=0, keepdims=True)
     return patch_sum.reshape(1, 1, TILE, TILE)

time: 67.4 us -> 67.4 us (level)
  the two profiles are of different devices: /device:TPU:32 before, /device:TPU:1 now
where the time goes in v8:
time: 67.4 us; the launch traced here: 66.9 us
  blocking collectives  33.3 us (49%)
  starting transfers between devices  12 us (18%)
  Pallas kernels  9.01 us (13%)
  local copies, waits for them, and re-layouts  5.92 us (9%)
  other arithmetic  5.28 us (8%)
  waiting for transfers between devices  1.2 us (2%)
    all_to_all x1, blocking collectives, shards(): lax.all_to_all(outgoing, 'ccd', split_axis=0, concat_axis=0, tiled=True)  33.3 us
    pallas_call x1, Pallas kernels, shards(): pl.pallas_call(match_kernel, grid=(strips,), in_specs=[pl.BlockSpec(memor...  9.01 us
    ppermute x1, starting transfers between devices, shards(): got_straight = lax.ppermute(own, axes, straight)  4.99 us
    ppermute x1, starting transfers between devices, shards(): got_cross = lax.ppermute(other, axes, cross)  4.92 us
    unnamed x13, local copies, waits for them, and re-layouts  2.08 us
    concatenate x1, local copies, waits for them, and re-layouts, shards(): jnp.concatenate([pick(got_edge, got_edge_cross), pick(got_cross, got_stra...  1.5 us
  transfers between devices with their start and end apart: 5, of which 1 were waited for; matrix products, arithmetic and copies ran while one was open for 3% of the time, Pallas kernels for 0%

profile of v8, /device:TPU:1, one launch (start us, length us, event | category | flops | bytes accessed | tf_op | source)
XLA Modules:
  0.0 66.9 jit_solution(1694262060474752876)
XLA Ops:
  0.0 0.7 copy-done.5
  0.7 0.1 copy.14
  0.9 0.7 copy-done.4
  1.5 1.3 %fusion = bf16[64,2048]{1,0:T(8,128)(2,1)S(1)} fusion(f32[1,1,64,2048]{3,2,1,0:T(8,128)} %param.11, f32[1,1,64,2048]{3,2,1,0:T(8,128)} %param.9, f32[64]{0:T(128)S(1)} %bitcast.11), kind=kLoop, calls=%fused_computation.4 | loop fusion | flops 393216 | bytes 1310976 | tf_op jit(solution)/shard_map/squeeze | solution.py:80
  2.8 0.2 pad_dynamic-slice_fusion
  3.0 0.1 concatenate.17
  3.1 4.9 %collective-permute-start.2 = (bf16[64,1152]{1,0:T(8,128)(2,1)S(1)}, bf16[64,1152]{1,0:T(8,128)(2,1)S(1)}, u32[]{:S(2)}, u32[]{:S(2)}) collective-permute-start(bf16[64,1152]{1,0:T(8,128)(2,1)S(1)} %concatenate.17), channel_id=1, source_target_pairs={{128,1},{129,2},{130,3},{131,4},{132,5},{133,6},{134,7},{135,8},{1... | collective-permute-start | bytes 442376 | tf_op jit(solution)/shard_map/ppermute | solution.py:111
  8.2 0.7 collective-permute-start.1
  9.0 5.0 %collective-permute-start.3 = (bf16[64,1152]{1,0:T(8,128)(2,1)S(1)}, bf16[64,1152]{1,0:T(8,128)(2,1)S(1)}, u32[]{:S(2)}, u32[]{:S(2)}) collective-permute-start(bf16[64,1152]{1,0:T(8,128)(2,1)S(1)} %concatenate.16), channel_id=1, source_target_pairs={{128,129},{129,130},{130,131},{131,132},{132,133},{133,134},{134,1... | collective-permute-start | bytes 442376 | tf_op jit(solution)/shard_map/ppermute | solution.py:112
  14.0 1.3 %collective-permute-start = (bf16[10,1152]{1,0:T(8,128)(2,1)S(1)}, bf16[10,1152]{1,0:T(8,128)(2,1)S(1)}, u32[]{:S(2)}, u32[]{:S(2)}) collective-permute-start(bf16[10,1152]{1,0:T(8,128)(2,1)S(1)} %slice_select_fusion.1), channel_id=1, source_target_pairs={{0,1},{1,2},{2,3},{3,4},{4,5},{5,6},{6,7},{7,8},{8,9},{9,10},{10,1... | collective-permute-start | bytes 69128 | tf_op jit(solution)/shard_map/ppermute | solution.py:113
  15.6 0.6 copy-done.1
  16.2 0.2 multiply_reduce_fusion
  16.5 0.6 pad_convert_fusion.tap_ref
  17.2 0.6 pad_maximum_fusion.3.kp_ref
  17.8 1.2 %collective-permute-done = bf16[10,1152]{1,0:T(8,128)(2,1)S(1)} collective-permute-done((bf16[10,1152]{1,0:T(8,128)(2,1)S(1)}, bf16[10,1152]{1,0:T(8,128)(2,1)S(1)}, u32[]{:S(2)}, u32[]{:S(2)}) %collective-permute-start) | collective-permute-done | bytes 23072 | tf_op jit(solution)/shard_map/ppermute | solution.py:113
  19.1 0.2 convert_reduce_fusion.1
  19.3 1.5 %concatenate.18 = bf16[276,1152]{1,0:T(8,128)(2,1)S(1)} concatenate(bf16[10,1152]{1,0:T(8,128)(2,1)S(1)} %get-tuple-element.12, bf16[64,1152]{1,0:T(8,128)(2,1)S(1)} %get-tuple-element.6, bf16[64,1152]{1,0:T(8,128)(2,1)S(1)} %get-tuple-element.8, bf16[64,1152]{1,0:T(8,128)(2,1)S(1)} %get-tuple-element.7, bf16[64,1152]{1,0:T(8,128)(2,1)S(1)} %get-tuple-element.5, ...), dimensions={0} | concatenate | bytes 1271808 | tf_op jit(solution)/shard_map/concatenate | solution.py:116
  20.8 1.0 %gather_fusion = bf16[160,1152]{1,0:T(8,128)(2,1)S(1)} fusion(bf16[276,1152]{1,0:T(8,128)(2,1)S(1)} %concatenate.18, s32[1024]{0:T(1024)S(1)} %select_clamp_fusion), kind=kCustom, calls=%fused_computation | custom fusion | bytes 737920 | tf_op jit(solution)/shard_map/jit(_take)/gather | solution.py:133
  21.8 0.9 %broadcast_select_fusion.img_ref = bf16[160,1152]{1,0:T(8,128)(2,1)} fusion(bf16[160,1152]{1,0:T(8,128)(2,1)S(1)} %gather_fusion, pred[160]{0:T(512)(128)(4,1)S(1)} %compare_and_fusion), kind=kLoop, calls=%fused_computation.3 | loop fusion | flops 184320 | bytes 737440 | tf_op jit(solution)/shard_map/jit(_where)/select_n | solution.py:134
  22.7 9.0 %shard_map.91 = f32[1024,128]{1,0:T(8,128)} custom-call(f32[80]{0:T(128)} %pad_maximum_fusion.3.kp_ref, bf16[160,1152]{1,0:T(8,128)(2,1)} %broadcast_select_fusion.img_ref, f32[26,256]{1,0:T(8,128)} %pad_convert_fusion.tap_ref, s32[1,128]{1,0:T(1,128)} %bitcast.12, f32[1,128]{1,0:T(1,128)} %bitcast.13), custom_call_target="tpu_custom_call" | custom-call | tf_op jit(solution)/shard_map/pallas_call | solution.py:210
  31.7 1.1 %convert_bitcast_fusion = bf16[128,8,128]{2,1,0:T(8,128)(2,1)S(1)} fusion(f32[1024,128]{1,0:T(8,128)} %shard_map.91), kind=kLoop, calls=%fused_computation.5 | loop fusion | flops 131072 | bytes 786432 | tf_op jit(solution)/shard_map/convert_element_type | solution.py:231
  32.8 33.3 %all_to_all.5 = bf16[128,8,128]{2,1,0:T(8,128)(2,1)S(1)} all-to-all(bf16[128,8,128]{2,1,0:T(8,128)(2,1)S(1)} %convert_bitcast_fusion), channel_id=1, replica_groups=mesh['section'=2,'ccd'=128] {'ccd'}, dimensions={0} | all-to-all | bytes 524288 | tf_op jit(solution)/shard_map/all_to_all | solution.py:232
  66.1 0.1 convert_reduce_fusion
  66.3 0.7 %reshape_broadcast_in_dim.3 = f32[1,1,32,32]{3,2,1,0:T(8,128)} reshape(f32[8,128]{1,0:T(8,128)S(1)} %convert_reduce_fusion) | data formatting | bytes 8192 | tf_op jit(solution)/shard_map/reshape;broadcast_in_dim | solution.py:234
  (33 shorter events, 0.9 us)
Async XLA Ops:
  0.0 0.7 copy-start.5
  0.9 0.7 copy-start.4
  3.1 15.9 %collective-permute-start.2 = (bf16[64,1152]{1,0:T(8,128)(2,1)S(1)}, bf16[64,1152]{1,0:T(8,128)(2,1)S(1)}, u32[]{:S(2)}, u32[]{:S(2)}) collective-permute-start(bf16[64,1152]{1,0:T(8,128)(2,1)S(1)} %concatenate.17), channel_id=1, source_target_pairs={{128,1},{129,2},{130,3},{131,4},{132,5},{133,6},{134,7},{135,8},{1... | collective-permute-start | bytes 442376 | tf_op jit(solution)/shard_map/ppermute | solution.py:111
  8.1 10.9 %collective-permute-start.4 = (bf16[64,1152]{1,0:T(8,128)(2,1)S(1)}, bf16[64,1152]{1,0:T(8,128)(2,1)S(1)}, u32[]{:S(2)}, u32[]{:S(2)}) collective-permute-start(bf16[64,1152]{1,0:T(8,128)(2,1)S(1)} %concatenate.17), channel_id=1, source_target_pairs={{0,128},{1,129},{2,130},{3,131},{4,132},{5,133},{6,134},{7,135},{8... | collective-permute-start | bytes 442376 | tf_op jit(solution)/shard_map/ppermute | solution.py:110
  8.2 9.6 %collective-permute-start.1 = (bf16[10,1152]{1,0:T(8,128)(2,1)S(1)}, bf16[10,1152]{1,0:T(8,128)(2,1)S(1)}, u32[]{:S(2)}, u32[]{:S(2)}) collective-permute-start(bf16[10,1152]{1,0:T(8,128)(2,1)S(1)} %slice_select_fusion), channel_id=1, source_target_pairs={{0,129},{1,130},{2,131},{3,132},{4,133},{5,134},{6,135},{7,136},{8... | collective-permute-start | bytes 69128 | tf_op jit(solution)/shard_map/ppermute | solution.py:114
  9.0 10.1 %collective-permute-start.3 = (bf16[64,1152]{1,0:T(8,128)(2,1)S(1)}, bf16[64,1152]{1,0:T(8,128)(2,1)S(1)}, u32[]{:S(2)}, u32[]{:S(2)}) collective-permute-start(bf16[64,1152]{1,0:T(8,128)(2,1)S(1)} %concatenate.16), channel_id=1, source_target_pairs={{128,129},{129,130},{130,131},{131,132},{132,133},{133,134},{134,1... | collective-permute-start | bytes 442376 | tf_op jit(solution)/shard_map/ppermute | solution.py:112
  14.0 1.4 %copy-start = (f32[13,6]{0,1:T(8,128)S(1)}, f32[13,6]{0,1:T(8,128)}, u32[]{:S(2)}) copy-start(f32[13,6]{0,1:T(8,128)} %param.13) | copy-start | bytes 940
  14.0 5.0 %collective-permute-start = (bf16[10,1152]{1,0:T(8,128)(2,1)S(1)}, bf16[10,1152]{1,0:T(8,128)(2,1)S(1)}, u32[]{:S(2)}, u32[]{:S(2)}) collective-permute-start(bf16[10,1152]{1,0:T(8,128)(2,1)S(1)} %slice_select_fusion.1), channel_id=1, source_target_pairs={{0,1},{1,2},{2,3},{3,4},{4,5},{5,6},{6,7},{7,8},{8,9},{9,10},{10,1... | collective-permute-start | bytes 69128 | tf_op jit(solution)/shard_map/ppermute | solution.py:113
  15.5 0.7 copy-start.1
  15.6 0.7 copy-start.2
  15.6 0.7 copy-start.3

commit v9 on v8

--- a/solution.py
+++ b/solution.py
@@ -82,11 +82,10 @@
     my_shifts = lax.dynamic_slice_in_dim(shifts, half * rh, rh)[:, None]
     wide = jnp.pad(calibrated, ((0, 0), (HALF_K, HALF_K)))
     width = CH + 2 * HALF_K
-    filler = jnp.zeros((rh, wide_cols - width - 1), jnp.bfloat16)
 
     def slab(col_start):
         cols = lax.dynamic_slice_in_dim(wide, col_start, width, 1)
-        return jnp.concatenate([cols, my_shifts, filler], axis=1)
+        return jnp.concatenate([cols, my_shifts], axis=1)
 
     own = slab(half * CH)
     other = slab((1 - half) * CH)
@@ -124,6 +123,7 @@
         ],
         axis=0,
     )
+    window = jnp.pad(window, ((0, 0), (0, wide_cols - width - 1)))
     lead = ROWS + 2 * HALF_K
     lead_pad = -(-lead // 16) * 16
     steps = window[REACH : REACH + lead, width].astype(jnp.int32)

time: 67.4 us -> 70.5 us (1.046)
  the two profiles are of different devices: /device:TPU:1 before, /device:TPU:32 now
where the time goes in v9:
time: 70.5 us; the launch traced here: 70.2 us
  blocking collectives  30.2 us (43%)
  starting transfers between devices  14.5 us (21%)
  Pallas kernels  9 us (13%)
  local copies, waits for them, and re-layouts  5.71 us (8%)
  other arithmetic  5.5 us (8%)
  waiting for transfers between devices  5.08 us (7%)
    all_to_all x1, blocking collectives, shards(): lax.all_to_all(outgoing, 'ccd', split_axis=0, concat_axis=0, tiled=True)  30.2 us
    pallas_call x1, Pallas kernels, shards(): pl.pallas_call(match_kernel, grid=(strips,), in_specs=[pl.BlockSpec(memor...  9 us
    ppermute x1, waiting for transfers between devices, shards(): got_straight = lax.ppermute(own, axes, straight)  5.07 us
    ppermute x1, starting transfers between devices, shards(): got_edge = lax.ppermute(edge(own), axes, straight_down)  5.04 us
    ppermute x1, starting transfers between devices, shards(): got_cross = lax.ppermute(other, axes, cross)  3.81 us
    ppermute x1, starting transfers between devices, shards(): got_edge_cross = lax.ppermute(edge(other), axes, cross_down)  3.68 us
    unnamed x13, local copies, waits for them, and re-layouts  2.08 us
    ppermute x1, starting transfers between devices, shards(): got_straight = lax.ppermute(own, axes, straight)  1.91 us
  transfers between devices with their start and end apart: 5, of which 1 were waited for; matrix products, arithmetic and copies ran while one was open for 3% of the time, Pallas kernels for 0%

profile of v9, /device:TPU:32, one launch (start us, length us, event | category | flops | bytes accessed | tf_op | source)
XLA Modules:
  0.0 70.2 jit_solution(4784316110439741019)
XLA Ops:
  0.0 0.7 copy-done.5
  0.7 0.1 copy.14
  0.9 0.7 copy-done.4
  1.5 1.3 %fusion = bf16[64,2048]{1,0:T(8,128)(2,1)S(1)} fusion(f32[1,1,64,2048]{3,2,1,0:T(8,128)} %param.11, f32[1,1,64,2048]{3,2,1,0:T(8,128)} %param.9, f32[64]{0:T(128)S(1)} %bitcast.11), kind=kLoop, calls=%fused_computation.8 | loop fusion | flops 393216 | bytes 1310976 | tf_op jit(solution)/shard_map/squeeze | solution.py:80
  2.8 0.2 pad_dynamic-slice_fusion
  3.1 3.8 %collective-permute-start.2 = (bf16[64,1045]{1,0:T(8,128)(2,1)S(1)}, bf16[64,1045]{1,0:T(8,128)(2,1)S(1)}, u32[]{:S(2)}, u32[]{:S(2)}) collective-permute-start(bf16[64,1045]{1,0:T(8,128)(2,1)S(1)} %pad_maximum_fusion), channel_id=1, source_target_pairs={{128,1},{129,2},{130,3},{131,4},{132,5},{133,6},{134,7},{135,8},{1... | collective-permute-start | bytes 401288 | tf_op jit(solution)/shard_map/ppermute | solution.py:110
  7.0 3.7 %collective-permute-start.1 = (bf16[10,1045]{1,0:T(8,128)(2,1)S(1)}, bf16[10,1045]{1,0:T(8,128)(2,1)S(1)}, u32[]{:S(2)}, u32[]{:S(2)}) collective-permute-start(bf16[10,1045]{1,0:T(8,128)(2,1)S(1)} %get-tuple-element.13), channel_id=1, source_target_pairs={{0,129},{1,130},{2,131},{3,132},{4,133},{5,134},{6,135},{7,136},{8... | collective-permute-start | bytes 62708 | tf_op jit(solution)/shard_map/ppermute | solution.py:113
  10.7 5.0 %collective-permute-start = (bf16[10,1045]{1,0:T(8,128)(2,1)S(1)}, bf16[10,1045]{1,0:T(8,128)(2,1)S(1)}, u32[]{:S(2)}, u32[]{:S(2)}) collective-permute-start(bf16[10,1045]{1,0:T(8,128)(2,1)S(1)} %get-tuple-element.14), channel_id=1, source_target_pairs={{0,1},{1,2},{2,3},{3,4},{4,5},{5,6},{6,7},{7,8},{8,9},{9,10},{10,1... | collective-permute-start | bytes 62708 | tf_op jit(solution)/shard_map/ppermute | solution.py:112
  16.0 0.6 copy-done.1
  16.7 0.2 multiply_reduce_fusion
  16.9 0.1 divide_convert_fusion
  17.0 0.6 pad_convert_fusion.tap_ref
  17.7 0.6 pad_maximum_fusion.5.kp_ref
  18.4 1.9 %collective-permute-start.3 = (bf16[64,1045]{1,0:T(8,128)(2,1)S(1)}, bf16[64,1045]{1,0:T(8,128)(2,1)S(1)}, u32[]{:S(2)}, u32[]{:S(2)}) collective-permute-start(bf16[64,1045]{1,0:T(8,128)(2,1)S(1)} %get-tuple-element.6), channel_id=1, source_target_pairs={{128,129},{129,130},{130,131},{131,132},{132,133},{133,134},{134,1... | collective-permute-start | bytes 401288 | tf_op jit(solution)/shard_map/ppermute | solution.py:111
  20.4 5.1 %collective-permute-done.3 = bf16[64,1045]{1,0:T(8,128)(2,1)S(1)} collective-permute-done((bf16[64,1045]{1,0:T(8,128)(2,1)S(1)}, bf16[64,1045]{1,0:T(8,128)(2,1)S(1)}, u32[]{:S(2)}, u32[]{:S(2)}) %collective-permute-start.3) | collective-permute-done | bytes 133792 | tf_op jit(solution)/shard_map/ppermute | solution.py:111
  25.5 0.2 convert_reduce_fusion.1
  25.7 1.5 %concatenate.18 = bf16[276,1045]{1,0:T(8,128)(2,1)S(1)} concatenate(bf16[10,1045]{1,0:T(8,128)(2,1)S(1)} %get-tuple-element.12, bf16[64,1045]{1,0:T(8,128)(2,1)S(1)} %get-tuple-element.8, bf16[64,1045]{1,0:T(8,128)(2,1)S(1)} %broadcast_select_fusion.2, bf16[64,1045]{1,0:T(8,128)(2,1)S(1)} %get-tuple-element.5, bf16[64,1045]{1,0:T(8,128)(2,1)S(1)} %get-tuple-element.7, ...), dimensions={0} | concatenate | bytes 1153680 | tf_op jit(solution)/shard_map/concatenate | solution.py:115
  27.2 1.0 %gather_fusion = bf16[160,1045]{1,0:T(8,128)(2,1)S(1)} fusion(bf16[276,1045]{1,0:T(8,128)(2,1)S(1)} %concatenate.18, s32[1024]{0:T(1024)S(1)} %select_clamp_fusion), kind=kCustom, calls=%fused_computation | custom fusion | bytes 669440 | tf_op jit(solution)/shard_map/jit(_take)/gather | solution.py:133
  28.2 0.9 %pad_select_fusion.img_ref = bf16[160,1152]{1,0:T(8,128)(2,1)} fusion(bf16[160,1045]{1,0:T(8,128)(2,1)S(1)} %gather_fusion, pred[160]{0:T(512)(128)(4,1)S(1)} %compare_and_fusion), kind=kLoop, calls=%fused_computation.3 | loop fusion | flops 184320 | bytes 703200 | tf_op jit(solution)/shard_map/jit(_where)/select_n | solution.py:134
  29.1 9.0 %shard_map.91 = f32[1024,128]{1,0:T(8,128)} custom-call(f32[80]{0:T(128)} %pad_maximum_fusion.5.kp_ref, bf16[160,1152]{1,0:T(8,128)(2,1)} %pad_select_fusion.img_ref, f32[26,256]{1,0:T(8,128)} %pad_convert_fusion.tap_ref, s32[1,128]{1,0:T(1,128)} %bitcast.12, f32[1,128]{1,0:T(1,128)} %bitcast.13), custom_call_target="tpu_custom_call" | custom-call | tf_op jit(solution)/shard_map/pallas_call | solution.py:210
  38.1 1.1 %convert_bitcast_fusion = bf16[128,8,128]{2,1,0:T(8,128)(2,1)S(1)} fusion(f32[1024,128]{1,0:T(8,128)} %shard_map.91), kind=kLoop, calls=%fused_computation.9 | loop fusion | flops 131072 | bytes 786432 | tf_op jit(solution)/shard_map/convert_element_type | solution.py:231
  39.1 30.2 %all_to_all.5 = bf16[128,8,128]{2,1,0:T(8,128)(2,1)S(1)} all-to-all(bf16[128,8,128]{2,1,0:T(8,128)(2,1)S(1)} %convert_bitcast_fusion), channel_id=1, replica_groups=mesh['section'=2,'ccd'=128] {'ccd'}, dimensions={0} | all-to-all | bytes 524288 | tf_op jit(solution)/shard_map/all_to_all | solution.py:232
  69.3 0.1 convert_reduce_fusion
  69.5 0.7 reshape_broadcast_in_dim.3
  (31 shorter events, 0.8 us)
Async XLA Ops:
  0.0 0.7 copy-start.5
  0.9 0.7 copy-start.4
  3.1 15.2 %collective-permute-start.4 = (bf16[64,1045]{1,0:T(8,128)(2,1)S(1)}, bf16[64,1045]{1,0:T(8,128)(2,1)S(1)}, u32[]{:S(2)}, u32[]{:S(2)}) collective-permute-start(bf16[64,1045]{1,0:T(8,128)(2,1)S(1)} %pad_maximum_fusion), channel_id=1, source_target_pairs={{0,128},{1,129},{2,130},{3,131},{4,132},{5,133},{6,134},{7,135},{8... | collective-permute-start | bytes 401288 | tf_op jit(solution)/shard_map/ppermute | solution.py:109
  3.1 17.2 %collective-permute-start.2 = (bf16[64,1045]{1,0:T(8,128)(2,1)S(1)}, bf16[64,1045]{1,0:T(8,128)(2,1)S(1)}, u32[]{:S(2)}, u32[]{:S(2)}) collective-permute-start(bf16[64,1045]{1,0:T(8,128)(2,1)S(1)} %pad_maximum_fusion), channel_id=1, source_target_pairs={{128,1},{129,2},{130,3},{131,4},{132,5},{133,6},{134,7},{135,8},{1... | collective-permute-start | bytes 401288 | tf_op jit(solution)/shard_map/ppermute | solution.py:110
  7.0 8.8 %copy-start = (f32[13,6]{0,1:T(8,128)S(1)}, f32[13,6]{0,1:T(8,128)}, u32[]{:S(2)}) copy-start(f32[13,6]{0,1:T(8,128)} %param.13) | copy-start | bytes 940
  7.0 11.2 %collective-permute-start.1 = (bf16[10,1045]{1,0:T(8,128)(2,1)S(1)}, bf16[10,1045]{1,0:T(8,128)(2,1)S(1)}, u32[]{:S(2)}, u32[]{:S(2)}) collective-permute-start(bf16[10,1045]{1,0:T(8,128)(2,1)S(1)} %get-tuple-element.13), channel_id=1, source_target_pairs={{0,129},{1,130},{2,131},{3,132},{4,133},{5,134},{6,135},{7,136},{8... | collective-permute-start | bytes 62708 | tf_op jit(solution)/shard_map/ppermute | solution.py:113
  10.7 7.5 %collective-permute-start = (bf16[10,1045]{1,0:T(8,128)(2,1)S(1)}, bf16[10,1045]{1,0:T(8,128)(2,1)S(1)}, u32[]{:S(2)}, u32[]{:S(2)}) collective-permute-start(bf16[10,1045]{1,0:T(8,128)(2,1)S(1)} %get-tuple-element.14), channel_id=1, source_target_pairs={{0,1},{1,2},{2,3},{3,4},{4,5},{5,6},{6,7},{7,8},{8,9},{9,10},{10,1... | collective-permute-start | bytes 62708 | tf_op jit(solution)/shard_map/ppermute | solution.py:112
  16.0 0.7 copy-start.1
  16.0 0.7 copy-start.2
  16.0 0.7 copy-start.3
  18.4 7.0 %collective-permute-start.3 = (bf16[64,1045]{1,0:T(8,128)(2,1)S(1)}, bf16[64,1045]{1,0:T(8,128)(2,1)S(1)}, u32[]{:S(2)}, u32[]{:S(2)}) collective-permute-start(bf16[64,1045]{1,0:T(8,128)(2,1)S(1)} %get-tuple-element.6), channel_id=1, source_target_pairs={{128,129},{129,130},{130,131},{131,132},{132,133},{133,134},{134,1... | collective-permute-start | bytes 401288 | tf_op jit(solution)/shard_map/ppermute | solution.py:111

commit v10 on v8

--- a/solution.py
+++ b/solution.py
@@ -106,32 +106,34 @@
     cross_down = [(dev(0, b), dev(1, b + 1)) for b in range(nb - 1)] + [
         (dev(1, b), dev(0, b - 1)) for b in range(1, nb)
     ]
-    edge = lambda x: jnp.where(half == 0, x[rh - HALF_K :], x[:HALF_K])
+    rim = 16
+    edge = lambda x: jnp.where(half == 0, x[rh - rim :], x[:rim])
     got_swap = lax.ppermute(other, axes, swap)
     got_cross = lax.ppermute(other, axes, cross)
     got_straight = lax.ppermute(own, axes, straight)
     got_edge = lax.ppermute(edge(own), axes, straight_down)
     got_edge_cross = lax.ppermute(edge(other), axes, cross_down)
     pick = lambda a, b: jnp.where(half == 0, a, b)
-    window = jnp.concatenate(
-        [
-            pick(got_edge, got_edge_cross),
-            pick(got_cross, got_straight),
-            pick(own, got_swap),
-            pick(got_swap, own),
-            pick(got_straight, got_cross),
-            pick(got_edge_cross, got_edge),
-        ],
-        axis=0,
-    )
     lead = ROWS + 2 * HALF_K
     lead_pad = -(-lead // 16) * 16
-    steps = window[REACH : REACH + lead, width].astype(jnp.int32)
-    picks = jnp.pad(jnp.arange(lead) + REACH + steps, (0, lead_pad - lead))
-    out_rows = top_row - HALF_K + jnp.arange(lead_pad)
-    inside = (out_rows >= 0) & (out_rows < total_rows) & (jnp.arange(lead_pad) < lead)
-    warped = jnp.take(window, picks, axis=0, mode="clip")
-    image = jnp.where(inside[:, None], warped, jnp.zeros((), warped.dtype))
+    near = REACH - HALF_K
+    steps = jnp.concatenate(
+        [
+            pick(got_cross, got_straight)[near:, width],
+            pick(own, got_swap)[:, width],
+            pick(got_swap, own)[:, width],
+            pick(got_straight, got_cross)[: 2 * HALF_K - (REACH - near), width],
+        ]
+    ).astype(jnp.int32)
+    origin = rim + REACH
+    out_rows = top_row - HALF_K + jnp.arange(lead)
+    inside = (out_rows >= 0) & (out_rows < total_rows)
+    picks = jnp.where(inside, jnp.arange(lead) + origin - HALF_K + steps, -1)
+    picks = jnp.pad(picks, (0, lead_pad - lead), constant_values=-1)[:, None]
+    pieces = (got_edge, got_edge_cross, got_cross, got_straight, own, got_swap)
+    slot = (0, rim, rim + rh, rim + 2 * rh, rim + 3 * rh, rim + 4 * rh)
+    bases = ((slot[0], slot[5]), (slot[5], slot[0]), (slot[1], slot[4]),
+             (slot[4], slot[1]), (slot[2], slot[3]), (slot[3], slot[2]))
     span = 2 * STRIP
     both_taps = basis_taps(column_power + row_power, basis_sigma + basis_sigma)
     taps = jnp.pad(both_taps.astype(jnp.float32), ((0, 0), (0, span - KW)))
@@ -146,12 +148,24 @@
     row_tiles = ROWS // TILE
     per_lane = STRIP // TILE
 
-    def match_kernel(kp_ref, img_ref, tap_ref, own_ref, w_ref,
-                     out_ref, acc_ref, pack_ref, a_ref, b_ref, colm_ref, rowm_ref):
+    def match_kernel(kp_ref, picks_ref, e0_ref, e1_ref, p0_ref, p1_ref, p2_ref, p3_ref,
+                     tap_ref, own_ref, w_ref,
+                     out_ref, acc_ref, pack_ref, a_ref, b_ref, colm_ref, rowm_ref, img_ref):
         i = pl.program_id(0)
 
         @pl.when(i == 0)
         def _():
+            first = kp_ref[at + 1] == 0.0
+            gathered = jnp.zeros((lead_pad, wide_cols), jnp.float32)
+            piece_refs = (e0_ref, e1_ref, p0_ref, p1_ref, p2_ref, p3_ref)
+            for ref, (b0, b1) in zip(piece_refs, bases):
+                n = ref.shape[0]
+                base = jnp.where(first, b0, b1)
+                hit = lax.broadcasted_iota(jnp.int32, (lead_pad, n), 1) + base == picks_ref[...]
+                gathered = gathered + jnp.dot(
+                    hit.astype(jnp.bfloat16), ref[...], preferred_element_type=jnp.float32
+                )
+            img_ref[...] = gathered.astype(jnp.bfloat16)
             for k in range(NBASIS):
                 spread = jnp.broadcast_to(tap_ref[pl.ds(k, 1), :], (STRIP, span))
                 band_t = pltpu.roll(spread, 0, 1, stride=1, stride_axis=0)
@@ -210,13 +224,9 @@
     outgoing = pl.pallas_call(
         match_kernel,
         grid=(strips,),
-        in_specs=[
-            pl.BlockSpec(memory_space=pltpu.SMEM),
-            full(image.shape),
-            full(taps.shape),
-            full(owners.shape),
-            full(weights.shape),
-        ],
+        in_specs=[pl.BlockSpec(memory_space=pltpu.SMEM), full(picks.shape)]
+        + [full(x.shape) for x in pieces]
+        + [full(taps.shape), full(owners.shape), full(weights.shape)],
         out_specs=full((band_count * groups, STRIP)),
         out_shape=jax.ShapeDtypeStruct((band_count * groups, STRIP), jnp.float32),
         scratch_shapes=[
@@ -226,8 +236,9 @@
             pltpu.VMEM((NBASIS, ROWS, STRIP), jnp.float32),
             pltpu.VMEM((span, NBASIS * STRIP), jnp.bfloat16),
             pltpu.VMEM((NBASIS, ROWS, span), jnp.bfloat16),
+            pltpu.VMEM((lead_pad, wide_cols), jnp.bfloat16),
         ],
-    )(params, image, taps, owners, weights)
+    )(params, picks, *pieces, taps, owners, weights)
     outgoing = outgoing.reshape(band_count, groups, STRIP).astype(jnp.bfloat16)
     incoming = lax.all_to_all(outgoing, "ccd", split_axis=0, concat_axis=0, tiled=True)
     patch_sum = jnp.sum(incoming.astype(jnp.float32), axis=0, keepdims=True)

time: 67.4 us -> 66.3 us (0.984)
  blocking collectives: 33.3 us -> 34.6 us
  waiting for transfers between devices: 1.2 us -> 0.01 us
  other arithmetic: 5.28 us -> 4.57 us
    ppermute x1, starting transfers between devices: 0.09 us -> 3.29 us  [shards(): got_swap = lax.ppermute(other, axes, swap)]
    ppermute x1, starting transfers between devices: 4.92 us -> 1.91 us  [shards(): got_cross = lax.ppermute(other, axes, cross)]
    concatenate x1 -> x0, local copies, waits for them, and re-layouts: 1.5 us -> none  [shards(): jnp.concatenate([pick(got_edge, got_edge_cross), pick(got_cross, got_stra...]
    all_to_all x1, blocking collectives: 33.3 us -> 34.6 us  [shards(): lax.all_to_all(outgoing, 'ccd', split_axis=0, concat_axis=0, tiled=True)]
    unnamed x13 -> x25, local copies, waits for them, and re-layouts: 2.08 us -> 3.27 us
    ppermute x1, waiting for transfers between devices: 1.18 us -> 0.01 us  [shards(): got_edge = lax.ppermute(edge(own), axes, straight_down)]
    gather x1 -> x0, local copies, waits for them, and re-layouts: 1 us -> none  [shards(): warped = jnp.take(window, picks, axis=0, mode='clip')]
    select_n x6 -> x3, other arithmetic: 0.98 us -> 0.11 us  [the longest x1 0.08 us: shards(): picks = jnp.where(inside, jnp.arange(lead) + origin - HALF_K + steps, -1)]
  transfers between devices with their start and end apart: 5 -> 5, of which waited for: 1 -> 0; matrix products, arithmetic and copies ran while one was open for 3% -> 5% of each run, Pallas kernels for 0% -> 0%
where the time goes in v10:
time: 66.3 us; the launch traced here: 65.9 us
  blocking collectives  34.6 us (52%)
  starting transfers between devices  11.8 us (18%)
  Pallas kernels  9.34 us (14%)
  local copies, waits for them, and re-layouts  5.39 us (8%)
  other arithmetic  4.57 us (7%)
    all_to_all x1, blocking collectives, shards(): lax.all_to_all(outgoing, 'ccd', split_axis=0, concat_axis=0, tiled=True)  34.6 us
    pallas_call x1, Pallas kernels, shards(): pl.pallas_call(match_kernel, grid=(strips,), in_specs=[pl.BlockSpec(memor...  9.34 us
    ppermute x1, starting transfers between devices, shards(): got_straight = lax.ppermute(own, axes, straight)  4.64 us
    ppermute x1, starting transfers between devices, shards(): got_swap = lax.ppermute(other, axes, swap)  3.29 us
    unnamed x25, local copies, waits for them, and re-layouts  3.27 us
    ppermute x1, starting transfers between devices, shards(): got_cross = lax.ppermute(other, axes, cross)  1.91 us
  transfers between devices with their start and end apart: 5, of which 0 were waited for; matrix products, arithmetic and copies ran while one was open for 5% of the time, Pallas kernels for 0%

profile of v10, /device:TPU:1, one launch (start us, length us, event | category | flops | bytes accessed | tf_op | source)
XLA Modules:
  0.0 65.9 jit_solution(16017565225907534037)
XLA Ops:
  0.0 0.7 copy-done.11
  0.7 0.1 copy.14
  0.9 0.7 copy-done.10
  1.5 1.3 %fusion = bf16[64,2048]{1,0:T(8,128)(2,1)S(1)} fusion(f32[1,1,64,2048]{3,2,1,0:T(8,128)} %param.11, f32[1,1,64,2048]{3,2,1,0:T(8,128)} %param.9, f32[64]{0:T(128)S(1)} %bitcast.13), kind=kLoop, calls=%fused_computation.2 | loop fusion | flops 393216 | bytes 1310976 | tf_op jit(solution)/shard_map/squeeze | solution.py:80
  2.8 0.2 pad_dynamic-slice_fusion.1
  3.1 3.3 %collective-permute-start.2 = (bf16[64,1152]{1,0:T(8,128)(2,1)S(1)}, bf16[64,1152]{1,0:T(8,128)(2,1)S(1)}, u32[]{:S(2)}, u32[]{:S(2)}) collective-permute-start(bf16[64,1152]{1,0:T(8,128)(2,1)S(1)} %concatenate.13), channel_id=1, source_target_pairs={{0,128},{1,129},{2,130},{3,131},{4,132},{5,133},{6,134},{7,135},{8... | collective-permute-start | bytes 442376 | tf_op jit(solution)/shard_map/ppermute | solution.py:111
  6.4 1.9 %collective-permute-start = (bf16[64,1152]{1,0:T(8,128)(2,1)S(1)}, bf16[64,1152]{1,0:T(8,128)(2,1)S(1)}, u32[]{:S(2)}, u32[]{:S(2)}) collective-permute-start(bf16[64,1152]{1,0:T(8,128)(2,1)S(1)} %concatenate.13), channel_id=1, source_target_pairs={{128,1},{129,2},{130,3},{131,4},{132,5},{133,6},{134,7},{135,8},{1... | collective-permute-start | bytes 442376 | tf_op jit(solution)/shard_map/ppermute | solution.py:112
  8.4 0.7 %collective-permute-start.4 = (bf16[16,1152]{1,0:T(8,128)(2,1)S(1)}, bf16[16,1152]{1,0:T(8,128)(2,1)S(1)}, u32[]{:S(2)}, u32[]{:S(2)}) collective-permute-start(bf16[16,1152]{1,0:T(8,128)(2,1)S(1)} %slice_select_fusion), channel_id=1, source_target_pairs={{0,129},{1,130},{2,131},{3,132},{4,133},{5,134},{6,135},{7,136},{8... | collective-permute-start | bytes 110600 | tf_op jit(solution)/shard_map/ppermute | solution.py:115
  9.1 4.6 %collective-permute-start.1 = (bf16[64,1152]{1,0:T(8,128)(2,1)S(1)}, bf16[64,1152]{1,0:T(8,128)(2,1)S(1)}, u32[]{:S(2)}, u32[]{:S(2)}) collective-permute-start(bf16[64,1152]{1,0:T(8,128)(2,1)S(1)} %concatenate.14.p2_ref), channel_id=1, source_target_pairs={{128,129},{129,130},{130,131},{131,132},{132,133},{133,134},{134,1... | collective-permute-start | bytes 442376 | tf_op jit(solution)/shard_map/ppermute | solution.py:113
  13.8 1.3 %collective-permute-start.3 = (bf16[16,1152]{1,0:T(8,128)(2,1)S(1)}, bf16[16,1152]{1,0:T(8,128)(2,1)S(1)}, u32[]{:S(2)}, u32[]{:S(2)}) collective-permute-start(bf16[16,1152]{1,0:T(8,128)(2,1)S(1)} %slice_select_fusion.1), channel_id=1, source_target_pairs={{0,1},{1,2},{2,3},{3,4},{4,5},{5,6},{6,7},{7,8},{8,9},{9,10},{10,1... | collective-permute-start | bytes 110600 | tf_op jit(solution)/shard_map/ppermute | solution.py:114
  15.2 0.6 copy-done.7
  15.8 0.2 multiply_reduce_fusion
  16.1 0.6 pad_convert_fusion.tap_ref
  16.8 0.6 copy-done.6
  17.6 0.6 pad_maximum_fusion.kp_ref
  18.2 0.2 select_reduce_fusion.1
  18.4 0.2 fusion.3
  18.7 0.8 %copy.16.picks_ref = s32[160,1]{1,0:T(8,128)} copy(s32[160,1]{0,1:T(1,128)S(1)} %bitcast.12) | data formatting | bytes 1280 | tf_op jit(solution)/shard_map/broadcast_in_dim | solution.py:132
  19.5 0.6 copy-done.4
  20.1 9.3 %shard_map.91 = f32[1024,128]{1,0:T(8,128)} custom-call(f32[80]{0:T(128)} %pad_maximum_fusion.kp_ref, s32[160,1]{1,0:T(8,128)} %copy.16.picks_ref, bf16[16,1152]{1,0:T(8,128)(2,1)} %copy-done.5, bf16[16,1152]{1,0:T(8,128)(2,1)} %copy-done.4, bf16[64,1152]{1,0:T(8,128)(2,1)} %copy-done.2, bf16[64,1152]{1,0:T(8,128)(2,1)} %copy-done.3, ...), custom_call_target="tpu_custom_call" | custom-call | tf_op jit(solution)/shard_map/pallas_call | solution.py:224
  29.4 1.1 %convert_bitcast_fusion = bf16[128,8,128]{2,1,0:T(8,128)(2,1)S(1)} fusion(f32[1024,128]{1,0:T(8,128)} %shard_map.91), kind=kLoop, calls=%fused_computation.3 | loop fusion | flops 131072 | bytes 786432 | tf_op jit(solution)/shard_map/convert_element_type | solution.py:242
  30.5 34.6 %all_to_all.5 = bf16[128,8,128]{2,1,0:T(8,128)(2,1)S(1)} all-to-all(bf16[128,8,128]{2,1,0:T(8,128)(2,1)S(1)} %convert_bitcast_fusion), channel_id=1, replica_groups=mesh['section'=2,'ccd'=128] {'ccd'}, dimensions={0} | all-to-all | bytes 524288 | tf_op jit(solution)/shard_map/all_to_all | solution.py:243
  65.1 0.1 convert_reduce_fusion
  65.2 0.7 %reshape_broadcast_in_dim.3 = f32[1,1,32,32]{3,2,1,0:T(8,128)} reshape(f32[8,128]{1,0:T(8,128)S(1)} %convert_reduce_fusion) | data formatting | bytes 8192 | tf_op jit(solution)/shard_map/reshape;broadcast_in_dim | solution.py:245
  (40 shorter events, 0.9 us)
Async XLA Ops:
  0.0 0.7 copy-start.11
  0.9 0.7 copy-start.10
  3.1 15.1 %collective-permute-start.2 = (bf16[64,1152]{1,0:T(8,128)(2,1)S(1)}, bf16[64,1152]{1,0:T(8,128)(2,1)S(1)}, u32[]{:S(2)}, u32[]{:S(2)}) collective-permute-start(bf16[64,1152]{1,0:T(8,128)(2,1)S(1)} %concatenate.13), channel_id=1, source_target_pairs={{0,128},{1,129},{2,130},{3,131},{4,132},{5,133},{6,134},{7,135},{8... | collective-permute-start | bytes 442376 | tf_op jit(solution)/shard_map/ppermute | solution.py:111
  6.4 12.0 %collective-permute-start = (bf16[64,1152]{1,0:T(8,128)(2,1)S(1)}, bf16[64,1152]{1,0:T(8,128)(2,1)S(1)}, u32[]{:S(2)}, u32[]{:S(2)}) collective-permute-start(bf16[64,1152]{1,0:T(8,128)(2,1)S(1)} %concatenate.13), channel_id=1, source_target_pairs={{128,1},{129,2},{130,3},{131,4},{132,5},{133,6},{134,7},{135,8},{1... | collective-permute-start | bytes 442376 | tf_op jit(solution)/shard_map/ppermute | solution.py:112
  8.4 11.1 %collective-permute-start.4 = (bf16[16,1152]{1,0:T(8,128)(2,1)S(1)}, bf16[16,1152]{1,0:T(8,128)(2,1)S(1)}, u32[]{:S(2)}, u32[]{:S(2)}) collective-permute-start(bf16[16,1152]{1,0:T(8,128)(2,1)S(1)} %slice_select_fusion), channel_id=1, source_target_pairs={{0,129},{1,130},{2,131},{3,132},{4,133},{5,134},{6,135},{7,136},{8... | collective-permute-start | bytes 110600 | tf_op jit(solution)/shard_map/ppermute | solution.py:115
  9.1 10.3 %copy-start = (bf16[64,1152]{1,0:T(8,128)(2,1)}, bf16[64,1152]{1,0:T(8,128)(2,1)S(1)}, u32[]{:S(2)}) copy-start(bf16[64,1152]{1,0:T(8,128)(2,1)S(1)} %concatenate.14.p2_ref) | copy-start | bytes 442372
  9.1 9.2 %collective-permute-start.1 = (bf16[64,1152]{1,0:T(8,128)(2,1)S(1)}, bf16[64,1152]{1,0:T(8,128)(2,1)S(1)}, u32[]{:S(2)}, u32[]{:S(2)}) collective-permute-start(bf16[64,1152]{1,0:T(8,128)(2,1)S(1)} %concatenate.14.p2_ref), channel_id=1, source_target_pairs={{128,129},{129,130},{130,131},{131,132},{132,133},{133,134},{134,1... | collective-permute-start | bytes 442376 | tf_op jit(solution)/shard_map/ppermute | solution.py:113
  13.8 5.7 %collective-permute-start.3 = (bf16[16,1152]{1,0:T(8,128)(2,1)S(1)}, bf16[16,1152]{1,0:T(8,128)(2,1)S(1)}, u32[]{:S(2)}, u32[]{:S(2)}) collective-permute-start(bf16[16,1152]{1,0:T(8,128)(2,1)S(1)} %slice_select_fusion.1), channel_id=1, source_target_pairs={{0,1},{1,2},{2,3},{3,4},{4,5},{5,6},{6,7},{7,8},{8,9},{9,10},{10,1... | collective-permute-start | bytes 110600 | tf_op jit(solution)/shard_map/ppermute | solution.py:114
  15.1 0.7 copy-start.7
  15.1 0.7 %copy-start.8 = (pred[26]{0:T(512)(128)(4,1)S(1)}, pred[26]{0:T(512)(128)(4,1)}, u32[]{:S(2)}) copy-start(pred[26]{0:T(512)(128)(4,1)} %constant.70) | copy-start | bytes 82
  15.2 0.7 %copy-start.9 = (pred[26]{0:T(512)(128)(4,1)S(1)}, pred[26]{0:T(512)(128)(4,1)}, u32[]{:S(2)}) copy-start(pred[26]{0:T(512)(128)(4,1)} %constant.69) | copy-start | bytes 82
  16.7 0.7 %copy-start.6 = (f32[13,6]{0,1:T(8,128)S(1)}, f32[13,6]{0,1:T(8,128)}, u32[]{:S(2)}) copy-start(f32[13,6]{0,1:T(8,128)} %param.13) | copy-start | bytes 940
  18.2 1.3 %copy-start.1 = (bf16[64,1152]{1,0:T(8,128)(2,1)}, bf16[64,1152]{1,0:T(8,128)(2,1)S(1)}, u32[]{:S(2)}) copy-start(bf16[64,1152]{1,0:T(8,128)(2,1)S(1)} %collective-permute-done.2.p3_ref) | copy-start | bytes 442372
  18.4 1.1 %copy-start.3 = (bf16[64,1152]{1,0:T(8,128)(2,1)}, bf16[64,1152]{1,0:T(8,128)(2,1)S(1)}, u32[]{:S(2)}) copy-start(bf16[64,1152]{1,0:T(8,128)(2,1)S(1)} %collective-permute-done.1.p1_ref) | copy-start | bytes 442372
  18.4 1.1 %copy-start.2 = (bf16[64,1152]{1,0:T(8,128)(2,1)}, bf16[64,1152]{1,0:T(8,128)(2,1)S(1)}, u32[]{:S(2)}) copy-start(bf16[64,1152]{1,0:T(8,128)(2,1)S(1)} %collective-permute-done.p0_ref) | copy-start | bytes 442372
  19.5 0.6 copy-start.4
  19.5 0.6 copy-start.5

commit v11 on v10

--- a/solution.py
+++ b/solution.py
@@ -215,10 +215,10 @@
             sel = jnp.where(owner_ids == own_ref[...], w_ref[...], 0.0)
             for q in range(groups):
                 part = pack_ref[pl.ds(q, tiles, stride=groups), :]
-                out_ref[pl.ds(q, band_count, stride=groups), :] = jnp.dot(
+                out_ref[:, q, :] = jnp.dot(
                     sel, part, precision=lax.Precision.HIGHEST,
                     preferred_element_type=jnp.float32,
-                )
+                ).astype(out_ref.dtype)
 
     full = lambda shape: pl.BlockSpec(shape, lambda i: (0,) * len(shape))
     outgoing = pl.pallas_call(
@@ -227,8 +227,8 @@
         in_specs=[pl.BlockSpec(memory_space=pltpu.SMEM), full(picks.shape)]
         + [full(x.shape) for x in pieces]
         + [full(taps.shape), full(owners.shape), full(weights.shape)],
-        out_specs=full((band_count * groups, STRIP)),
-        out_shape=jax.ShapeDtypeStruct((band_count * groups, STRIP), jnp.float32),
+        out_specs=full((band_count, groups, STRIP)),
+        out_shape=jax.ShapeDtypeStruct((band_count, groups, STRIP), jnp.bfloat16),
         scratch_shapes=[
             pltpu.VMEM((ROWS, STRIP), jnp.float32),
             pltpu.VMEM((tiles * groups, STRIP), jnp.float32),
@@ -239,7 +239,6 @@
             pltpu.VMEM((lead_pad, wide_cols), jnp.bfloat16),
         ],
     )(params, picks, *pieces, taps, owners, weights)
-    outgoing = outgoing.reshape(band_count, groups, STRIP).astype(jnp.bfloat16)
     incoming = lax.all_to_all(outgoing, "ccd", split_axis=0, concat_axis=0, tiled=True)
     patch_sum = jnp.sum(incoming.astype(jnp.float32), axis=0, keepdims=True)
     return patch_sum.reshape(1, 1, TILE, TILE)

time: 66.3 us -> 65.8 us (level)
  other arithmetic: 4.57 us -> 3.51 us
    convert_element_type x1 -> x0, other arithmetic: 1.07 us -> none  [shards(): outgoing = outgoing.reshape(band_count, groups, STRIP).astype(jnp.bfloat16)]
where the time goes in v11:
time: 65.8 us; the launch traced here: 65.5 us
  blocking collectives  34.8 us (53%)
  starting transfers between devices  11.8 us (18%)
  Pallas kernels  9.76 us (15%)
  local copies, waits for them, and re-layouts  5.4 us (8%)
  other arithmetic  3.51 us (5%)
    all_to_all x1, blocking collectives, shards(): lax.all_to_all(outgoing, 'ccd', split_axis=0, concat_axis=0, tiled=True)  34.8 us
    pallas_call x1, Pallas kernels, shards(): pl.pallas_call(match_kernel, grid=(strips,), in_specs=[pl.BlockSpec(memor...  9.76 us
    ppermute x1, starting transfers between devices, shards(): got_straight = lax.ppermute(own, axes, straight)  4.64 us
    ppermute x1, starting transfers between devices, shards(): got_swap = lax.ppermute(other, axes, swap)  3.29 us
    unnamed x25, local copies, waits for them, and re-layouts  3.28 us
    ppermute x1, starting transfers between devices, shards(): got_cross = lax.ppermute(other, axes, cross)  1.91 us
  transfers between devices with their start and end apart: 5, of which 0 were waited for; matrix products, arithmetic and copies ran while one was open for 5% of the time, Pallas kernels for 0%

profile of v11, /device:TPU:1, one launch (start us, length us, event | category | flops | bytes accessed | tf_op | source)
XLA Modules:
  0.0 65.5 jit_solution(7215581418254574358)
XLA Ops:
  0.0 0.7 copy-done.11
  0.7 0.1 copy.14
  0.9 0.7 %copy-done.10 = f32[1,1,64]{2,1,0:T(1,128)S(1)} copy-done((f32[1,1,64]{2,1,0:T(1,128)S(1)}, f32[1,1,64]{2,1,0:T(1,128)}, u32[]{:S(2)}) %copy-start.10) | copy-done | bytes 280
  1.5 1.3 %fusion = bf16[64,2048]{1,0:T(8,128)(2,1)S(1)} fusion(f32[1,1,64,2048]{3,2,1,0:T(8,128)} %param.11, f32[1,1,64,2048]{3,2,1,0:T(8,128)} %param.9, f32[64]{0:T(128)S(1)} %bitcast.11), kind=kLoop, calls=%fused_computation.2 | loop fusion | flops 393216 | bytes 1310976 | tf_op jit(solution)/shard_map/squeeze | solution.py:80
  2.8 0.2 pad_dynamic-slice_fusion.1
  3.1 3.3 %collective-permute-start.2 = (bf16[64,1152]{1,0:T(8,128)(2,1)S(1)}, bf16[64,1152]{1,0:T(8,128)(2,1)S(1)}, u32[]{:S(2)}, u32[]{:S(2)}) collective-permute-start(bf16[64,1152]{1,0:T(8,128)(2,1)S(1)} %concatenate.13), channel_id=1, source_target_pairs={{0,128},{1,129},{2,130},{3,131},{4,132},{5,133},{6,134},{7,135},{8... | collective-permute-start | bytes 442376 | tf_op jit(solution)/shard_map/ppermute | solution.py:111
  6.4 1.9 %collective-permute-start = (bf16[64,1152]{1,0:T(8,128)(2,1)S(1)}, bf16[64,1152]{1,0:T(8,128)(2,1)S(1)}, u32[]{:S(2)}, u32[]{:S(2)}) collective-permute-start(bf16[64,1152]{1,0:T(8,128)(2,1)S(1)} %concatenate.13), channel_id=1, source_target_pairs={{128,1},{129,2},{130,3},{131,4},{132,5},{133,6},{134,7},{135,8},{1... | collective-permute-start | bytes 442376 | tf_op jit(solution)/shard_map/ppermute | solution.py:112
  8.4 0.7 %collective-permute-start.4 = (bf16[16,1152]{1,0:T(8,128)(2,1)S(1)}, bf16[16,1152]{1,0:T(8,128)(2,1)S(1)}, u32[]{:S(2)}, u32[]{:S(2)}) collective-permute-start(bf16[16,1152]{1,0:T(8,128)(2,1)S(1)} %slice_select_fusion), channel_id=1, source_target_pairs={{0,129},{1,130},{2,131},{3,132},{4,133},{5,134},{6,135},{7,136},{8... | collective-permute-start | bytes 110600 | tf_op jit(solution)/shard_map/ppermute | solution.py:115
  9.0 0.1 concatenate.14.p2_ref
  9.1 4.6 %collective-permute-start.1 = (bf16[64,1152]{1,0:T(8,128)(2,1)S(1)}, bf16[64,1152]{1,0:T(8,128)(2,1)S(1)}, u32[]{:S(2)}, u32[]{:S(2)}) collective-permute-start(bf16[64,1152]{1,0:T(8,128)(2,1)S(1)} %concatenate.14.p2_ref), channel_id=1, source_target_pairs={{128,129},{129,130},{130,131},{131,132},{132,133},{133,134},{134,1... | collective-permute-start | bytes 442376 | tf_op jit(solution)/shard_map/ppermute | solution.py:113
  13.8 1.3 %collective-permute-start.3 = (bf16[16,1152]{1,0:T(8,128)(2,1)S(1)}, bf16[16,1152]{1,0:T(8,128)(2,1)S(1)}, u32[]{:S(2)}, u32[]{:S(2)}) collective-permute-start(bf16[16,1152]{1,0:T(8,128)(2,1)S(1)} %slice_select_fusion.1), channel_id=1, source_target_pairs={{0,1},{1,2},{2,3},{3,4},{4,5},{5,6},{6,7},{7,8},{8,9},{9,10},{10,1... | collective-permute-start | bytes 110600 | tf_op jit(solution)/shard_map/ppermute | solution.py:114
  15.2 0.6 copy-done.7
  15.8 0.2 multiply_reduce_fusion
  16.1 0.6 pad_convert_fusion.tap_ref
  16.8 0.6 copy-done.6
  17.6 0.6 pad_maximum_fusion.kp_ref
  18.2 0.2 select_reduce_fusion.1
  18.4 0.2 fusion.3
  18.7 0.8 %copy.16.picks_ref = s32[160,1]{1,0:T(8,128)} copy(s32[160,1]{0,1:T(1,128)S(1)} %bitcast.10) | data formatting | bytes 1280 | tf_op jit(solution)/shard_map/broadcast_in_dim | solution.py:132
  19.5 0.6 copy-done.4
  20.1 9.8 %shard_map.91 = bf16[128,8,128]{2,1,0:T(8,128)(2,1)} custom-call(f32[80]{0:T(128)} %pad_maximum_fusion.kp_ref, s32[160,1]{1,0:T(8,128)} %copy.16.picks_ref, bf16[16,1152]{1,0:T(8,128)(2,1)} %copy-done.5, bf16[16,1152]{1,0:T(8,128)(2,1)} %copy-done.4, bf16[64,1152]{1,0:T(8,128)(2,1)} %copy-done.2, bf16[64,1152]{1,0:T(8,128)(2,1)} %copy-done.3, ...), custom_call_target="tpu_custom_call" | custom-call | tf_op jit(solution)/shard_map/pallas_call | solution.py:224
  29.9 34.8 %all_to_all.5 = bf16[128,8,128]{2,1,0:T(8,128)(2,1)S(1)} all-to-all(bf16[128,8,128]{2,1,0:T(8,128)(2,1)} %shard_map.91), channel_id=1, replica_groups=mesh['section'=2,'ccd'=128] {'ccd'}, dimensions={0} | all-to-all | bytes 524288 | tf_op jit(solution)/shard_map/all_to_all | solution.py:242
  64.6 0.1 convert_reduce_fusion
  64.8 0.7 %reshape_broadcast_in_dim.3 = f32[1,1,32,32]{3,2,1,0:T(8,128)} reshape(f32[8,128]{1,0:T(8,128)S(1)} %convert_reduce_fusion) | data formatting | bytes 8192 | tf_op jit(solution)/shard_map/reshape;broadcast_in_dim | solution.py:244
  (39 shorter events, 0.8 us)
Async XLA Ops:
  0.0 0.7 %copy-start.11 = (s32[128]{0:T(128)S(1)}, s32[128]{0:T(128)}, u32[]{:S(2)}) copy-start(s32[128]{0:T(128)} %param.12) | copy-start | bytes 1540
  0.9 0.7 %copy-start.10 = (f32[1,1,64]{2,1,0:T(1,128)S(1)}, f32[1,1,64]{2,1,0:T(1,128)}, u32[]{:S(2)}) copy-start(f32[1,1,64]{2,1,0:T(1,128)} %param.10) | copy-start | bytes 772
  3.1 15.1 %collective-permute-start.2 = (bf16[64,1152]{1,0:T(8,128)(2,1)S(1)}, bf16[64,1152]{1,0:T(8,128)(2,1)S(1)}, u32[]{:S(2)}, u32[]{:S(2)}) collective-permute-start(bf16[64,1152]{1,0:T(8,128)(2,1)S(1)} %concatenate.13), channel_id=1, source_target_pairs={{0,128},{1,129},{2,130},{3,131},{4,132},{5,133},{6,134},{7,135},{8... | collective-permute-start | bytes 442376 | tf_op jit(solution)/shard_map/ppermute | solution.py:111
  6.4 12.0 %collective-permute-start = (bf16[64,1152]{1,0:T(8,128)(2,1)S(1)}, bf16[64,1152]{1,0:T(8,128)(2,1)S(1)}, u32[]{:S(2)}, u32[]{:S(2)}) collective-permute-start(bf16[64,1152]{1,0:T(8,128)(2,1)S(1)} %concatenate.13), channel_id=1, source_target_pairs={{128,1},{129,2},{130,3},{131,4},{132,5},{133,6},{134,7},{135,8},{1... | collective-permute-start | bytes 442376 | tf_op jit(solution)/shard_map/ppermute | solution.py:112
  8.4 11.1 %collective-permute-start.4 = (bf16[16,1152]{1,0:T(8,128)(2,1)S(1)}, bf16[16,1152]{1,0:T(8,128)(2,1)S(1)}, u32[]{:S(2)}, u32[]{:S(2)}) collective-permute-start(bf16[16,1152]{1,0:T(8,128)(2,1)S(1)} %slice_select_fusion), channel_id=1, source_target_pairs={{0,129},{1,130},{2,131},{3,132},{4,133},{5,134},{6,135},{7,136},{8... | collective-permute-start | bytes 110600 | tf_op jit(solution)/shard_map/ppermute | solution.py:115
  9.1 10.3 %copy-start = (bf16[64,1152]{1,0:T(8,128)(2,1)}, bf16[64,1152]{1,0:T(8,128)(2,1)S(1)}, u32[]{:S(2)}) copy-start(bf16[64,1152]{1,0:T(8,128)(2,1)S(1)} %concatenate.14.p2_ref) | copy-start | bytes 442372
  9.1 9.2 %collective-permute-start.1 = (bf16[64,1152]{1,0:T(8,128)(2,1)S(1)}, bf16[64,1152]{1,0:T(8,128)(2,1)S(1)}, u32[]{:S(2)}, u32[]{:S(2)}) collective-permute-start(bf16[64,1152]{1,0:T(8,128)(2,1)S(1)} %concatenate.14.p2_ref), channel_id=1, source_target_pairs={{128,129},{129,130},{130,131},{131,132},{132,133},{133,134},{134,1... | collective-permute-start | bytes 442376 | tf_op jit(solution)/shard_map/ppermute | solution.py:113
  13.8 5.7 %collective-permute-start.3 = (bf16[16,1152]{1,0:T(8,128)(2,1)S(1)}, bf16[16,1152]{1,0:T(8,128)(2,1)S(1)}, u32[]{:S(2)}, u32[]{:S(2)}) collective-permute-start(bf16[16,1152]{1,0:T(8,128)(2,1)S(1)} %slice_select_fusion.1), channel_id=1, source_target_pairs={{0,1},{1,2},{2,3},{3,4},{4,5},{5,6},{6,7},{7,8},{8,9},{9,10},{10,1... | collective-permute-start | bytes 110600 | tf_op jit(solution)/shard_map/ppermute | solution.py:114
  15.1 0.7 %copy-start.7 = (f32[26]{0:T(128)S(1)}, f32[26]{0:T(128)}, u32[]{:S(2)}) copy-start(f32[26]{0:T(128)} %constant.71) | copy-start | bytes 316
  15.1 0.7 %copy-start.8 = (pred[26]{0:T(512)(128)(4,1)S(1)}, pred[26]{0:T(512)(128)(4,1)}, u32[]{:S(2)}) copy-start(pred[26]{0:T(512)(128)(4,1)} %constant.70) | copy-start | bytes 82
  15.2 0.7 %copy-start.9 = (pred[26]{0:T(512)(128)(4,1)S(1)}, pred[26]{0:T(512)(128)(4,1)}, u32[]{:S(2)}) copy-start(pred[26]{0:T(512)(128)(4,1)} %constant.69) | copy-start | bytes 82
  16.7 0.7 %copy-start.6 = (f32[13,6]{0,1:T(8,128)S(1)}, f32[13,6]{0,1:T(8,128)}, u32[]{:S(2)}) copy-start(f32[13,6]{0,1:T(8,128)} %param.13) | copy-start | bytes 940
  18.2 1.3 %copy-start.1 = (bf16[64,1152]{1,0:T(8,128)(2,1)}, bf16[64,1152]{1,0:T(8,128)(2,1)S(1)}, u32[]{:S(2)}) copy-start(bf16[64,1152]{1,0:T(8,128)(2,1)S(1)} %collective-permute-done.2.p3_ref) | copy-start | bytes 442372
  18.4 1.1 %copy-start.3 = (bf16[64,1152]{1,0:T(8,128)(2,1)}, bf16[64,1152]{1,0:T(8,128)(2,1)S(1)}, u32[]{:S(2)}) copy-start(bf16[64,1152]{1,0:T(8,128)(2,1)S(1)} %collective-permute-done.1.p1_ref) | copy-start | bytes 442372
  18.4 1.1 %copy-start.2 = (bf16[64,1152]{1,0:T(8,128)(2,1)}, bf16[64,1152]{1,0:T(8,128)(2,1)S(1)}, u32[]{:S(2)}) copy-start(bf16[64,1152]{1,0:T(8,128)(2,1)S(1)} %collective-permute-done.p0_ref) | copy-start | bytes 442372
  19.5 0.6 copy-start.4
  19.5 0.6 copy-start.5

commit v12 on v11

--- a/solution.py
+++ b/solution.py
@@ -91,38 +91,26 @@
     own = slab(half * CH)
     other = slab((1 - half) * CH)
     nb = band_count
-    dev = lambda s, b: s * nb + b
     axes = ("section", "ccd")
-    swap = [(dev(s, b), dev(1 - s, b)) for s in range(2) for b in range(nb)]
-    cross = [(dev(1, b), dev(0, b + 1)) for b in range(nb - 1)] + [
-        (dev(0, b), dev(1, b - 1)) for b in range(1, nb)
-    ]
-    straight = [(dev(1, b), dev(1, b + 1)) for b in range(nb - 1)] + [
-        (dev(0, b), dev(0, b - 1)) for b in range(1, nb)
-    ]
-    straight_down = [(dev(0, b), dev(0, b + 1)) for b in range(nb - 1)] + [
-        (dev(1, b), dev(1, b - 1)) for b in range(1, nb)
-    ]
-    cross_down = [(dev(0, b), dev(1, b + 1)) for b in range(nb - 1)] + [
-        (dev(1, b), dev(0, b - 1)) for b in range(1, nb)
-    ]
+    swap = [(s * nb + b, (1 - s) * nb + b) for s in range(2) for b in range(nb)]
+    got_swap = lax.ppermute(other, axes, swap)
+    pick = lambda a, b: jnp.where(half == 0, a, b)
+    first_rows = pick(own, got_swap)
+    second_rows = pick(got_swap, own)
     rim = 16
-    edge = lambda x: jnp.where(half == 0, x[rh - rim :], x[:rim])
-    got_swap = lax.ppermute(other, axes, swap)
-    got_cross = lax.ppermute(other, axes, cross)
-    got_straight = lax.ppermute(own, axes, straight)
-    got_edge = lax.ppermute(edge(own), axes, straight_down)
-    got_edge_cross = lax.ppermute(edge(other), axes, cross_down)
-    pick = lambda a, b: jnp.where(half == 0, a, b)
+    sent_up = jnp.concatenate([first_rows, second_rows[:rim]], axis=0)
+    sent_down = jnp.concatenate([first_rows[rh - rim :], second_rows], axis=0)
+    from_below = lax.ppermute(sent_up, "ccd", [(b, b - 1) for b in range(1, nb)])
+    from_above = lax.ppermute(sent_down, "ccd", [(b, b + 1) for b in range(nb - 1)])
     lead = ROWS + 2 * HALF_K
     lead_pad = -(-lead // 16) * 16
-    near = REACH - HALF_K
+    above = rh + rim
     steps = jnp.concatenate(
         [
-            pick(got_cross, got_straight)[near:, width],
-            pick(own, got_swap)[:, width],
-            pick(got_swap, own)[:, width],
-            pick(got_straight, got_cross)[: 2 * HALF_K - (REACH - near), width],
+            from_above[above - HALF_K :, width],
+            first_rows[:, width],
+            second_rows[:, width],
+            from_below[:HALF_K, width],
         ]
     ).astype(jnp.int32)
     origin = rim + REACH
@@ -130,10 +118,8 @@
     inside = (out_rows >= 0) & (out_rows < total_rows)
     picks = jnp.where(inside, jnp.arange(lead) + origin - HALF_K + steps, -1)
     picks = jnp.pad(picks, (0, lead_pad - lead), constant_values=-1)[:, None]
-    pieces = (got_edge, got_edge_cross, got_cross, got_straight, own, got_swap)
-    slot = (0, rim, rim + rh, rim + 2 * rh, rim + 3 * rh, rim + 4 * rh)
-    bases = ((slot[0], slot[5]), (slot[5], slot[0]), (slot[1], slot[4]),
-             (slot[4], slot[1]), (slot[2], slot[3]), (slot[3], slot[2]))
+    pieces = (from_above, own, got_swap, from_below)
+    bases = ((0, 0), (above, above + rh), (above + rh, above), (above + 2 * rh, above + 2 * rh))
     span = 2 * STRIP
     both_taps = basis_taps(column_power + row_power, basis_sigma + basis_sigma)
     taps = jnp.pad(both_taps.astype(jnp.float32), ((0, 0), (0, span - KW)))
@@ -148,7 +134,7 @@
     row_tiles = ROWS // TILE
     per_lane = STRIP // TILE
 
-    def match_kernel(kp_ref, picks_ref, e0_ref, e1_ref, p0_ref, p1_ref, p2_ref, p3_ref,
+    def match_kernel(kp_ref, picks_ref, p0_ref, p1_ref, p2_ref, p3_ref,
                      tap_ref, own_ref, w_ref,
                      out_ref, acc_ref, pack_ref, a_ref, b_ref, colm_ref, rowm_ref, img_ref):
         i = pl.program_id(0)
@@ -157,7 +143,7 @@
         def _():
             first = kp_ref[at + 1] == 0.0
             gathered = jnp.zeros((lead_pad, wide_cols), jnp.float32)
-            piece_refs = (e0_ref, e1_ref, p0_ref, p1_ref, p2_ref, p3_ref)
+            piece_refs = (p0_ref, p1_ref, p2_ref, p3_ref)
             for ref, (b0, b1) in zip(piece_refs, bases):
                 n = ref.shape[0]
                 base = jnp.where(first, b0, b1)

time: 65.8 us -> 62 us (0.942)
  blocking collectives: 34.8 us -> 30.7 us
  waiting for transfers between devices: 0.01 us -> 3.3 us
  starting transfers between devices: 11.8 us -> 8.58 us
    all_to_all x1, blocking collectives: 34.8 us -> 30.7 us  [shards(): lax.all_to_all(outgoing, 'ccd', split_axis=0, concat_axis=0, tiled=True)]
    ppermute x4 -> x2, waiting for transfers between devices: 0.01 us -> 3.29 us  [the longest x1 2.55 us: shards(): lax.ppermute(sent_up, 'ccd', [(b, b - 1) for b in range(1, nb)])]
    ppermute x4 -> x2, starting transfers between devices: 8.5 us -> 5.29 us  [the longest x1 4 us: shards(): lax.ppermute(sent_down, 'ccd', [(b, b + 1) for b in range(nb - 1)])]
    unnamed x25 -> x21, local copies, waits for them, and re-layouts: 3.28 us -> 3.3 us
  transfers between devices with their start and end apart: 5 -> 3, of which waited for: 0 -> 2; matrix products, arithmetic and copies ran while one was open for 5% -> 4% of each run, Pallas kernels for 0% -> 0%
where the time goes in v12:
time: 62 us; the launch traced here: 61.7 us
  blocking collectives  30.7 us (50%)
  Pallas kernels  9.8 us (16%)
  starting transfers between devices  8.58 us (14%)
  local copies, waits for them, and re-layouts  5.97 us (10%)
  waiting for transfers between devices  3.3 us (5%)
  other arithmetic  3.22 us (5%)
    all_to_all x1, blocking collectives, shards(): lax.all_to_all(outgoing, 'ccd', split_axis=0, concat_axis=0, tiled=True)  30.7 us
    pallas_call x1, Pallas kernels, shards(): pl.pallas_call(match_kernel, grid=(strips,), in_specs=[pl.BlockSpec(memor...  9.8 us
    ppermute x1, starting transfers between devices, shards(): lax.ppermute(sent_down, 'ccd', [(b, b + 1) for b in range(nb - 1)])  4 us
    unnamed x21, local copies, waits for them, and re-layouts  3.3 us
    ppermute x1, starting transfers between devices, shards(): got_swap = lax.ppermute(other, axes, swap)  3.29 us
    ppermute x1, waiting for transfers between devices, shards(): lax.ppermute(sent_up, 'ccd', [(b, b - 1) for b in range(1, nb)])  2.55 us
    squeeze x1, other arithmetic, shards(): ((raw_counts - overscan[..., None]) * response).astype(jnp.bfloat16)[0, 0]  1.31 us
    ppermute x1, starting transfers between devices, shards(): lax.ppermute(sent_up, 'ccd', [(b, b - 1) for b in range(1, nb)])  1.29 us
  transfers between devices with their start and end apart: 3, of which 2 were waited for; matrix products, arithmetic and copies ran while one was open for 4% of the time, Pallas kernels for 0%

profile of v12, /device:TPU:1, one launch (start us, length us, event | category | flops | bytes accessed | tf_op | source)
XLA Modules:
  0.0 61.7 jit_solution(8321350834733631265)
XLA Ops:
  0.0 0.7 %copy-done.9 = s32[128]{0:T(128)S(1)} copy-done((s32[128]{0:T(128)S(1)}, s32[128]{0:T(128)}, u32[]{:S(2)}) %copy-start.9) | copy-done | bytes 536
  0.7 0.1 copy.14
  0.9 0.7 %copy-done.8 = f32[1,1,64]{2,1,0:T(1,128)S(1)} copy-done((f32[1,1,64]{2,1,0:T(1,128)S(1)}, f32[1,1,64]{2,1,0:T(1,128)}, u32[]{:S(2)}) %copy-start.8) | copy-done | bytes 280
  1.5 1.3 %fusion = bf16[64,2048]{1,0:T(8,128)(2,1)S(1)} fusion(f32[1,1,64,2048]{3,2,1,0:T(8,128)} %param.11, f32[1,1,64,2048]{3,2,1,0:T(8,128)} %param.9, f32[64]{0:T(128)S(1)} %bitcast.11), kind=kLoop, calls=%fused_computation.2 | loop fusion | flops 393216 | bytes 1310976 | tf_op jit(solution)/shard_map/squeeze | solution.py:80
  2.8 0.2 pad_dynamic-slice_fusion.1
  3.1 3.3 %collective-permute-start = (bf16[64,1152]{1,0:T(8,128)(2,1)S(1)}, bf16[64,1152]{1,0:T(8,128)(2,1)S(1)}, u32[]{:S(2)}, u32[]{:S(2)}) collective-permute-start(bf16[64,1152]{1,0:T(8,128)(2,1)S(1)} %concatenate.20), channel_id=1, source_target_pairs={{0,128},{1,129},{2,130},{3,131},{4,132},{5,133},{6,134},{7,135},{8... | collective-permute-start | bytes 442376 | tf_op jit(solution)/shard_map/ppermute | solution.py:96
  6.5 0.6 %copy-done.5 = f32[26]{0:T(128)S(1)} copy-done((f32[26]{0:T(128)S(1)}, f32[26]{0:T(128)}, u32[]{:S(2)}) %copy-start.5) | copy-done | bytes 128
  7.1 0.2 multiply_reduce_fusion
  7.4 0.6 copy-done.4
  8.3 0.6 pad_maximum_fusion.2.kp_ref
  9.0 0.7 %pad_convert_fusion.tap_ref = f32[26,256]{1,0:T(8,128)} fusion(bf16[26,21]{1,0:T(8,128)(2,1)S(1)} %divide_convert_fusion), kind=kLoop, calls=%fused_computation.13 | loop fusion | flops 6656 | bytes 27716 | tf_op jit(solution)/shard_map/jit(_pad)/pad | solution.py:125
  9.7 0.6 copy-done.1
  10.3 1.3 %collective-permute-start.2 = (bf16[80,1152]{1,0:T(8,128)(2,1)S(1)}, bf16[80,1152]{1,0:T(8,128)(2,1)S(1)}, u32[]{:S(2)}, u32[]{:S(2)}) collective-permute-start(bf16[80,1152]{1,0:T(8,128)(2,1)S(1)} %pad_maximum_fusion.1), channel_id=1, source_target_pairs={{1,0},{2,1},{3,2},{4,3},{5,4},{6,5},{7,6},{8,7},{9,8},{10,9},{11,1... | collective-permute-start | bytes 552968 | tf_op jit(solution)/shard_map/ppermute | solution.py:103
  11.7 4.0 %collective-permute-start.1 = (bf16[80,1152]{1,0:T(8,128)(2,1)S(1)}, bf16[80,1152]{1,0:T(8,128)(2,1)S(1)}, u32[]{:S(2)}, u32[]{:S(2)}) collective-permute-start(bf16[80,1152]{1,0:T(8,128)(2,1)S(1)} %pad_maximum_fusion), channel_id=1, source_target_pairs={{0,1},{1,2},{2,3},{3,4},{4,5},{5,6},{6,7},{7,8},{8,9},{9,10},{10,1... | collective-permute-start | bytes 552968 | tf_op jit(solution)/shard_map/ppermute | solution.py:104
  15.7 0.2 slice_reduce_fusion
  15.8 2.6 %collective-permute-done.2.p3_ref = bf16[80,1152]{1,0:T(8,128)(2,1)S(1)} collective-permute-done((bf16[80,1152]{1,0:T(8,128)(2,1)S(1)}, bf16[80,1152]{1,0:T(8,128)(2,1)S(1)}, u32[]{:S(2)}, u32[]{:S(2)}) %collective-permute-start.2) | collective-permute-done | bytes 184352 | tf_op jit(solution)/shard_map/ppermute | solution.py:103
  18.4 0.2 slice_reduce_fusion.2
  18.6 0.7 %collective-permute-done.1.p0_ref = bf16[80,1152]{1,0:T(8,128)(2,1)S(1)} collective-permute-done((bf16[80,1152]{1,0:T(8,128)(2,1)S(1)}, bf16[80,1152]{1,0:T(8,128)(2,1)S(1)}, u32[]{:S(2)}, u32[]{:S(2)}) %collective-permute-start.1) | collective-permute-done | bytes 184352 | tf_op jit(solution)/shard_map/ppermute | solution.py:104
  19.3 0.2 slice_reduce_fusion.3
  19.6 0.8 %copy.16.picks_ref = s32[160,1]{1,0:T(8,128)} copy(s32[160,1]{0,1:T(1,128)S(1)} %bitcast.10) | data formatting | bytes 1280 | tf_op jit(solution)/shard_map/broadcast_in_dim | solution.py:120
  20.4 9.8 %shard_map.91 = bf16[128,8,128]{2,1,0:T(8,128)(2,1)} custom-call(f32[80]{0:T(128)} %pad_maximum_fusion.2.kp_ref, s32[160,1]{1,0:T(8,128)} %copy.16.picks_ref, bf16[80,1152]{1,0:T(8,128)(2,1)} %copy-done.3, bf16[64,1152]{1,0:T(8,128)(2,1)} %copy-done, bf16[64,1152]{1,0:T(8,128)(2,1)} %copy-done.1, bf16[80,1152]{1,0:T(8,128)(2,1)} %copy-done.2, ...), custom_call_target="tpu_custom_call" | custom-call | tf_op jit(solution)/shard_map/pallas_call | solution.py:210
  30.2 30.7 %all_to_all.5 = bf16[128,8,128]{2,1,0:T(8,128)(2,1)S(1)} all-to-all(bf16[128,8,128]{2,1,0:T(8,128)(2,1)} %shard_map.91), channel_id=1, replica_groups=mesh['section'=2,'ccd'=128] {'ccd'}, dimensions={0} | all-to-all | bytes 524288 | tf_op jit(solution)/shard_map/all_to_all | solution.py:228
  60.9 0.1 convert_reduce_fusion
  61.0 0.7 %reshape_broadcast_in_dim.3 = f32[1,1,32,32]{3,2,1,0:T(8,128)} reshape(f32[8,128]{1,0:T(8,128)S(1)} %convert_reduce_fusion) | data formatting | bytes 8192 | tf_op jit(solution)/shard_map/reshape;broadcast_in_dim | solution.py:230
  (35 shorter events, 0.9 us)
Async XLA Ops:
  0.0 0.7 %copy-start.9 = (s32[128]{0:T(128)S(1)}, s32[128]{0:T(128)}, u32[]{:S(2)}) copy-start(s32[128]{0:T(128)} %param.12) | copy-start | bytes 1540
  0.9 0.7 %copy-start.8 = (f32[1,1,64]{2,1,0:T(1,128)S(1)}, f32[1,1,64]{2,1,0:T(1,128)}, u32[]{:S(2)}) copy-start(f32[1,1,64]{2,1,0:T(1,128)} %param.10) | copy-start | bytes 772
  3.1 6.5 %collective-permute-start = (bf16[64,1152]{1,0:T(8,128)(2,1)S(1)}, bf16[64,1152]{1,0:T(8,128)(2,1)S(1)}, u32[]{:S(2)}, u32[]{:S(2)}) collective-permute-start(bf16[64,1152]{1,0:T(8,128)(2,1)S(1)} %concatenate.20), channel_id=1, source_target_pairs={{0,128},{1,129},{2,130},{3,131},{4,132},{5,133},{6,134},{7,135},{8... | collective-permute-start | bytes 442376 | tf_op jit(solution)/shard_map/ppermute | solution.py:96
  6.4 0.7 %copy-start.5 = (f32[26]{0:T(128)S(1)}, f32[26]{0:T(128)}, u32[]{:S(2)}) copy-start(f32[26]{0:T(128)} %constant.71) | copy-start | bytes 316
  6.4 0.7 %copy-start.6 = (pred[26]{0:T(512)(128)(4,1)S(1)}, pred[26]{0:T(512)(128)(4,1)}, u32[]{:S(2)}) copy-start(pred[26]{0:T(512)(128)(4,1)} %constant.70) | copy-start | bytes 82
  6.4 0.7 %copy-start.7 = (pred[26]{0:T(512)(128)(4,1)S(1)}, pred[26]{0:T(512)(128)(4,1)}, u32[]{:S(2)}) copy-start(pred[26]{0:T(512)(128)(4,1)} %constant.69) | copy-start | bytes 82
  7.3 0.7 %copy-start.4 = (f32[13,6]{0,1:T(8,128)S(1)}, f32[13,6]{0,1:T(8,128)}, u32[]{:S(2)}) copy-start(f32[13,6]{0,1:T(8,128)} %param.13) | copy-start | bytes 940
  9.0 0.7 %copy-start = (bf16[64,1152]{1,0:T(8,128)(2,1)}, bf16[64,1152]{1,0:T(8,128)(2,1)S(1)}, u32[]{:S(2)}) copy-start(bf16[64,1152]{1,0:T(8,128)(2,1)S(1)} %concatenate.19.p1_ref) | copy-start | bytes 442372
  9.6 0.7 %copy-start.1 = (bf16[64,1152]{1,0:T(8,128)(2,1)}, bf16[64,1152]{1,0:T(8,128)(2,1)S(1)}, u32[]{:S(2)}) copy-start(bf16[64,1152]{1,0:T(8,128)(2,1)S(1)} %collective-permute-done.p2_ref) | copy-start | bytes 442372
  10.3 8.1 %collective-permute-start.2 = (bf16[80,1152]{1,0:T(8,128)(2,1)S(1)}, bf16[80,1152]{1,0:T(8,128)(2,1)S(1)}, u32[]{:S(2)}, u32[]{:S(2)}) collective-permute-start(bf16[80,1152]{1,0:T(8,128)(2,1)S(1)} %pad_maximum_fusion.1), channel_id=1, source_target_pairs={{1,0},{2,1},{3,2},{4,3},{5,4},{6,5},{7,6},{8,7},{9,8},{10,9},{11,1... | collective-permute-start | bytes 552968 | tf_op jit(solution)/shard_map/ppermute | solution.py:103
  11.7 7.7 %collective-permute-start.1 = (bf16[80,1152]{1,0:T(8,128)(2,1)S(1)}, bf16[80,1152]{1,0:T(8,128)(2,1)S(1)}, u32[]{:S(2)}, u32[]{:S(2)}) collective-permute-start(bf16[80,1152]{1,0:T(8,128)(2,1)S(1)} %pad_maximum_fusion), channel_id=1, source_target_pairs={{0,1},{1,2},{2,3},{3,4},{4,5},{5,6},{6,7},{7,8},{8,9},{9,10},{10,1... | collective-permute-start | bytes 552968 | tf_op jit(solution)/shard_map/ppermute | solution.py:104
  18.4 2.0 %copy-start.2 = (bf16[80,1152]{1,0:T(8,128)(2,1)}, bf16[80,1152]{1,0:T(8,128)(2,1)S(1)}, u32[]{:S(2)}) copy-start(bf16[80,1152]{1,0:T(8,128)(2,1)S(1)} %collective-permute-done.2.p3_ref) | copy-start | bytes 552964
  19.3 1.0 %copy-start.3 = (bf16[80,1152]{1,0:T(8,128)(2,1)}, bf16[80,1152]{1,0:T(8,128)(2,1)S(1)}, u32[]{:S(2)}) copy-start(bf16[80,1152]{1,0:T(8,128)(2,1)S(1)} %collective-permute-done.1.p0_ref) | copy-start | bytes 552964

commit v13 on v12

--- a/solution.py
+++ b/solution.py
@@ -100,8 +100,14 @@
     rim = 16
     sent_up = jnp.concatenate([first_rows, second_rows[:rim]], axis=0)
     sent_down = jnp.concatenate([first_rows[rh - rim :], second_rows], axis=0)
-    from_below = lax.ppermute(sent_up, "ccd", [(b, b - 1) for b in range(1, nb)])
-    from_above = lax.ppermute(sent_down, "ccd", [(b, b + 1) for b in range(nb - 1)])
+    upward = [(b, b - 1) for b in range(1, nb)]
+    downward = [(b, b + 1) for b in range(nb - 1)]
+    mixed = [(x, y) for x, y in upward] + [(nb + x, nb + y) for x, y in downward]
+    mirrored = [(x, y) for x, y in downward] + [(nb + x, nb + y) for x, y in upward]
+    got_mixed = lax.ppermute(pick(sent_up, sent_down), axes, mixed)
+    got_mirrored = lax.ppermute(pick(sent_down, sent_up), axes, mirrored)
+    from_below = pick(got_mixed, got_mirrored)
+    from_above = pick(got_mirrored, got_mixed)
     lead = ROWS + 2 * HALF_K
     lead_pad = -(-lead // 16) * 16
     above = rh + rim
@@ -118,8 +124,8 @@
     inside = (out_rows >= 0) & (out_rows < total_rows)
     picks = jnp.where(inside, jnp.arange(lead) + origin - HALF_K + steps, -1)
     picks = jnp.pad(picks, (0, lead_pad - lead), constant_values=-1)[:, None]
-    pieces = (from_above, own, got_swap, from_below)
-    bases = ((0, 0), (above, above + rh), (above + rh, above), (above + 2 * rh, above + 2 * rh))
+    pieces = (got_mirrored, own, got_swap, got_mixed)
+    bases = ((0, above + 2 * rh), (above, above + rh), (above + rh, above), (above + 2 * rh, 0))
     span = 2 * STRIP
     both_taps = basis_taps(column_power + row_power, basis_sigma + basis_sigma)
     taps = jnp.pad(both_taps.astype(jnp.float32), ((0, 0), (0, span - KW)))

time: 62 us -> 59.9 us (0.966)
  waiting for transfers between devices: 3.3 us -> 1.69 us
    ppermute x2, waiting for transfers between devices: 3.29 us -> 1.69 us  [the longest x1 1.47 us: shards(): got_mixed = lax.ppermute(pick(sent_up, sent_down), axes, mixed)]
  transfers between devices with their start and end apart: 3 -> 3, of which waited for: 2 -> 2; matrix products, arithmetic and copies ran while one was open for 4% -> 3% of each run, Pallas kernels for 0% -> 0%
where the time goes in v13:
time: 59.9 us; the launch traced here: 59.6 us
  blocking collectives  30.5 us (51%)
  Pallas kernels  9.72 us (16%)
  starting transfers between devices  8.58 us (14%)
  local copies, waits for them, and re-layouts  5.57 us (9%)
  other arithmetic  3.41 us (6%)
  waiting for transfers between devices  1.69 us (3%)
    all_to_all x1, blocking collectives, shards(): lax.all_to_all(outgoing, 'ccd', split_axis=0, concat_axis=0, tiled=True)  30.5 us
    pallas_call x1, Pallas kernels, shards(): pl.pallas_call(match_kernel, grid=(strips,), in_specs=[pl.BlockSpec(memor...  9.72 us
    ppermute x1, starting transfers between devices, shards(): got_mixed = lax.ppermute(pick(sent_up, sent_down), axes, mixed)  4 us
    ppermute x1, starting transfers between devices, shards(): got_swap = lax.ppermute(other, axes, swap)  3.29 us
    unnamed x21, local copies, waits for them, and re-layouts  3.27 us
    ppermute x1, waiting for transfers between devices, shards(): got_mixed = lax.ppermute(pick(sent_up, sent_down), axes, mixed)  1.47 us
    squeeze x1, other arithmetic, shards(): ((raw_counts - overscan[..., None]) * response).astype(jnp.bfloat16)[0, 0]  1.31 us
    ppermute x1, starting transfers between devices, shards(): got_mirrored = lax.ppermute(pick(sent_down, sent_up), axes, mirrored)  1.29 us
  transfers between devices with their start and end apart: 3, of which 2 were waited for; matrix products, arithmetic and copies ran while one was open for 3% of the time, Pallas kernels for 0%

profile of v13, /device:TPU:1, one launch (start us, length us, event | category | flops | bytes accessed | tf_op | source)
XLA Modules:
  0.0 59.6 jit_solution(1220330352378178926)
XLA Ops:
  0.0 0.7 %copy-done.9 = s32[128]{0:T(128)S(1)} copy-done((s32[128]{0:T(128)S(1)}, s32[128]{0:T(128)}, u32[]{:S(2)}) %copy-start.9) | copy-done | bytes 536
  0.7 0.1 copy.14
  0.9 0.7 %copy-done.8 = f32[1,1,64]{2,1,0:T(1,128)S(1)} copy-done((f32[1,1,64]{2,1,0:T(1,128)S(1)}, f32[1,1,64]{2,1,0:T(1,128)}, u32[]{:S(2)}) %copy-start.8) | copy-done | bytes 280
  1.5 1.3 %fusion = bf16[64,2048]{1,0:T(8,128)(2,1)S(1)} fusion(f32[1,1,64,2048]{3,2,1,0:T(8,128)} %param.11, f32[1,1,64,2048]{3,2,1,0:T(8,128)} %param.9, f32[64]{0:T(128)S(1)} %bitcast.11), kind=kLoop, calls=%fused_computation.2 | loop fusion | flops 393216 | bytes 1310976 | tf_op jit(solution)/shard_map/squeeze | solution.py:80
  2.8 0.2 pad_dynamic-slice_fusion.1
  3.0 0.1 concatenate.20
  3.1 3.3 %collective-permute-start = (bf16[64,1152]{1,0:T(8,128)(2,1)S(1)}, bf16[64,1152]{1,0:T(8,128)(2,1)S(1)}, u32[]{:S(2)}, u32[]{:S(2)}) collective-permute-start(bf16[64,1152]{1,0:T(8,128)(2,1)S(1)} %concatenate.20), channel_id=1, source_target_pairs={{0,128},{1,129},{2,130},{3,131},{4,132},{5,133},{6,134},{7,135},{8... | collective-permute-start | bytes 442376 | tf_op jit(solution)/shard_map/ppermute | solution.py:96
  6.5 0.6 %copy-done.5 = pred[26]{0:T(512)(128)(4,1)S(1)} copy-done((pred[26]{0:T(512)(128)(4,1)S(1)}, pred[26]{0:T(512)(128)(4,1)}, u32[]{:S(2)}) %copy-start.5) | copy-done | bytes 50
  7.1 0.2 multiply_reduce_fusion
  7.6 0.6 copy-done.4
  8.4 0.6 %pad_convert_fusion.tap_ref = f32[26,256]{1,0:T(8,128)} fusion(bf16[26,21]{1,0:T(8,128)(2,1)S(1)} %divide_convert_fusion), kind=kLoop, calls=%fused_computation.15 | loop fusion | flops 6656 | bytes 27716 | tf_op jit(solution)/shard_map/jit(_pad)/pad | solution.py:131
  9.0 0.6 %copy-done.1 = bf16[64,1152]{1,0:T(8,128)(2,1)} copy-done((bf16[64,1152]{1,0:T(8,128)(2,1)}, bf16[64,1152]{1,0:T(8,128)(2,1)S(1)}, u32[]{:S(2)}) %copy-start.1) | copy-done | bytes 147480
  9.7 1.3 %collective-permute-start.1 = (bf16[80,1152]{1,0:T(8,128)(2,1)S(1)}, bf16[80,1152]{1,0:T(8,128)(2,1)S(1)}, u32[]{:S(2)}, u32[]{:S(2)}) collective-permute-start(bf16[80,1152]{1,0:T(8,128)(2,1)S(1)} %get-tuple-element.7), channel_id=1, source_target_pairs={{0,1},{1,2},{2,3},{3,4},{4,5},{5,6},{6,7},{7,8},{8,9},{9,10},{10,1... | collective-permute-start | bytes 552968 | tf_op jit(solution)/shard_map/ppermute | solution.py:108
  11.0 4.0 %collective-permute-start.2 = (bf16[80,1152]{1,0:T(8,128)(2,1)S(1)}, bf16[80,1152]{1,0:T(8,128)(2,1)S(1)}, u32[]{:S(2)}, u32[]{:S(2)}) collective-permute-start(bf16[80,1152]{1,0:T(8,128)(2,1)S(1)} %get-tuple-element.8), channel_id=1, source_target_pairs={{1,0},{2,1},{3,2},{4,3},{5,4},{6,5},{7,6},{8,7},{9,8},{10,9},{11,1... | collective-permute-start | bytes 552968 | tf_op jit(solution)/shard_map/ppermute | solution.py:107
  15.0 0.6 pad_maximum_fusion.2.kp_ref
  15.6 0.2 slice_reduce_fusion
  15.8 0.2 collective-permute-done.1.p0_ref
  16.0 1.5 %collective-permute-done.2.p3_ref = bf16[80,1152]{1,0:T(8,128)(2,1)S(1)} collective-permute-done((bf16[80,1152]{1,0:T(8,128)(2,1)S(1)}, bf16[80,1152]{1,0:T(8,128)(2,1)S(1)}, u32[]{:S(2)}, u32[]{:S(2)}) %collective-permute-start.2) | collective-permute-done | bytes 184352 | tf_op jit(solution)/shard_map/ppermute | solution.py:107
  17.5 0.2 fusion.3
  17.8 0.8 %copy.16.picks_ref = s32[160,1]{1,0:T(8,128)} copy(s32[160,1]{0,1:T(1,128)S(1)} %bitcast.10) | data formatting | bytes 1280 | tf_op jit(solution)/shard_map/broadcast_in_dim | solution.py:126
  18.5 9.7 %shard_map.91 = bf16[128,8,128]{2,1,0:T(8,128)(2,1)} custom-call(f32[80]{0:T(128)} %pad_maximum_fusion.2.kp_ref, s32[160,1]{1,0:T(8,128)} %copy.16.picks_ref, bf16[80,1152]{1,0:T(8,128)(2,1)} %copy-done.2, bf16[64,1152]{1,0:T(8,128)(2,1)} %copy-done, bf16[64,1152]{1,0:T(8,128)(2,1)} %copy-done.1, bf16[80,1152]{1,0:T(8,128)(2,1)} %copy-done.3, ...), custom_call_target="tpu_custom_call" | custom-call | tf_op jit(solution)/shard_map/pallas_call | solution.py:216
  28.3 30.5 %all_to_all.5 = bf16[128,8,128]{2,1,0:T(8,128)(2,1)S(1)} all-to-all(bf16[128,8,128]{2,1,0:T(8,128)(2,1)} %shard_map.91), channel_id=1, replica_groups=mesh['section'=2,'ccd'=128] {'ccd'}, dimensions={0} | all-to-all | bytes 524288 | tf_op jit(solution)/shard_map/all_to_all | solution.py:234
  58.8 0.1 convert_reduce_fusion
  58.9 0.7 %reshape_broadcast_in_dim.3 = f32[1,1,32,32]{3,2,1,0:T(8,128)} reshape(f32[8,128]{1,0:T(8,128)S(1)} %convert_reduce_fusion) | data formatting | bytes 8192 | tf_op jit(solution)/shard_map/reshape;broadcast_in_dim | solution.py:236
  (33 shorter events, 0.8 us)
Async XLA Ops:
  0.0 0.7 %copy-start.9 = (s32[128]{0:T(128)S(1)}, s32[128]{0:T(128)}, u32[]{:S(2)}) copy-start(s32[128]{0:T(128)} %param.12) | copy-start | bytes 1540
  0.9 0.7 %copy-start.8 = (f32[1,1,64]{2,1,0:T(1,128)S(1)}, f32[1,1,64]{2,1,0:T(1,128)}, u32[]{:S(2)}) copy-start(f32[1,1,64]{2,1,0:T(1,128)} %param.10) | copy-start | bytes 772
  3.1 5.9 %collective-permute-start = (bf16[64,1152]{1,0:T(8,128)(2,1)S(1)}, bf16[64,1152]{1,0:T(8,128)(2,1)S(1)}, u32[]{:S(2)}, u32[]{:S(2)}) collective-permute-start(bf16[64,1152]{1,0:T(8,128)(2,1)S(1)} %concatenate.20), channel_id=1, source_target_pairs={{0,128},{1,129},{2,130},{3,131},{4,132},{5,133},{6,134},{7,135},{8... | collective-permute-start | bytes 442376 | tf_op jit(solution)/shard_map/ppermute | solution.py:96
  6.4 0.7 %copy-start.5 = (pred[26]{0:T(512)(128)(4,1)S(1)}, pred[26]{0:T(512)(128)(4,1)}, u32[]{:S(2)}) copy-start(pred[26]{0:T(512)(128)(4,1)} %constant.69) | copy-start | bytes 82
  6.4 0.7 %copy-start.6 = (pred[26]{0:T(512)(128)(4,1)S(1)}, pred[26]{0:T(512)(128)(4,1)}, u32[]{:S(2)}) copy-start(pred[26]{0:T(512)(128)(4,1)} %constant.70) | copy-start | bytes 82
  6.4 0.7 %copy-start.7 = (f32[26]{0:T(128)S(1)}, f32[26]{0:T(128)}, u32[]{:S(2)}) copy-start(f32[26]{0:T(128)} %constant.71) | copy-start | bytes 316
  7.5 0.7 %copy-start.4 = (f32[13,6]{0,1:T(8,128)S(1)}, f32[13,6]{0,1:T(8,128)}, u32[]{:S(2)}) copy-start(f32[13,6]{0,1:T(8,128)} %param.13) | copy-start | bytes 940
  7.6 1.4 %copy-start = (bf16[64,1152]{1,0:T(8,128)(2,1)}, bf16[64,1152]{1,0:T(8,128)(2,1)S(1)}, u32[]{:S(2)}) copy-start(bf16[64,1152]{1,0:T(8,128)(2,1)S(1)} %concatenate.19.p1_ref) | copy-start | bytes 442372
  9.0 0.7 %copy-start.1 = (bf16[64,1152]{1,0:T(8,128)(2,1)}, bf16[64,1152]{1,0:T(8,128)(2,1)S(1)}, u32[]{:S(2)}) copy-start(bf16[64,1152]{1,0:T(8,128)(2,1)S(1)} %collective-permute-done.p2_ref) | copy-start | bytes 442372
  9.7 6.3 %collective-permute-start.1 = (bf16[80,1152]{1,0:T(8,128)(2,1)S(1)}, bf16[80,1152]{1,0:T(8,128)(2,1)S(1)}, u32[]{:S(2)}, u32[]{:S(2)}) collective-permute-start(bf16[80,1152]{1,0:T(8,128)(2,1)S(1)} %get-tuple-element.7), channel_id=1, source_target_pairs={{0,1},{1,2},{2,3},{3,4},{4,5},{5,6},{6,7},{7,8},{8,9},{9,10},{10,1... | collective-permute-start | bytes 552968 | tf_op jit(solution)/shard_map/ppermute | solution.py:108
  11.0 6.5 %collective-permute-start.2 = (bf16[80,1152]{1,0:T(8,128)(2,1)S(1)}, bf16[80,1152]{1,0:T(8,128)(2,1)S(1)}, u32[]{:S(2)}, u32[]{:S(2)}) collective-permute-start(bf16[80,1152]{1,0:T(8,128)(2,1)S(1)} %get-tuple-element.8), channel_id=1, source_target_pairs={{1,0},{2,1},{3,2},{4,3},{5,4},{6,5},{7,6},{8,7},{9,8},{10,9},{11,1... | collective-permute-start | bytes 552968 | tf_op jit(solution)/shard_map/ppermute | solution.py:107
  16.0 2.5 %copy-start.2 = (bf16[80,1152]{1,0:T(8,128)(2,1)}, bf16[80,1152]{1,0:T(8,128)(2,1)S(1)}, u32[]{:S(2)}) copy-start(bf16[80,1152]{1,0:T(8,128)(2,1)S(1)} %collective-permute-done.1.p0_ref) | copy-start | bytes 552964
  17.5 1.0 %copy-start.3 = (bf16[80,1152]{1,0:T(8,128)(2,1)}, bf16[80,1152]{1,0:T(8,128)(2,1)S(1)}, u32[]{:S(2)}) copy-start(bf16[80,1152]{1,0:T(8,128)(2,1)S(1)} %collective-permute-done.2.p3_ref) | copy-start | bytes 552964

commit v14 on v13

--- a/solution.py
+++ b/solution.py
@@ -123,7 +123,7 @@
     out_rows = top_row - HALF_K + jnp.arange(lead)
     inside = (out_rows >= 0) & (out_rows < total_rows)
     picks = jnp.where(inside, jnp.arange(lead) + origin - HALF_K + steps, -1)
-    picks = jnp.pad(picks, (0, lead_pad - lead), constant_values=-1)[:, None]
+    picks = jnp.pad(picks, (0, lead_pad - lead), constant_values=-1)[None, :]
     pieces = (got_mirrored, own, got_swap, got_mixed)
     bases = ((0, above + 2 * rh), (above, above + rh), (above + rh, above), (above + 2 * rh, 0))
     span = 2 * STRIP
@@ -153,9 +153,10 @@
             for ref, (b0, b1) in zip(piece_refs, bases):
                 n = ref.shape[0]
                 base = jnp.where(first, b0, b1)
-                hit = lax.broadcasted_iota(jnp.int32, (lead_pad, n), 1) + base == picks_ref[...]
-                gathered = gathered + jnp.dot(
-                    hit.astype(jnp.bfloat16), ref[...], preferred_element_type=jnp.float32
+                hit = lax.broadcasted_iota(jnp.int32, (n, lead_pad), 0) + base == picks_ref[...]
+                gathered = gathered + lax.dot_general(
+                    hit.astype(jnp.bfloat16), ref[...], (((0,), (0,)), ((), ())),
+                    preferred_element_type=jnp.float32,
                 )
             img_ref[...] = gathered.astype(jnp.bfloat16)
             for k in range(NBASIS):

time: 59.9 us -> 59.8 us (level)
    broadcast_in_dim x1 -> x0, local copies, waits for them, and re-layouts: 0.76 us -> none  [shards(): picks = jnp.pad(picks, (0, lead_pad - lead), constant_values=-1)[:, None]]
where the time goes in v14:
time: 59.8 us; the launch traced here: 59.5 us
  blocking collectives  30.5 us (51%)
  Pallas kernels  9.8 us (16%)
  starting transfers between devices  8.58 us (14%)
  local copies, waits for them, and re-layouts  5.38 us (9%)
  other arithmetic  3.41 us (6%)
  waiting for transfers between devices  1.69 us (3%)
    all_to_all x1, blocking collectives, shards(): lax.all_to_all(outgoing, 'ccd', split_axis=0, concat_axis=0, tiled=True)  30.5 us
    pallas_call x1, Pallas kernels, shards(): pl.pallas_call(match_kernel, grid=(strips,), in_specs=[pl.BlockSpec(memor...  9.8 us
    ppermute x1, starting transfers between devices, shards(): got_mixed = lax.ppermute(pick(sent_up, sent_down), axes, mixed)  4 us
    ppermute x1, starting transfers between devices, shards(): got_swap = lax.ppermute(other, axes, swap)  3.29 us
    unnamed x21, local copies, waits for them, and re-layouts  3.27 us
    ppermute x1, waiting for transfers between devices, shards(): got_mixed = lax.ppermute(pick(sent_up, sent_down), axes, mixed)  1.47 us
    squeeze x1, other arithmetic, shards(): ((raw_counts - overscan[..., None]) * response).astype(jnp.bfloat16)[0, 0]  1.31 us
    ppermute x1, starting transfers between devices, shards(): got_mirrored = lax.ppermute(pick(sent_down, sent_up), axes, mirrored)  1.29 us
  transfers between devices with their start and end apart: 3, of which 2 were waited for; matrix products, arithmetic and copies ran while one was open for 3% of the time, Pallas kernels for 0%

profile of v14, /device:TPU:1, one launch (start us, length us, event | category | flops | bytes accessed | tf_op | source)
XLA Modules:
  0.0 59.5 jit_solution(8203294043303953701)
XLA Ops:
  0.0 0.7 %copy-done.9 = s32[128]{0:T(128)S(1)} copy-done((s32[128]{0:T(128)S(1)}, s32[128]{0:T(128)}, u32[]{:S(2)}) %copy-start.9) | copy-done | bytes 536
  0.7 0.1 copy.14
  0.9 0.7 %copy-done.8 = f32[1,1,64]{2,1,0:T(1,128)S(1)} copy-done((f32[1,1,64]{2,1,0:T(1,128)S(1)}, f32[1,1,64]{2,1,0:T(1,128)}, u32[]{:S(2)}) %copy-start.8) | copy-done | bytes 280
  1.5 1.3 %fusion = bf16[64,2048]{1,0:T(8,128)(2,1)S(1)} fusion(f32[1,1,64,2048]{3,2,1,0:T(8,128)} %param.11, f32[1,1,64,2048]{3,2,1,0:T(8,128)} %param.9, f32[64]{0:T(128)S(1)} %bitcast.13), kind=kLoop, calls=%fused_computation.2 | loop fusion | flops 393216 | bytes 1310976 | tf_op jit(solution)/shard_map/squeeze | solution.py:80
  2.8 0.2 pad_dynamic-slice_fusion.1
  3.0 0.1 concatenate.20
  3.1 3.3 %collective-permute-start = (bf16[64,1152]{1,0:T(8,128)(2,1)S(1)}, bf16[64,1152]{1,0:T(8,128)(2,1)S(1)}, u32[]{:S(2)}, u32[]{:S(2)}) collective-permute-start(bf16[64,1152]{1,0:T(8,128)(2,1)S(1)} %concatenate.20), channel_id=1, source_target_pairs={{0,128},{1,129},{2,130},{3,131},{4,132},{5,133},{6,134},{7,135},{8... | collective-permute-start | bytes 442376 | tf_op jit(solution)/shard_map/ppermute | solution.py:96
  6.5 0.6 %copy-done.5 = pred[26]{0:T(512)(128)(4,1)S(1)} copy-done((pred[26]{0:T(512)(128)(4,1)S(1)}, pred[26]{0:T(512)(128)(4,1)}, u32[]{:S(2)}) %copy-start.5) | copy-done | bytes 50
  7.1 0.2 multiply_reduce_fusion
  7.6 0.6 copy-done.4
  8.4 0.6 %pad_convert_fusion.tap_ref = f32[26,256]{1,0:T(8,128)} fusion(bf16[26,21]{1,0:T(8,128)(2,1)S(1)} %divide_convert_fusion), kind=kLoop, calls=%fused_computation.15 | loop fusion | flops 6656 | bytes 27716 | tf_op jit(solution)/shard_map/jit(_pad)/pad | solution.py:131
  9.0 0.6 %copy-done.1 = bf16[64,1152]{1,0:T(8,128)(2,1)} copy-done((bf16[64,1152]{1,0:T(8,128)(2,1)}, bf16[64,1152]{1,0:T(8,128)(2,1)S(1)}, u32[]{:S(2)}) %copy-start.1) | copy-done | bytes 147480
  9.7 1.3 %collective-permute-start.1 = (bf16[80,1152]{1,0:T(8,128)(2,1)S(1)}, bf16[80,1152]{1,0:T(8,128)(2,1)S(1)}, u32[]{:S(2)}, u32[]{:S(2)}) collective-permute-start(bf16[80,1152]{1,0:T(8,128)(2,1)S(1)} %get-tuple-element.7), channel_id=1, source_target_pairs={{0,1},{1,2},{2,3},{3,4},{4,5},{5,6},{6,7},{7,8},{8,9},{9,10},{10,1... | collective-permute-start | bytes 552968 | tf_op jit(solution)/shard_map/ppermute | solution.py:108
  11.0 4.0 %collective-permute-start.2 = (bf16[80,1152]{1,0:T(8,128)(2,1)S(1)}, bf16[80,1152]{1,0:T(8,128)(2,1)S(1)}, u32[]{:S(2)}, u32[]{:S(2)}) collective-permute-start(bf16[80,1152]{1,0:T(8,128)(2,1)S(1)} %get-tuple-element.8), channel_id=1, source_target_pairs={{1,0},{2,1},{3,2},{4,3},{5,4},{6,5},{7,6},{8,7},{9,8},{10,9},{11,1... | collective-permute-start | bytes 552968 | tf_op jit(solution)/shard_map/ppermute | solution.py:107
  15.0 0.6 pad_maximum_fusion.2.kp_ref
  15.6 0.2 slice_reduce_fusion
  15.8 0.2 collective-permute-done.1.p0_ref
  16.0 1.5 %collective-permute-done.2.p3_ref = bf16[80,1152]{1,0:T(8,128)(2,1)S(1)} collective-permute-done((bf16[80,1152]{1,0:T(8,128)(2,1)S(1)}, bf16[80,1152]{1,0:T(8,128)(2,1)S(1)}, u32[]{:S(2)}, u32[]{:S(2)}) %collective-permute-start.2) | collective-permute-done | bytes 184352 | tf_op jit(solution)/shard_map/ppermute | solution.py:107
  17.5 0.2 fusion.3
  17.8 0.6 pad.15
  18.4 9.8 %shard_map.91 = bf16[128,8,128]{2,1,0:T(8,128)(2,1)} custom-call(f32[80]{0:T(128)} %pad_maximum_fusion.2.kp_ref, s32[1,160]{1,0:T(1,128)} %bitcast.10, bf16[80,1152]{1,0:T(8,128)(2,1)} %copy-done.2, bf16[64,1152]{1,0:T(8,128)(2,1)} %copy-done, bf16[64,1152]{1,0:T(8,128)(2,1)} %copy-done.1, bf16[80,1152]{1,0:T(8,128)(2,1)} %copy-done.3, ...), custom_call_target="tpu_custom_call" | custom-call | tf_op jit(solution)/shard_map/pallas_call | solution.py:217
  28.2 30.5 %all_to_all.5 = bf16[128,8,128]{2,1,0:T(8,128)(2,1)S(1)} all-to-all(bf16[128,8,128]{2,1,0:T(8,128)(2,1)} %shard_map.91), channel_id=1, replica_groups=mesh['section'=2,'ccd'=128] {'ccd'}, dimensions={0} | all-to-all | bytes 524288 | tf_op jit(solution)/shard_map/all_to_all | solution.py:235
  58.7 0.1 convert_reduce_fusion
  58.8 0.7 %reshape_broadcast_in_dim.3 = f32[1,1,32,32]{3,2,1,0:T(8,128)} reshape(f32[8,128]{1,0:T(8,128)S(1)} %convert_reduce_fusion) | data formatting | bytes 8192 | tf_op jit(solution)/shard_map/reshape;broadcast_in_dim | solution.py:237
  (32 shorter events, 0.8 us)
Async XLA Ops:
  0.0 0.7 %copy-start.9 = (s32[128]{0:T(128)S(1)}, s32[128]{0:T(128)}, u32[]{:S(2)}) copy-start(s32[128]{0:T(128)} %param.12) | copy-start | bytes 1540
  0.9 0.7 %copy-start.8 = (f32[1,1,64]{2,1,0:T(1,128)S(1)}, f32[1,1,64]{2,1,0:T(1,128)}, u32[]{:S(2)}) copy-start(f32[1,1,64]{2,1,0:T(1,128)} %param.10) | copy-start | bytes 772
  3.1 5.9 %collective-permute-start = (bf16[64,1152]{1,0:T(8,128)(2,1)S(1)}, bf16[64,1152]{1,0:T(8,128)(2,1)S(1)}, u32[]{:S(2)}, u32[]{:S(2)}) collective-permute-start(bf16[64,1152]{1,0:T(8,128)(2,1)S(1)} %concatenate.20), channel_id=1, source_target_pairs={{0,128},{1,129},{2,130},{3,131},{4,132},{5,133},{6,134},{7,135},{8... | collective-permute-start | bytes 442376 | tf_op jit(solution)/shard_map/ppermute | solution.py:96
  6.4 0.7 %copy-start.5 = (pred[26]{0:T(512)(128)(4,1)S(1)}, pred[26]{0:T(512)(128)(4,1)}, u32[]{:S(2)}) copy-start(pred[26]{0:T(512)(128)(4,1)} %constant.69) | copy-start | bytes 82
  6.4 0.7 %copy-start.6 = (pred[26]{0:T(512)(128)(4,1)S(1)}, pred[26]{0:T(512)(128)(4,1)}, u32[]{:S(2)}) copy-start(pred[26]{0:T(512)(128)(4,1)} %constant.70) | copy-start | bytes 82
  6.4 0.7 %copy-start.7 = (f32[26]{0:T(128)S(1)}, f32[26]{0:T(128)}, u32[]{:S(2)}) copy-start(f32[26]{0:T(128)} %constant.71) | copy-start | bytes 316
  7.5 0.7 %copy-start.4 = (f32[13,6]{0,1:T(8,128)S(1)}, f32[13,6]{0,1:T(8,128)}, u32[]{:S(2)}) copy-start(f32[13,6]{0,1:T(8,128)} %param.13) | copy-start | bytes 940
  7.6 1.4 %copy-start = (bf16[64,1152]{1,0:T(8,128)(2,1)}, bf16[64,1152]{1,0:T(8,128)(2,1)S(1)}, u32[]{:S(2)}) copy-start(bf16[64,1152]{1,0:T(8,128)(2,1)S(1)} %concatenate.19.p1_ref) | copy-start | bytes 442372
  9.0 0.7 %copy-start.1 = (bf16[64,1152]{1,0:T(8,128)(2,1)}, bf16[64,1152]{1,0:T(8,128)(2,1)S(1)}, u32[]{:S(2)}) copy-start(bf16[64,1152]{1,0:T(8,128)(2,1)S(1)} %collective-permute-done.p2_ref) | copy-start | bytes 442372
  9.7 6.3 %collective-permute-start.1 = (bf16[80,1152]{1,0:T(8,128)(2,1)S(1)}, bf16[80,1152]{1,0:T(8,128)(2,1)S(1)}, u32[]{:S(2)}, u32[]{:S(2)}) collective-permute-start(bf16[80,1152]{1,0:T(8,128)(2,1)S(1)} %get-tuple-element.7), channel_id=1, source_target_pairs={{0,1},{1,2},{2,3},{3,4},{4,5},{5,6},{6,7},{7,8},{8,9},{9,10},{10,1... | collective-permute-start | bytes 552968 | tf_op jit(solution)/shard_map/ppermute | solution.py:108
  11.0 6.5 %collective-permute-start.2 = (bf16[80,1152]{1,0:T(8,128)(2,1)S(1)}, bf16[80,1152]{1,0:T(8,128)(2,1)S(1)}, u32[]{:S(2)}, u32[]{:S(2)}) collective-permute-start(bf16[80,1152]{1,0:T(8,128)(2,1)S(1)} %get-tuple-element.8), channel_id=1, source_target_pairs={{1,0},{2,1},{3,2},{4,3},{5,4},{6,5},{7,6},{8,7},{9,8},{10,9},{11,1... | collective-permute-start | bytes 552968 | tf_op jit(solution)/shard_map/ppermute | solution.py:107
  16.0 2.3 %copy-start.2 = (bf16[80,1152]{1,0:T(8,128)(2,1)}, bf16[80,1152]{1,0:T(8,128)(2,1)S(1)}, u32[]{:S(2)}) copy-start(bf16[80,1152]{1,0:T(8,128)(2,1)S(1)} %collective-permute-done.1.p0_ref) | copy-start | bytes 552964
  17.5 0.9 %copy-start.3 = (bf16[80,1152]{1,0:T(8,128)(2,1)}, bf16[80,1152]{1,0:T(8,128)(2,1)S(1)}, u32[]{:S(2)}) copy-start(bf16[80,1152]{1,0:T(8,128)(2,1)S(1)} %collective-permute-done.2.p3_ref) | copy-start | bytes 552964

commit v15 on v14

--- a/solution.py
+++ b/solution.py
@@ -221,7 +221,7 @@
         + [full(x.shape) for x in pieces]
         + [full(taps.shape), full(owners.shape), full(weights.shape)],
         out_specs=full((band_count, groups, STRIP)),
-        out_shape=jax.ShapeDtypeStruct((band_count, groups, STRIP), jnp.bfloat16),
+        out_shape=jax.ShapeDtypeStruct((band_count, groups, STRIP), jnp.float32),
         scratch_shapes=[
             pltpu.VMEM((ROWS, STRIP), jnp.float32),
             pltpu.VMEM((tiles * groups, STRIP), jnp.float32),

time: 59.8 us -> 65.3 us (1.092)
  blocking collectives: 30.5 us -> 36.2 us
    all_to_all x1, blocking collectives: 30.5 us -> 36.2 us  [shards(): lax.all_to_all(outgoing, 'ccd', split_axis=0, concat_axis=0, tiled=True)]
where the time goes in v15:
time: 65.3 us; the launch traced here: 65 us
  blocking collectives  36.2 us (55%)
  Pallas kernels  9.51 us (15%)
  starting transfers between devices  8.58 us (13%)
  local copies, waits for them, and re-layouts  5.4 us (8%)
  other arithmetic  3.45 us (5%)
  waiting for transfers between devices  1.7 us (3%)
    all_to_all x1, blocking collectives, shards(): lax.all_to_all(outgoing, 'ccd', split_axis=0, concat_axis=0, tiled=True)  36.2 us
    pallas_call x1, Pallas kernels, shards(): pl.pallas_call(match_kernel, grid=(strips,), in_specs=[pl.BlockSpec(memor...  9.51 us
    ppermute x1, starting transfers between devices, shards(): got_mixed = lax.ppermute(pick(sent_up, sent_down), axes, mixed)  4 us
    unnamed x21, local copies, waits for them, and re-layouts  3.29 us
    ppermute x1, starting transfers between devices, shards(): got_swap = lax.ppermute(other, axes, swap)  3.29 us
    ppermute x1, waiting for transfers between devices, shards(): got_mixed = lax.ppermute(pick(sent_up, sent_down), axes, mixed)  1.47 us
    squeeze x1, other arithmetic, shards(): ((raw_counts - overscan[..., None]) * response).astype(jnp.bfloat16)[0, 0]  1.31 us
  transfers between devices with their start and end apart: 3, of which 2 were waited for; matrix products, arithmetic and copies ran while one was open for 3% of the time, Pallas kernels for 0%

profile of v15, /device:TPU:1, one launch (start us, length us, event | category | flops | bytes accessed | tf_op | source)
XLA Modules:
  0.0 65.0 jit_solution(5479977762499026416)
XLA Ops:
  0.0 0.7 %copy-done.9 = s32[128]{0:T(128)S(1)} copy-done((s32[128]{0:T(128)S(1)}, s32[128]{0:T(128)}, u32[]{:S(2)}) %copy-start.9) | copy-done | bytes 536
  0.7 0.1 copy.14
  0.9 0.7 %copy-done.8 = f32[1,1,64]{2,1,0:T(1,128)S(1)} copy-done((f32[1,1,64]{2,1,0:T(1,128)S(1)}, f32[1,1,64]{2,1,0:T(1,128)}, u32[]{:S(2)}) %copy-start.8) | copy-done | bytes 280
  1.5 1.3 %fusion = bf16[64,2048]{1,0:T(8,128)(2,1)S(1)} fusion(f32[1,1,64,2048]{3,2,1,0:T(8,128)} %param.11, f32[1,1,64,2048]{3,2,1,0:T(8,128)} %param.9, f32[64]{0:T(128)S(1)} %bitcast.11), kind=kLoop, calls=%fused_computation.1 | loop fusion | flops 393216 | bytes 1310976 | tf_op jit(solution)/shard_map/squeeze | solution.py:80
  2.8 0.2 pad_dynamic-slice_fusion.1
  3.0 0.1 concatenate.20
  3.1 3.3 %collective-permute-start = (bf16[64,1152]{1,0:T(8,128)(2,1)S(1)}, bf16[64,1152]{1,0:T(8,128)(2,1)S(1)}, u32[]{:S(2)}, u32[]{:S(2)}) collective-permute-start(bf16[64,1152]{1,0:T(8,128)(2,1)S(1)} %concatenate.20), channel_id=1, source_target_pairs={{0,128},{1,129},{2,130},{3,131},{4,132},{5,133},{6,134},{7,135},{8... | collective-permute-start | bytes 442376 | tf_op jit(solution)/shard_map/ppermute | solution.py:96
  6.5 0.6 copy-done.5
  7.1 0.2 multiply_reduce_fusion
  7.5 0.6 copy-done.4
  8.4 0.7 %pad_convert_fusion.tap_ref = f32[26,256]{1,0:T(8,128)} fusion(bf16[26,21]{1,0:T(8,128)(2,1)S(1)} %divide_convert_fusion), kind=kLoop, calls=%fused_computation.14 | loop fusion | flops 6656 | bytes 27716 | tf_op jit(solution)/shard_map/jit(_pad)/pad | solution.py:131
  9.1 0.6 copy-done.1
  9.8 1.3 %collective-permute-start.1 = (bf16[80,1152]{1,0:T(8,128)(2,1)S(1)}, bf16[80,1152]{1,0:T(8,128)(2,1)S(1)}, u32[]{:S(2)}, u32[]{:S(2)}) collective-permute-start(bf16[80,1152]{1,0:T(8,128)(2,1)S(1)} %get-tuple-element.7), channel_id=1, source_target_pairs={{0,1},{1,2},{2,3},{3,4},{4,5},{5,6},{6,7},{7,8},{8,9},{9,10},{10,1... | collective-permute-start | bytes 552968 | tf_op jit(solution)/shard_map/ppermute | solution.py:108
  11.1 4.0 %collective-permute-start.2 = (bf16[80,1152]{1,0:T(8,128)(2,1)S(1)}, bf16[80,1152]{1,0:T(8,128)(2,1)S(1)}, u32[]{:S(2)}, u32[]{:S(2)}) collective-permute-start(bf16[80,1152]{1,0:T(8,128)(2,1)S(1)} %get-tuple-element.8), channel_id=1, source_target_pairs={{1,0},{2,1},{3,2},{4,3},{5,4},{6,5},{7,6},{8,7},{9,8},{10,9},{11,1... | collective-permute-start | bytes 552968 | tf_op jit(solution)/shard_map/ppermute | solution.py:107
  15.1 0.6 pad_maximum_fusion.2.kp_ref
  15.7 0.2 slice_reduce_fusion
  15.9 0.2 collective-permute-done.1.p0_ref
  16.1 1.5 %collective-permute-done.2.p3_ref = bf16[80,1152]{1,0:T(8,128)(2,1)S(1)} collective-permute-done((bf16[80,1152]{1,0:T(8,128)(2,1)S(1)}, bf16[80,1152]{1,0:T(8,128)(2,1)S(1)}, u32[]{:S(2)}, u32[]{:S(2)}) %collective-permute-start.2) | collective-permute-done | bytes 184352 | tf_op jit(solution)/shard_map/ppermute | solution.py:107
  17.6 0.2 fusion.3
  17.9 0.6 pad.15
  18.4 9.5 %shard_map.91 = f32[128,8,128]{2,1,0:T(8,128)} custom-call(f32[80]{0:T(128)} %pad_maximum_fusion.2.kp_ref, s32[1,160]{1,0:T(1,128)} %bitcast.10, bf16[80,1152]{1,0:T(8,128)(2,1)} %copy-done.2, bf16[64,1152]{1,0:T(8,128)(2,1)} %copy-done, bf16[64,1152]{1,0:T(8,128)(2,1)} %copy-done.1, bf16[80,1152]{1,0:T(8,128)(2,1)} %copy-done.3, ...), custom_call_target="tpu_custom_call" | custom-call | tf_op jit(solution)/shard_map/pallas_call | solution.py:217
  27.9 36.2 %all_to_all.5 = f32[128,8,128]{2,1,0:T(8,128)S(1)} all-to-all(f32[128,8,128]{2,1,0:T(8,128)} %shard_map.91), channel_id=1, replica_groups=mesh['section'=2,'ccd'=128] {'ccd'}, dimensions={0} | all-to-all | bytes 1048576 | tf_op jit(solution)/shard_map/all_to_all | solution.py:235
  64.2 0.1 reduce_sum.19
  64.3 0.7 %reshape_broadcast_in_dim.3 = f32[1,1,32,32]{3,2,1,0:T(8,128)} reshape(f32[8,128]{1,0:T(8,128)S(1)} %reduce_sum.19) | data formatting | bytes 8192 | tf_op jit(solution)/shard_map/reshape;broadcast_in_dim | solution.py:237
  (32 shorter events, 0.8 us)
Async XLA Ops:
  0.0 0.7 %copy-start.9 = (s32[128]{0:T(128)S(1)}, s32[128]{0:T(128)}, u32[]{:S(2)}) copy-start(s32[128]{0:T(128)} %param.12) | copy-start | bytes 1540
  0.9 0.7 %copy-start.8 = (f32[1,1,64]{2,1,0:T(1,128)S(1)}, f32[1,1,64]{2,1,0:T(1,128)}, u32[]{:S(2)}) copy-start(f32[1,1,64]{2,1,0:T(1,128)} %param.10) | copy-start | bytes 772
  3.1 6.0 %collective-permute-start = (bf16[64,1152]{1,0:T(8,128)(2,1)S(1)}, bf16[64,1152]{1,0:T(8,128)(2,1)S(1)}, u32[]{:S(2)}, u32[]{:S(2)}) collective-permute-start(bf16[64,1152]{1,0:T(8,128)(2,1)S(1)} %concatenate.20), channel_id=1, source_target_pairs={{0,128},{1,129},{2,130},{3,131},{4,132},{5,133},{6,134},{7,135},{8... | collective-permute-start | bytes 442376 | tf_op jit(solution)/shard_map/ppermute | solution.py:96
  6.4 0.7 %copy-start.5 = (f32[26]{0:T(128)S(1)}, f32[26]{0:T(128)}, u32[]{:S(2)}) copy-start(f32[26]{0:T(128)} %constant.71) | copy-start | bytes 316
  6.4 0.7 %copy-start.6 = (pred[26]{0:T(512)(128)(4,1)S(1)}, pred[26]{0:T(512)(128)(4,1)}, u32[]{:S(2)}) copy-start(pred[26]{0:T(512)(128)(4,1)} %constant.70) | copy-start | bytes 82
  6.4 0.7 %copy-start.7 = (pred[26]{0:T(512)(128)(4,1)S(1)}, pred[26]{0:T(512)(128)(4,1)}, u32[]{:S(2)}) copy-start(pred[26]{0:T(512)(128)(4,1)} %constant.69) | copy-start | bytes 82
  7.4 0.7 %copy-start.4 = (f32[13,6]{0,1:T(8,128)S(1)}, f32[13,6]{0,1:T(8,128)}, u32[]{:S(2)}) copy-start(f32[13,6]{0,1:T(8,128)} %param.13) | copy-start | bytes 940
  8.4 0.7 %copy-start = (bf16[64,1152]{1,0:T(8,128)(2,1)}, bf16[64,1152]{1,0:T(8,128)(2,1)S(1)}, u32[]{:S(2)}) copy-start(bf16[64,1152]{1,0:T(8,128)(2,1)S(1)} %concatenate.19.p1_ref) | copy-start | bytes 442372
  9.1 0.7 %copy-start.1 = (bf16[64,1152]{1,0:T(8,128)(2,1)}, bf16[64,1152]{1,0:T(8,128)(2,1)S(1)}, u32[]{:S(2)}) copy-start(bf16[64,1152]{1,0:T(8,128)(2,1)S(1)} %collective-permute-done.p2_ref) | copy-start | bytes 442372
  9.8 6.3 %collective-permute-start.1 = (bf16[80,1152]{1,0:T(8,128)(2,1)S(1)}, bf16[80,1152]{1,0:T(8,128)(2,1)S(1)}, u32[]{:S(2)}, u32[]{:S(2)}) collective-permute-start(bf16[80,1152]{1,0:T(8,128)(2,1)S(1)} %get-tuple-element.7), channel_id=1, source_target_pairs={{0,1},{1,2},{2,3},{3,4},{4,5},{5,6},{6,7},{7,8},{8,9},{9,10},{10,1... | collective-permute-start | bytes 552968 | tf_op jit(solution)/shard_map/ppermute | solution.py:108
  11.1 6.5 %collective-permute-start.2 = (bf16[80,1152]{1,0:T(8,128)(2,1)S(1)}, bf16[80,1152]{1,0:T(8,128)(2,1)S(1)}, u32[]{:S(2)}, u32[]{:S(2)}) collective-permute-start(bf16[80,1152]{1,0:T(8,128)(2,1)S(1)} %get-tuple-element.8), channel_id=1, source_target_pairs={{1,0},{2,1},{3,2},{4,3},{5,4},{6,5},{7,6},{8,7},{9,8},{10,9},{11,1... | collective-permute-start | bytes 552968 | tf_op jit(solution)/shard_map/ppermute | solution.py:107
  16.1 2.3 %copy-start.2 = (bf16[80,1152]{1,0:T(8,128)(2,1)}, bf16[80,1152]{1,0:T(8,128)(2,1)S(1)}, u32[]{:S(2)}) copy-start(bf16[80,1152]{1,0:T(8,128)(2,1)S(1)} %collective-permute-done.1.p0_ref) | copy-start | bytes 552964
  17.6 0.9 %copy-start.3 = (bf16[80,1152]{1,0:T(8,128)(2,1)}, bf16[80,1152]{1,0:T(8,128)(2,1)S(1)}, u32[]{:S(2)}) copy-start(bf16[80,1152]{1,0:T(8,128)(2,1)S(1)} %collective-permute-done.2.p3_ref) | copy-start | bytes 552964

commit v16 on v14

--- a/solution.py
+++ b/solution.py
@@ -140,9 +140,35 @@
     row_tiles = ROWS // TILE
     per_lane = STRIP // TILE
 
+    def setup_kernel(kp_ref, tap_ref, colm_ref, rowm_ref, a_ref, b_ref):
+        for k in range(NBASIS):
+            spread = jnp.broadcast_to(tap_ref[pl.ds(k, 1), :], (STRIP, span))
+            band_t = pltpu.roll(spread, 0, 1, stride=1, stride_axis=0)
+            colm_ref[:, k * STRIP : (k + 1) * STRIP] = band_t.T.astype(jnp.bfloat16)
+            spread = jnp.broadcast_to(tap_ref[pl.ds(NBASIS + k, 1), :], (ROWS, span))
+            band = pltpu.roll(spread, 0, 1, stride=1, stride_axis=0)
+            rowm_ref[k] = band.astype(jnp.bfloat16)
+        rows = lax.broadcasted_iota(jnp.int32, (ROWS, STRIP), 0).astype(jnp.float32)
+        u = 2.0 * (rows + kp_ref[at] + 0.5) / total_rows - 1.0
+        for k in range(NBASIS):
+            p = lambda m: kp_ref[k * NPOLY + m]
+            a_ref[k] = p(0) + p(1) * u + p(3) * u * u
+            b_ref[k] = p(2) + p(4) * u
+
+    colm, rowm, a_tab, b_tab = pl.pallas_call(
+        setup_kernel,
+        in_specs=[pl.BlockSpec(memory_space=pltpu.SMEM), pl.BlockSpec(memory_space=pltpu.VMEM)],
+        out_shape=(
+            jax.ShapeDtypeStruct((span, NBASIS * STRIP), jnp.bfloat16),
+            jax.ShapeDtypeStruct((NBASIS, ROWS, span), jnp.bfloat16),
+            jax.ShapeDtypeStruct((NBASIS, ROWS, STRIP), jnp.float32),
+            jax.ShapeDtypeStruct((NBASIS, ROWS, STRIP), jnp.float32),
+        ),
+    )(params, taps)
+
     def match_kernel(kp_ref, picks_ref, p0_ref, p1_ref, p2_ref, p3_ref,
-                     tap_ref, own_ref, w_ref,
-                     out_ref, acc_ref, pack_ref, a_ref, b_ref, colm_ref, rowm_ref, img_ref):
+                     colm_ref, rowm_ref, a_ref, b_ref, own_ref, w_ref,
+                     out_ref, acc_ref, pack_ref, img_ref):
         i = pl.program_id(0)
 
         @pl.when(i == 0)
@@ -159,19 +185,6 @@
                     preferred_element_type=jnp.float32,
                 )
             img_ref[...] = gathered.astype(jnp.bfloat16)
-            for k in range(NBASIS):
-                spread = jnp.broadcast_to(tap_ref[pl.ds(k, 1), :], (STRIP, span))
-                band_t = pltpu.roll(spread, 0, 1, stride=1, stride_axis=0)
-                colm_ref[:, k * STRIP : (k + 1) * STRIP] = band_t.T.astype(jnp.bfloat16)
-                spread = jnp.broadcast_to(tap_ref[pl.ds(NBASIS + k, 1), :], (ROWS, span))
-                band = pltpu.roll(spread, 0, 1, stride=1, stride_axis=0)
-                rowm_ref[k] = band.astype(jnp.bfloat16)
-            rows = lax.broadcasted_iota(jnp.int32, (ROWS, STRIP), 0).astype(jnp.float32)
-            u = 2.0 * (rows + kp_ref[at] + 0.5) / total_rows - 1.0
-            for k in range(NBASIS):
-                p = lambda m: kp_ref[k * NPOLY + m]
-                a_ref[k] = p(0) + p(1) * u + p(3) * u * u
-                b_ref[k] = p(2) + p(4) * u
 
         offset = pl.multiple_of(i * STRIP, STRIP)
         strip = img_ref[:, pl.ds(offset, span)]
@@ -219,19 +232,16 @@
         grid=(strips,),
         in_specs=[pl.BlockSpec(memory_space=pltpu.SMEM), full(picks.shape)]
         + [full(x.shape) for x in pieces]
-        + [full(taps.shape), full(owners.shape), full(weights.shape)],
+        + [full(colm.shape), full(rowm.shape), full(a_tab.shape), full(b_tab.shape)]
+        + [full(owners.shape), full(weights.shape)],
         out_specs=full((band_count, groups, STRIP)),
         out_shape=jax.ShapeDtypeStruct((band_count, groups, STRIP), jnp.bfloat16),
         scratch_shapes=[
             pltpu.VMEM((ROWS, STRIP), jnp.float32),
             pltpu.VMEM((tiles * groups, STRIP), jnp.float32),
-            pltpu.VMEM((NBASIS, ROWS, STRIP), jnp.float32),
-            pltpu.VMEM((NBASIS, ROWS, STRIP), jnp.float32),
-            pltpu.VMEM((span, NBASIS * STRIP), jnp.bfloat16),
-            pltpu.VMEM((NBASIS, ROWS, span), jnp.bfloat16),
             pltpu.VMEM((lead_pad, wide_cols), jnp.bfloat16),
         ],
-    )(params, picks, *pieces, taps, owners, weights)
+    )(params, picks, *pieces, colm, rowm, a_tab, b_tab, owners, weights)
     incoming = lax.all_to_all(outgoing, "ccd", split_axis=0, concat_axis=0, tiled=True)
     patch_sum = jnp.sum(incoming.astype(jnp.float32), axis=0, keepdims=True)
     return patch_sum.reshape(1, 1, TILE, TILE)

time: 59.8 us -> 62.3 us (1.042)
  Pallas kernels: 9.8 us -> 13.5 us
  waiting for transfers between devices: 1.69 us -> 0.01 us
    pallas_call x0 -> x1, Pallas kernels: none -> 3.24 us  [shards(): pl.pallas_call(setup_kernel, in_specs=[pl.BlockSpec(memory_space=pltpu.SM...]
    ppermute x1, waiting for transfers between devices: 1.47 us -> 0.01 us  [shards(): got_mixed = lax.ppermute(pick(sent_up, sent_down), axes, mixed)]
  transfers between devices with their start and end apart: 3 -> 3, of which waited for: 2 -> 0; matrix products, arithmetic and copies ran while one was open for 3% -> 4% of each run, Pallas kernels for 0% -> 5%
where the time goes in v16:
time: 62.3 us; the launch traced here: 62 us
  blocking collectives  30.8 us (49%)
  Pallas kernels  13.5 us (22%)
  starting transfers between devices  8.58 us (14%)
  local copies, waits for them, and re-layouts  5.39 us (9%)
  other arithmetic  3.53 us (6%)
    all_to_all x1, blocking collectives, shards(): lax.all_to_all(outgoing, 'ccd', split_axis=0, concat_axis=0, tiled=True)  30.8 us
    pallas_call x1, Pallas kernels, shards(): pl.pallas_call(match_kernel, grid=(strips,), in_specs=[pl.BlockSpec(memor...  10.3 us
    ppermute x1, starting transfers between devices, shards(): got_mixed = lax.ppermute(pick(sent_up, sent_down), axes, mixed)  4 us
    unnamed x21, local copies, waits for them, and re-layouts  3.29 us
    ppermute x1, starting transfers between devices, shards(): got_swap = lax.ppermute(other, axes, swap)  3.29 us
    pallas_call x1, Pallas kernels, shards(): pl.pallas_call(setup_kernel, in_specs=[pl.BlockSpec(memory_space=pltpu.SM...  3.24 us
    squeeze x1, other arithmetic, shards(): ((raw_counts - overscan[..., None]) * response).astype(jnp.bfloat16)[0, 0]  1.31 us
    ppermute x1, starting transfers between devices, shards(): got_mirrored = lax.ppermute(pick(sent_down, sent_up), axes, mirrored)  1.29 us
  transfers between devices with their start and end apart: 3, of which 0 were waited for; matrix products, arithmetic and copies ran while one was open for 4% of the time, Pallas kernels for 5%

profile of v16, /device:TPU:1, one launch (start us, length us, event | category | flops | bytes accessed | tf_op | source)
XLA Modules:
  0.0 62.0 jit_solution(13017493487380653786)
XLA Ops:
  0.0 0.7 %copy-done.9 = s32[128]{0:T(128)S(1)} copy-done((s32[128]{0:T(128)S(1)}, s32[128]{0:T(128)}, u32[]{:S(2)}) %copy-start.9) | copy-done | bytes 536
  0.7 0.1 copy.14
  0.9 0.7 %copy-done.8 = f32[1,1,64]{2,1,0:T(1,128)S(1)} copy-done((f32[1,1,64]{2,1,0:T(1,128)S(1)}, f32[1,1,64]{2,1,0:T(1,128)}, u32[]{:S(2)}) %copy-start.8) | copy-done | bytes 280
  1.5 1.3 %fusion = bf16[64,2048]{1,0:T(8,128)(2,1)S(1)} fusion(f32[1,1,64,2048]{3,2,1,0:T(8,128)} %param.11, f32[1,1,64,2048]{3,2,1,0:T(8,128)} %param.9, f32[64]{0:T(128)S(1)} %bitcast.11), kind=kLoop, calls=%fused_computation.2 | loop fusion | flops 393216 | bytes 1310976 | tf_op jit(solution)/shard_map/squeeze | solution.py:80
  2.8 0.2 pad_dynamic-slice_fusion.1
  3.0 0.1 concatenate.20
  3.1 3.3 %collective-permute-start = (bf16[64,1152]{1,0:T(8,128)(2,1)S(1)}, bf16[64,1152]{1,0:T(8,128)(2,1)S(1)}, u32[]{:S(2)}, u32[]{:S(2)}) collective-permute-start(bf16[64,1152]{1,0:T(8,128)(2,1)S(1)} %concatenate.20), channel_id=1, source_target_pairs={{0,128},{1,129},{2,130},{3,131},{4,132},{5,133},{6,134},{7,135},{8... | collective-permute-start | bytes 442376 | tf_op jit(solution)/shard_map/ppermute | solution.py:96
  6.5 0.6 %copy-done.5 = f32[26]{0:T(128)S(1)} copy-done((f32[26]{0:T(128)S(1)}, f32[26]{0:T(128)}, u32[]{:S(2)}) %copy-start.5) | copy-done | bytes 128
  7.1 0.2 multiply_reduce_fusion
  7.5 0.6 copy-done.4
  8.3 0.1 concatenate.19.p1_ref
  8.4 0.7 %pad_convert_fusion.tap_ref = f32[26,256]{1,0:T(8,128)} fusion(bf16[26,21]{1,0:T(8,128)(2,1)S(1)} %divide_convert_fusion), kind=kLoop, calls=%fused_computation.15 | loop fusion | flops 6656 | bytes 27716 | tf_op jit(solution)/shard_map/jit(_pad)/pad | solution.py:131
  9.1 0.6 copy-done.1
  9.8 1.3 %collective-permute-start.1 = (bf16[80,1152]{1,0:T(8,128)(2,1)S(1)}, bf16[80,1152]{1,0:T(8,128)(2,1)S(1)}, u32[]{:S(2)}, u32[]{:S(2)}) collective-permute-start(bf16[80,1152]{1,0:T(8,128)(2,1)S(1)} %get-tuple-element.15), channel_id=1, source_target_pairs={{0,1},{1,2},{2,3},{3,4},{4,5},{5,6},{6,7},{7,8},{8,9},{9,10},{10,1... | collective-permute-start | bytes 552968 | tf_op jit(solution)/shard_map/ppermute | solution.py:108
  11.1 4.0 %collective-permute-start.2 = (bf16[80,1152]{1,0:T(8,128)(2,1)S(1)}, bf16[80,1152]{1,0:T(8,128)(2,1)S(1)}, u32[]{:S(2)}, u32[]{:S(2)}) collective-permute-start(bf16[80,1152]{1,0:T(8,128)(2,1)S(1)} %get-tuple-element.16), channel_id=1, source_target_pairs={{1,0},{2,1},{3,2},{4,3},{5,4},{6,5},{7,6},{8,7},{9,8},{10,9},{11,1... | collective-permute-start | bytes 552968 | tf_op jit(solution)/shard_map/ppermute | solution.py:107
  15.1 0.7 %pad_maximum_fusion.2.kp_ref = f32[80]{0:T(128)} fusion(f32[2]{0:T(128)S(1)} %add_convert_fusion, f32[78]{0:T(128)S(1)} %reshape.36), kind=kLoop, calls=%fused_computation.24 | loop fusion | flops 80 | bytes 640 | tf_op jit(solution)/shard_map/concatenate | solution.py:132
  15.8 3.2 %shard_map.91 = (bf16[256,1664]{1,0:T(8,128)(2,1)}, bf16[13,128,256]{2,1,0:T(8,128)(2,1)}, f32[13,128,128]{2,1,0:T(8,128)}, f32[13,128,128]{2,1,0:T(8,128)}) custom-call(f32[80]{0:T(128)} %pad_maximum_fusion.2.kp_ref, f32[26,256]{1,0:T(8,128)} %pad_convert_fusion.tap_ref), custom_call_target="tpu_custom_call" | custom-call | tf_op jit(solution)/shard_map/pallas_call | solution.py:158
  19.0 0.2 slice_reduce_fusion
  19.2 0.2 fusion.3
  19.5 0.6 pad.15
  20.1 10.3 %shard_map.92 = bf16[128,8,128]{2,1,0:T(8,128)(2,1)} custom-call(f32[80]{0:T(128)} %pad_maximum_fusion.2.kp_ref, s32[1,160]{1,0:T(1,128)} %bitcast.10, bf16[80,1152]{1,0:T(8,128)(2,1)} %copy-done.2, bf16[64,1152]{1,0:T(8,128)(2,1)} %copy-done, bf16[64,1152]{1,0:T(8,128)(2,1)} %copy-done.1, bf16[80,1152]{1,0:T(8,128)(2,1)} %copy-done.3, ...), custom_call_target="tpu_custom_call" | custom-call | tf_op jit(solution)/shard_map/pallas_call | solution.py:230
  30.4 30.8 %all_to_all.5 = bf16[128,8,128]{2,1,0:T(8,128)(2,1)S(1)} all-to-all(bf16[128,8,128]{2,1,0:T(8,128)(2,1)} %shard_map.92), channel_id=1, replica_groups=mesh['section'=2,'ccd'=128] {'ccd'}, dimensions={0} | all-to-all | bytes 524288 | tf_op jit(solution)/shard_map/all_to_all | solution.py:245
  61.2 0.1 convert_reduce_fusion
  61.3 0.7 %reshape_broadcast_in_dim.3 = f32[1,1,32,32]{3,2,1,0:T(8,128)} reshape(f32[8,128]{1,0:T(8,128)S(1)} %convert_reduce_fusion) | data formatting | bytes 8192 | tf_op jit(solution)/shard_map/reshape;broadcast_in_dim | solution.py:247
  (33 shorter events, 0.7 us)
Async XLA Ops:
  0.0 0.7 %copy-start.9 = (s32[128]{0:T(128)S(1)}, s32[128]{0:T(128)}, u32[]{:S(2)}) copy-start(s32[128]{0:T(128)} %param.12) | copy-start | bytes 1540
  0.9 0.7 %copy-start.8 = (f32[1,1,64]{2,1,0:T(1,128)S(1)}, f32[1,1,64]{2,1,0:T(1,128)}, u32[]{:S(2)}) copy-start(f32[1,1,64]{2,1,0:T(1,128)} %param.10) | copy-start | bytes 772
  3.1 5.9 %collective-permute-start = (bf16[64,1152]{1,0:T(8,128)(2,1)S(1)}, bf16[64,1152]{1,0:T(8,128)(2,1)S(1)}, u32[]{:S(2)}, u32[]{:S(2)}) collective-permute-start(bf16[64,1152]{1,0:T(8,128)(2,1)S(1)} %concatenate.20), channel_id=1, source_target_pairs={{0,128},{1,129},{2,130},{3,131},{4,132},{5,133},{6,134},{7,135},{8... | collective-permute-start | bytes 442376 | tf_op jit(solution)/shard_map/ppermute | solution.py:96
  6.4 0.7 %copy-start.5 = (f32[26]{0:T(128)S(1)}, f32[26]{0:T(128)}, u32[]{:S(2)}) copy-start(f32[26]{0:T(128)} %constant.71) | copy-start | bytes 316
  6.4 0.7 %copy-start.6 = (pred[26]{0:T(512)(128)(4,1)S(1)}, pred[26]{0:T(512)(128)(4,1)}, u32[]{:S(2)}) copy-start(pred[26]{0:T(512)(128)(4,1)} %constant.70) | copy-start | bytes 82
  6.4 0.7 %copy-start.7 = (pred[26]{0:T(512)(128)(4,1)S(1)}, pred[26]{0:T(512)(128)(4,1)}, u32[]{:S(2)}) copy-start(pred[26]{0:T(512)(128)(4,1)} %constant.69) | copy-start | bytes 82
  7.4 0.7 %copy-start.4 = (f32[13,6]{0,1:T(8,128)S(1)}, f32[13,6]{0,1:T(8,128)}, u32[]{:S(2)}) copy-start(f32[13,6]{0,1:T(8,128)} %param.13) | copy-start | bytes 940
  8.4 0.7 %copy-start = (bf16[64,1152]{1,0:T(8,128)(2,1)}, bf16[64,1152]{1,0:T(8,128)(2,1)S(1)}, u32[]{:S(2)}) copy-start(bf16[64,1152]{1,0:T(8,128)(2,1)S(1)} %concatenate.19.p1_ref) | copy-start | bytes 442372
  9.1 0.6 %copy-start.1 = (bf16[64,1152]{1,0:T(8,128)(2,1)}, bf16[64,1152]{1,0:T(8,128)(2,1)S(1)}, u32[]{:S(2)}) copy-start(bf16[64,1152]{1,0:T(8,128)(2,1)S(1)} %collective-permute-done.p2_ref) | copy-start | bytes 442372
  9.8 9.4 %collective-permute-start.1 = (bf16[80,1152]{1,0:T(8,128)(2,1)S(1)}, bf16[80,1152]{1,0:T(8,128)(2,1)S(1)}, u32[]{:S(2)}, u32[]{:S(2)}) collective-permute-start(bf16[80,1152]{1,0:T(8,128)(2,1)S(1)} %get-tuple-element.15), channel_id=1, source_target_pairs={{0,1},{1,2},{2,3},{3,4},{4,5},{5,6},{6,7},{7,8},{8,9},{9,10},{10,1... | collective-permute-start | bytes 552968 | tf_op jit(solution)/shard_map/ppermute | solution.py:108
  11.1 8.1 %collective-permute-start.2 = (bf16[80,1152]{1,0:T(8,128)(2,1)S(1)}, bf16[80,1152]{1,0:T(8,128)(2,1)S(1)}, u32[]{:S(2)}, u32[]{:S(2)}) collective-permute-start(bf16[80,1152]{1,0:T(8,128)(2,1)S(1)} %get-tuple-element.16), channel_id=1, source_target_pairs={{1,0},{2,1},{3,2},{4,3},{5,4},{6,5},{7,6},{8,7},{9,8},{10,9},{11,1... | collective-permute-start | bytes 552968 | tf_op jit(solution)/shard_map/ppermute | solution.py:107
  19.2 0.9 %copy-start.2 = (bf16[80,1152]{1,0:T(8,128)(2,1)}, bf16[80,1152]{1,0:T(8,128)(2,1)S(1)}, u32[]{:S(2)}) copy-start(bf16[80,1152]{1,0:T(8,128)(2,1)S(1)} %collective-permute-done.1.p0_ref) | copy-start | bytes 552964
  19.2 0.9 %copy-start.3 = (bf16[80,1152]{1,0:T(8,128)(2,1)}, bf16[80,1152]{1,0:T(8,128)(2,1)S(1)}, u32[]{:S(2)}) copy-start(bf16[80,1152]{1,0:T(8,128)(2,1)S(1)} %collective-permute-done.2.p3_ref) | copy-start | bytes 552964

commit v17 on v14

--- a/solution.py
+++ b/solution.py
@@ -97,7 +97,7 @@
     pick = lambda a, b: jnp.where(half == 0, a, b)
     first_rows = pick(own, got_swap)
     second_rows = pick(got_swap, own)
-    rim = 16
+    rim = HALF_K
     sent_up = jnp.concatenate([first_rows, second_rows[:rim]], axis=0)
     sent_down = jnp.concatenate([first_rows[rh - rim :], second_rows], axis=0)
     upward = [(b, b - 1) for b in range(1, nb)]

time: 59.8 us -> 59.8 us (level)
  no operation moved by 1% of the time
where the time goes in v17:
time: 59.8 us; the launch traced here: 59.5 us
  blocking collectives  30.5 us (51%)
  Pallas kernels  9.79 us (16%)
  starting transfers between devices  8.58 us (14%)
  local copies, waits for them, and re-layouts  5.39 us (9%)
  other arithmetic  3.43 us (6%)
  waiting for transfers between devices  1.69 us (3%)
    all_to_all x1, blocking collectives, shards(): lax.all_to_all(outgoing, 'ccd', split_axis=0, concat_axis=0, tiled=True)  30.5 us
    pallas_call x1, Pallas kernels, shards(): pl.pallas_call(match_kernel, grid=(strips,), in_specs=[pl.BlockSpec(memor...  9.79 us
    ppermute x1, starting transfers between devices, shards(): got_mixed = lax.ppermute(pick(sent_up, sent_down), axes, mixed)  4 us
    ppermute x1, starting transfers between devices, shards(): got_swap = lax.ppermute(other, axes, swap)  3.29 us
    unnamed x21, local copies, waits for them, and re-layouts  3.27 us
    ppermute x1, waiting for transfers between devices, shards(): got_mixed = lax.ppermute(pick(sent_up, sent_down), axes, mixed)  1.47 us
    squeeze x1, other arithmetic, shards(): ((raw_counts - overscan[..., None]) * response).astype(jnp.bfloat16)[0, 0]  1.31 us
    ppermute x1, starting transfers between devices, shards(): got_mirrored = lax.ppermute(pick(sent_down, sent_up), axes, mirrored)  1.29 us
  transfers between devices with their start and end apart: 3, of which 2 were waited for; matrix products, arithmetic and copies ran while one was open for 3% of the time, Pallas kernels for 0%

profile of v17, /device:TPU:1, one launch (start us, length us, event | category | flops | bytes accessed | tf_op | source)
XLA Modules:
  0.0 59.5 jit_solution(432839752619175055)
XLA Ops:
  0.0 0.7 %copy-done.9 = s32[128]{0:T(128)S(1)} copy-done((s32[128]{0:T(128)S(1)}, s32[128]{0:T(128)}, u32[]{:S(2)}) %copy-start.9) | copy-done | bytes 536
  0.7 0.1 copy.14
  0.9 0.7 %copy-done.8 = f32[1,1,64]{2,1,0:T(1,128)S(1)} copy-done((f32[1,1,64]{2,1,0:T(1,128)S(1)}, f32[1,1,64]{2,1,0:T(1,128)}, u32[]{:S(2)}) %copy-start.8) | copy-done | bytes 280
  1.5 1.3 %fusion = bf16[64,2048]{1,0:T(8,128)(2,1)S(1)} fusion(f32[1,1,64,2048]{3,2,1,0:T(8,128)} %param.11, f32[1,1,64,2048]{3,2,1,0:T(8,128)} %param.9, f32[64]{0:T(128)S(1)} %bitcast.13), kind=kLoop, calls=%fused_computation.2 | loop fusion | flops 393216 | bytes 1310976 | tf_op jit(solution)/shard_map/squeeze | solution.py:80
  2.8 0.2 pad_dynamic-slice_fusion.1
  3.0 0.1 concatenate.20
  3.1 3.3 %collective-permute-start = (bf16[64,1152]{1,0:T(8,128)(2,1)S(1)}, bf16[64,1152]{1,0:T(8,128)(2,1)S(1)}, u32[]{:S(2)}, u32[]{:S(2)}) collective-permute-start(bf16[64,1152]{1,0:T(8,128)(2,1)S(1)} %concatenate.20), channel_id=1, source_target_pairs={{0,128},{1,129},{2,130},{3,131},{4,132},{5,133},{6,134},{7,135},{8... | collective-permute-start | bytes 442376 | tf_op jit(solution)/shard_map/ppermute | solution.py:96
  6.5 0.6 %copy-done.5 = pred[26]{0:T(512)(128)(4,1)S(1)} copy-done((pred[26]{0:T(512)(128)(4,1)S(1)}, pred[26]{0:T(512)(128)(4,1)}, u32[]{:S(2)}) %copy-start.5) | copy-done | bytes 50
  7.1 0.2 multiply_reduce_fusion
  7.6 0.6 copy-done.4
  8.4 0.6 %pad_convert_fusion.tap_ref = f32[26,256]{1,0:T(8,128)} fusion(bf16[26,21]{1,0:T(8,128)(2,1)S(1)} %divide_convert_fusion), kind=kLoop, calls=%fused_computation.15 | loop fusion | flops 6656 | bytes 27716 | tf_op jit(solution)/shard_map/jit(_pad)/pad | solution.py:131
  9.0 0.6 %copy-done.1 = bf16[64,1152]{1,0:T(8,128)(2,1)} copy-done((bf16[64,1152]{1,0:T(8,128)(2,1)}, bf16[64,1152]{1,0:T(8,128)(2,1)S(1)}, u32[]{:S(2)}) %copy-start.1) | copy-done | bytes 147480
  9.8 1.3 %collective-permute-start.1 = (bf16[74,1152]{1,0:T(8,128)(2,1)S(1)}, bf16[74,1152]{1,0:T(8,128)(2,1)S(1)}, u32[]{:S(2)}, u32[]{:S(2)}) collective-permute-start(bf16[74,1152]{1,0:T(8,128)(2,1)S(1)} %get-tuple-element.7), channel_id=1, source_target_pairs={{0,1},{1,2},{2,3},{3,4},{4,5},{5,6},{6,7},{7,8},{8,9},{9,10},{10,1... | collective-permute-start | bytes 511496 | tf_op jit(solution)/shard_map/ppermute | solution.py:108
  11.1 4.0 %collective-permute-start.2 = (bf16[74,1152]{1,0:T(8,128)(2,1)S(1)}, bf16[74,1152]{1,0:T(8,128)(2,1)S(1)}, u32[]{:S(2)}, u32[]{:S(2)}) collective-permute-start(bf16[74,1152]{1,0:T(8,128)(2,1)S(1)} %get-tuple-element.8), channel_id=1, source_target_pairs={{1,0},{2,1},{3,2},{4,3},{5,4},{6,5},{7,6},{8,7},{9,8},{10,9},{11,1... | collective-permute-start | bytes 511496 | tf_op jit(solution)/shard_map/ppermute | solution.py:107
  15.1 0.6 pad_maximum_fusion.2.kp_ref
  15.7 0.2 slice_reduce_fusion
  15.9 0.2 collective-permute-done.1.p0_ref
  16.1 1.5 %collective-permute-done.2.p3_ref = bf16[74,1152]{1,0:T(8,128)(2,1)S(1)} collective-permute-done((bf16[74,1152]{1,0:T(8,128)(2,1)S(1)}, bf16[74,1152]{1,0:T(8,128)(2,1)S(1)}, u32[]{:S(2)}, u32[]{:S(2)}) %collective-permute-start.2) | collective-permute-done | bytes 170528 | tf_op jit(solution)/shard_map/ppermute | solution.py:107
  17.5 0.2 fusion.3
  17.8 0.6 pad.15
  18.4 9.8 %shard_map.91 = bf16[128,8,128]{2,1,0:T(8,128)(2,1)} custom-call(f32[80]{0:T(128)} %pad_maximum_fusion.2.kp_ref, s32[1,160]{1,0:T(1,128)} %bitcast.10, bf16[74,1152]{1,0:T(8,128)(2,1)} %copy-done.2, bf16[64,1152]{1,0:T(8,128)(2,1)} %copy-done, bf16[64,1152]{1,0:T(8,128)(2,1)} %copy-done.1, bf16[74,1152]{1,0:T(8,128)(2,1)} %copy-done.3, ...), custom_call_target="tpu_custom_call" | custom-call | tf_op jit(solution)/shard_map/pallas_call | solution.py:217
  28.2 30.5 %all_to_all.5 = bf16[128,8,128]{2,1,0:T(8,128)(2,1)S(1)} all-to-all(bf16[128,8,128]{2,1,0:T(8,128)(2,1)} %shard_map.91), channel_id=1, replica_groups=mesh['section'=2,'ccd'=128] {'ccd'}, dimensions={0} | all-to-all | bytes 524288 | tf_op jit(solution)/shard_map/all_to_all | solution.py:235
  58.7 0.1 convert_reduce_fusion
  58.8 0.7 %reshape_broadcast_in_dim.3 = f32[1,1,32,32]{3,2,1,0:T(8,128)} reshape(f32[8,128]{1,0:T(8,128)S(1)} %convert_reduce_fusion) | data formatting | bytes 8192 | tf_op jit(solution)/shard_map/reshape;broadcast_in_dim | solution.py:237
  (32 shorter events, 0.9 us)
Async XLA Ops:
  0.0 0.7 %copy-start.9 = (s32[128]{0:T(128)S(1)}, s32[128]{0:T(128)}, u32[]{:S(2)}) copy-start(s32[128]{0:T(128)} %param.12) | copy-start | bytes 1540
  0.9 0.7 %copy-start.8 = (f32[1,1,64]{2,1,0:T(1,128)S(1)}, f32[1,1,64]{2,1,0:T(1,128)}, u32[]{:S(2)}) copy-start(f32[1,1,64]{2,1,0:T(1,128)} %param.10) | copy-start | bytes 772
  3.1 5.9 %collective-permute-start = (bf16[64,1152]{1,0:T(8,128)(2,1)S(1)}, bf16[64,1152]{1,0:T(8,128)(2,1)S(1)}, u32[]{:S(2)}, u32[]{:S(2)}) collective-permute-start(bf16[64,1152]{1,0:T(8,128)(2,1)S(1)} %concatenate.20), channel_id=1, source_target_pairs={{0,128},{1,129},{2,130},{3,131},{4,132},{5,133},{6,134},{7,135},{8... | collective-permute-start | bytes 442376 | tf_op jit(solution)/shard_map/ppermute | solution.py:96
  6.4 0.7 %copy-start.5 = (pred[26]{0:T(512)(128)(4,1)S(1)}, pred[26]{0:T(512)(128)(4,1)}, u32[]{:S(2)}) copy-start(pred[26]{0:T(512)(128)(4,1)} %constant.68) | copy-start | bytes 82
  6.4 0.7 %copy-start.6 = (pred[26]{0:T(512)(128)(4,1)S(1)}, pred[26]{0:T(512)(128)(4,1)}, u32[]{:S(2)}) copy-start(pred[26]{0:T(512)(128)(4,1)} %constant.69) | copy-start | bytes 82
  6.4 0.7 %copy-start.7 = (f32[26]{0:T(128)S(1)}, f32[26]{0:T(128)}, u32[]{:S(2)}) copy-start(f32[26]{0:T(128)} %constant.70) | copy-start | bytes 316
  7.5 0.7 %copy-start.4 = (f32[13,6]{0,1:T(8,128)S(1)}, f32[13,6]{0,1:T(8,128)}, u32[]{:S(2)}) copy-start(f32[13,6]{0,1:T(8,128)} %param.13) | copy-start | bytes 940
  7.6 1.4 %copy-start = (bf16[64,1152]{1,0:T(8,128)(2,1)}, bf16[64,1152]{1,0:T(8,128)(2,1)S(1)}, u32[]{:S(2)}) copy-start(bf16[64,1152]{1,0:T(8,128)(2,1)S(1)} %concatenate.19.p1_ref) | copy-start | bytes 442372
  9.0 0.7 %copy-start.1 = (bf16[64,1152]{1,0:T(8,128)(2,1)}, bf16[64,1152]{1,0:T(8,128)(2,1)S(1)}, u32[]{:S(2)}) copy-start(bf16[64,1152]{1,0:T(8,128)(2,1)S(1)} %collective-permute-done.p2_ref) | copy-start | bytes 442372
  9.8 6.3 %collective-permute-start.1 = (bf16[74,1152]{1,0:T(8,128)(2,1)S(1)}, bf16[74,1152]{1,0:T(8,128)(2,1)S(1)}, u32[]{:S(2)}, u32[]{:S(2)}) collective-permute-start(bf16[74,1152]{1,0:T(8,128)(2,1)S(1)} %get-tuple-element.7), channel_id=1, source_target_pairs={{0,1},{1,2},{2,3},{3,4},{4,5},{5,6},{6,7},{7,8},{8,9},{9,10},{10,1... | collective-permute-start | bytes 511496 | tf_op jit(solution)/shard_map/ppermute | solution.py:108
  11.1 6.5 %collective-permute-start.2 = (bf16[74,1152]{1,0:T(8,128)(2,1)S(1)}, bf16[74,1152]{1,0:T(8,128)(2,1)S(1)}, u32[]{:S(2)}, u32[]{:S(2)}) collective-permute-start(bf16[74,1152]{1,0:T(8,128)(2,1)S(1)} %get-tuple-element.8), channel_id=1, source_target_pairs={{1,0},{2,1},{3,2},{4,3},{5,4},{6,5},{7,6},{8,7},{9,8},{10,9},{11,1... | collective-permute-start | bytes 511496 | tf_op jit(solution)/shard_map/ppermute | solution.py:107
  16.1 2.3 %copy-start.2 = (bf16[74,1152]{1,0:T(8,128)(2,1)}, bf16[74,1152]{1,0:T(8,128)(2,1)S(1)}, u32[]{:S(2)}) copy-start(bf16[74,1152]{1,0:T(8,128)(2,1)S(1)} %collective-permute-done.1.p0_ref) | copy-start | bytes 511492
  17.5 0.9 %copy-start.3 = (bf16[74,1152]{1,0:T(8,128)(2,1)}, bf16[74,1152]{1,0:T(8,128)(2,1)S(1)}, u32[]{:S(2)}) copy-start(bf16[74,1152]{1,0:T(8,128)(2,1)S(1)} %collective-permute-done.2.p3_ref) | copy-start | bytes 511492

commit v18 on v17

--- a/solution.py
+++ b/solution.py
@@ -209,7 +209,7 @@
             for q in range(groups):
                 part = pack_ref[pl.ds(q, tiles, stride=groups), :]
                 out_ref[:, q, :] = jnp.dot(
-                    sel, part, precision=lax.Precision.HIGHEST,
+                    sel, part, precision=lax.Precision.HIGH,
                     preferred_element_type=jnp.float32,
                 ).astype(out_ref.dtype)
 

time: 59.8 us -> 59.6 us (level)
  no operation moved by 1% of the time
where the time goes in v18:
time: 59.6 us; the launch traced here: 59.3 us
  blocking collectives  30.5 us (51%)
  Pallas kernels  9.61 us (16%)
  starting transfers between devices  8.58 us (14%)
  local copies, waits for them, and re-layouts  5.39 us (9%)
  other arithmetic  3.43 us (6%)
  waiting for transfers between devices  1.69 us (3%)
    all_to_all x1, blocking collectives, shards(): lax.all_to_all(outgoing, 'ccd', split_axis=0, concat_axis=0, tiled=True)  30.5 us
    pallas_call x1, Pallas kernels, shards(): pl.pallas_call(match_kernel, grid=(strips,), in_specs=[pl.BlockSpec(memor...  9.61 us
    ppermute x1, starting transfers between devices, shards(): got_mixed = lax.ppermute(pick(sent_up, sent_down), axes, mixed)  4 us
    ppermute x1, starting transfers between devices, shards(): got_swap = lax.ppermute(other, axes, swap)  3.29 us
    unnamed x21, local copies, waits for them, and re-layouts  3.27 us
    ppermute x1, waiting for transfers between devices, shards(): got_mixed = lax.ppermute(pick(sent_up, sent_down), axes, mixed)  1.47 us
    squeeze x1, other arithmetic, shards(): ((raw_counts - overscan[..., None]) * response).astype(jnp.bfloat16)[0, 0]  1.31 us
    ppermute x1, starting transfers between devices, shards(): got_mirrored = lax.ppermute(pick(sent_down, sent_up), axes, mirrored)  1.29 us
  transfers between devices with their start and end apart: 3, of which 2 were waited for; matrix products, arithmetic and copies ran while one was open for 3% of the time, Pallas kernels for 0%

profile of v18, /device:TPU:1, one launch (start us, length us, event | category | flops | bytes accessed | tf_op | source)
XLA Modules:
  0.0 59.3 jit_solution(4614784313527870262)
XLA Ops:
  0.0 0.7 %copy-done.9 = s32[128]{0:T(128)S(1)} copy-done((s32[128]{0:T(128)S(1)}, s32[128]{0:T(128)}, u32[]{:S(2)}) %copy-start.9) | copy-done | bytes 536
  0.7 0.1 copy.14
  0.9 0.7 %copy-done.8 = f32[1,1,64]{2,1,0:T(1,128)S(1)} copy-done((f32[1,1,64]{2,1,0:T(1,128)S(1)}, f32[1,1,64]{2,1,0:T(1,128)}, u32[]{:S(2)}) %copy-start.8) | copy-done | bytes 280
  1.5 1.3 %fusion = bf16[64,2048]{1,0:T(8,128)(2,1)S(1)} fusion(f32[1,1,64,2048]{3,2,1,0:T(8,128)} %param.11, f32[1,1,64,2048]{3,2,1,0:T(8,128)} %param.9, f32[64]{0:T(128)S(1)} %bitcast.13), kind=kLoop, calls=%fused_computation.2 | loop fusion | flops 393216 | bytes 1310976 | tf_op jit(solution)/shard_map/squeeze | solution.py:80
  2.8 0.2 pad_dynamic-slice_fusion.1
  3.0 0.1 concatenate.20
  3.1 3.3 %collective-permute-start = (bf16[64,1152]{1,0:T(8,128)(2,1)S(1)}, bf16[64,1152]{1,0:T(8,128)(2,1)S(1)}, u32[]{:S(2)}, u32[]{:S(2)}) collective-permute-start(bf16[64,1152]{1,0:T(8,128)(2,1)S(1)} %concatenate.20), channel_id=1, source_target_pairs={{0,128},{1,129},{2,130},{3,131},{4,132},{5,133},{6,134},{7,135},{8... | collective-permute-start | bytes 442376 | tf_op jit(solution)/shard_map/ppermute | solution.py:96
  6.5 0.6 %copy-done.5 = pred[26]{0:T(512)(128)(4,1)S(1)} copy-done((pred[26]{0:T(512)(128)(4,1)S(1)}, pred[26]{0:T(512)(128)(4,1)}, u32[]{:S(2)}) %copy-start.5) | copy-done | bytes 50
  7.1 0.2 multiply_reduce_fusion
  7.6 0.6 copy-done.4
  8.4 0.6 %pad_convert_fusion.tap_ref = f32[26,256]{1,0:T(8,128)} fusion(bf16[26,21]{1,0:T(8,128)(2,1)S(1)} %divide_convert_fusion), kind=kLoop, calls=%fused_computation.15 | loop fusion | flops 6656 | bytes 27716 | tf_op jit(solution)/shard_map/jit(_pad)/pad | solution.py:131
  9.0 0.6 %copy-done.1 = bf16[64,1152]{1,0:T(8,128)(2,1)} copy-done((bf16[64,1152]{1,0:T(8,128)(2,1)}, bf16[64,1152]{1,0:T(8,128)(2,1)S(1)}, u32[]{:S(2)}) %copy-start.1) | copy-done | bytes 147480
  9.8 1.3 %collective-permute-start.1 = (bf16[74,1152]{1,0:T(8,128)(2,1)S(1)}, bf16[74,1152]{1,0:T(8,128)(2,1)S(1)}, u32[]{:S(2)}, u32[]{:S(2)}) collective-permute-start(bf16[74,1152]{1,0:T(8,128)(2,1)S(1)} %get-tuple-element.7), channel_id=1, source_target_pairs={{0,1},{1,2},{2,3},{3,4},{4,5},{5,6},{6,7},{7,8},{8,9},{9,10},{10,1... | collective-permute-start | bytes 511496 | tf_op jit(solution)/shard_map/ppermute | solution.py:108
  11.1 4.0 %collective-permute-start.2 = (bf16[74,1152]{1,0:T(8,128)(2,1)S(1)}, bf16[74,1152]{1,0:T(8,128)(2,1)S(1)}, u32[]{:S(2)}, u32[]{:S(2)}) collective-permute-start(bf16[74,1152]{1,0:T(8,128)(2,1)S(1)} %get-tuple-element.8), channel_id=1, source_target_pairs={{1,0},{2,1},{3,2},{4,3},{5,4},{6,5},{7,6},{8,7},{9,8},{10,9},{11,1... | collective-permute-start | bytes 511496 | tf_op jit(solution)/shard_map/ppermute | solution.py:107
  15.1 0.6 pad_maximum_fusion.2.kp_ref
  15.7 0.2 slice_reduce_fusion
  15.9 0.2 collective-permute-done.1.p0_ref
  16.1 1.5 %collective-permute-done.2.p3_ref = bf16[74,1152]{1,0:T(8,128)(2,1)S(1)} collective-permute-done((bf16[74,1152]{1,0:T(8,128)(2,1)S(1)}, bf16[74,1152]{1,0:T(8,128)(2,1)S(1)}, u32[]{:S(2)}, u32[]{:S(2)}) %collective-permute-start.2) | collective-permute-done | bytes 170528 | tf_op jit(solution)/shard_map/ppermute | solution.py:107
  17.5 0.2 fusion.3
  17.8 0.6 pad.15
  18.4 9.6 %shard_map.91 = bf16[128,8,128]{2,1,0:T(8,128)(2,1)} custom-call(f32[80]{0:T(128)} %pad_maximum_fusion.2.kp_ref, s32[1,160]{1,0:T(1,128)} %bitcast.10, bf16[74,1152]{1,0:T(8,128)(2,1)} %copy-done.2, bf16[64,1152]{1,0:T(8,128)(2,1)} %copy-done, bf16[64,1152]{1,0:T(8,128)(2,1)} %copy-done.1, bf16[74,1152]{1,0:T(8,128)(2,1)} %copy-done.3, ...), custom_call_target="tpu_custom_call" | custom-call | tf_op jit(solution)/shard_map/pallas_call | solution.py:217
  28.0 30.5 %all_to_all.5 = bf16[128,8,128]{2,1,0:T(8,128)(2,1)S(1)} all-to-all(bf16[128,8,128]{2,1,0:T(8,128)(2,1)} %shard_map.91), channel_id=1, replica_groups=mesh['section'=2,'ccd'=128] {'ccd'}, dimensions={0} | all-to-all | bytes 524288 | tf_op jit(solution)/shard_map/all_to_all | solution.py:235
  58.5 0.1 convert_reduce_fusion
  58.7 0.7 %reshape_broadcast_in_dim.3 = f32[1,1,32,32]{3,2,1,0:T(8,128)} reshape(f32[8,128]{1,0:T(8,128)S(1)} %convert_reduce_fusion) | data formatting | bytes 8192 | tf_op jit(solution)/shard_map/reshape;broadcast_in_dim | solution.py:237
  (32 shorter events, 0.9 us)
Async XLA Ops:
  0.0 0.7 %copy-start.9 = (s32[128]{0:T(128)S(1)}, s32[128]{0:T(128)}, u32[]{:S(2)}) copy-start(s32[128]{0:T(128)} %param.12) | copy-start | bytes 1540
  0.9 0.7 %copy-start.8 = (f32[1,1,64]{2,1,0:T(1,128)S(1)}, f32[1,1,64]{2,1,0:T(1,128)}, u32[]{:S(2)}) copy-start(f32[1,1,64]{2,1,0:T(1,128)} %param.10) | copy-start | bytes 772
  3.1 5.9 %collective-permute-start = (bf16[64,1152]{1,0:T(8,128)(2,1)S(1)}, bf16[64,1152]{1,0:T(8,128)(2,1)S(1)}, u32[]{:S(2)}, u32[]{:S(2)}) collective-permute-start(bf16[64,1152]{1,0:T(8,128)(2,1)S(1)} %concatenate.20), channel_id=1, source_target_pairs={{0,128},{1,129},{2,130},{3,131},{4,132},{5,133},{6,134},{7,135},{8... | collective-permute-start | bytes 442376 | tf_op jit(solution)/shard_map/ppermute | solution.py:96
  6.4 0.7 %copy-start.5 = (pred[26]{0:T(512)(128)(4,1)S(1)}, pred[26]{0:T(512)(128)(4,1)}, u32[]{:S(2)}) copy-start(pred[26]{0:T(512)(128)(4,1)} %constant.68) | copy-start | bytes 82
  6.4 0.7 %copy-start.6 = (pred[26]{0:T(512)(128)(4,1)S(1)}, pred[26]{0:T(512)(128)(4,1)}, u32[]{:S(2)}) copy-start(pred[26]{0:T(512)(128)(4,1)} %constant.69) | copy-start | bytes 82
  6.4 0.7 %copy-start.7 = (f32[26]{0:T(128)S(1)}, f32[26]{0:T(128)}, u32[]{:S(2)}) copy-start(f32[26]{0:T(128)} %constant.70) | copy-start | bytes 316
  7.5 0.7 %copy-start.4 = (f32[13,6]{0,1:T(8,128)S(1)}, f32[13,6]{0,1:T(8,128)}, u32[]{:S(2)}) copy-start(f32[13,6]{0,1:T(8,128)} %param.13) | copy-start | bytes 940
  7.6 1.4 %copy-start = (bf16[64,1152]{1,0:T(8,128)(2,1)}, bf16[64,1152]{1,0:T(8,128)(2,1)S(1)}, u32[]{:S(2)}) copy-start(bf16[64,1152]{1,0:T(8,128)(2,1)S(1)} %concatenate.19.p1_ref) | copy-start | bytes 442372
  9.0 0.7 %copy-start.1 = (bf16[64,1152]{1,0:T(8,128)(2,1)}, bf16[64,1152]{1,0:T(8,128)(2,1)S(1)}, u32[]{:S(2)}) copy-start(bf16[64,1152]{1,0:T(8,128)(2,1)S(1)} %collective-permute-done.p2_ref) | copy-start | bytes 442372
  9.8 6.3 %collective-permute-start.1 = (bf16[74,1152]{1,0:T(8,128)(2,1)S(1)}, bf16[74,1152]{1,0:T(8,128)(2,1)S(1)}, u32[]{:S(2)}, u32[]{:S(2)}) collective-permute-start(bf16[74,1152]{1,0:T(8,128)(2,1)S(1)} %get-tuple-element.7), channel_id=1, source_target_pairs={{0,1},{1,2},{2,3},{3,4},{4,5},{5,6},{6,7},{7,8},{8,9},{9,10},{10,1... | collective-permute-start | bytes 511496 | tf_op jit(solution)/shard_map/ppermute | solution.py:108
  11.1 6.5 %collective-permute-start.2 = (bf16[74,1152]{1,0:T(8,128)(2,1)S(1)}, bf16[74,1152]{1,0:T(8,128)(2,1)S(1)}, u32[]{:S(2)}, u32[]{:S(2)}) collective-permute-start(bf16[74,1152]{1,0:T(8,128)(2,1)S(1)} %get-tuple-element.8), channel_id=1, source_target_pairs={{1,0},{2,1},{3,2},{4,3},{5,4},{6,5},{7,6},{8,7},{9,8},{10,9},{11,1... | collective-permute-start | bytes 511496 | tf_op jit(solution)/shard_map/ppermute | solution.py:107
  16.1 2.3 %copy-start.2 = (bf16[74,1152]{1,0:T(8,128)(2,1)}, bf16[74,1152]{1,0:T(8,128)(2,1)S(1)}, u32[]{:S(2)}) copy-start(bf16[74,1152]{1,0:T(8,128)(2,1)S(1)} %collective-permute-done.1.p0_ref) | copy-start | bytes 511492
  17.5 0.9 %copy-start.3 = (bf16[74,1152]{1,0:T(8,128)(2,1)}, bf16[74,1152]{1,0:T(8,128)(2,1)S(1)}, u32[]{:S(2)}) copy-start(bf16[74,1152]{1,0:T(8,128)(2,1)S(1)} %collective-permute-done.2.p3_ref) | copy-start | bytes 511492
